TPU v7x, 256 devices: a whole 4x4x8 slice. The times are simulated.
256 devices in a mesh: pp: 16 (over z_lo, y, core), ep: 16 (over x, z_hi).
Axes of the slice: x: 4, y: 4, z: 8 (z_hi: 4, z_lo: 2; z = z_hi * 2 + z_lo), core: 2. Of those that a mesh axis runs over, the one named last changes fastest.
Arguments:
- fwd_tokens: bfloat16 [16, 2048, 3584], P('pp', 'ep'), may hold values from -6 to 6
- fwd_routes: int32 [16, 2048, 2], P('pp', 'ep'), may hold values from 0 to 7, all different within a row; in each aligned block of 128 rows (0 to 127, 128 to 255, ..., all dimensions but the last counted through in order) at most 48 rows name the same one
- fwd_weights: float32 [16, 2048, 2], P('pp', 'ep'), may hold values from 0.2 to 1
- bwd_tokens: bfloat16 [16, 2048, 3584], P('pp', 'ep'), may hold values from -6 to 6
- bwd_grads: bfloat16 [16, 2048, 3584], P('pp', 'ep'), may hold values from -6 to 6
- bwd_routes: int32 [16, 2048, 2], P('pp', 'ep'), may hold values from 0 to 7, all different within a row; in each aligned block of 128 rows (0 to 127, 128 to 255, ..., all dimensions but the last counted through in order) at most 48 rows name the same one
- bwd_weights: float32 [16, 2048, 2], P('pp', 'ep'), may hold values from 0.2 to 1
- up_proj: bfloat16 [16, 3584, 8192], P('pp', None, 'ep'), may hold values from -0.09375 to 0.09375
- down_proj: bfloat16 [16, 8192, 3584], P('pp', 'ep'), may hold values from -0.1875 to 0.1875
Outputs:
- next_input: bfloat16 [16, 2048, 3584], P('pp', 'ep')
- prev_grad: bfloat16 [16, 2048, 3584], P('pp', 'ep')
Inputs may be any that keep to these rules, and one draw needn't show every extreme that they name: `fwd_routes`: each row names 2 different experts. Among the 128 rows of one device no expert is named more than 48 times; on some devices some expert is named exactly 48 times. `bwd_routes`: as for fwd_routes.
All inputs are finite; a program needn't handle non-finite values.
Results may differ from a plain program's by a relative error of at most 0.0043.
Values may be sent and summed in bfloat16 or wider, within the bound.
No kernel may reach another device: no remote copies, remote signals or barrier semaphores. Data moves between devices by JAX's collectives and lax.ppermute only.
A program may use at most 128 MiB of HBM per device.

v0:
```python
import jax
import jax.numpy as jnp
from jax import lax
from jax.sharding import PartitionSpec as P


def as_sent(value):

    def short(part):
        return part.astype(jnp.bfloat16) if part.dtype == jnp.float32 else part

    return jax.tree.map(short, value)


def from_behind(value, axis, by):
    size = lax.axis_size(axis)
    return lax.ppermute(value, axis, [(i, (i + by) % size) for i in range(size)])


def silu_slope(pre_act):
    sigmoid_value = jax.nn.sigmoid(pre_act)
    return sigmoid_value * (1.0 + pre_act * (1.0 - sigmoid_value))


def slot_numbers(routes, expert_count, capacity):
    chosen = routes[0]
    tok_rows, route_count = chosen.shape
    onehot = (
        chosen[:, :, None] == jnp.arange(expert_count, dtype=jnp.int32)[None, None, :]
    ).astype(jnp.int32)
    flat_hot = onehot.reshape(tok_rows * route_count, expert_count)
    earlier = jnp.cumsum(flat_hot, axis=0) - flat_hot
    position = jnp.sum(earlier * flat_hot, axis=1).reshape(tok_rows, route_count)
    return chosen * capacity + position


def pack_rows(sources, slots, slot_total):
    slot_table = jnp.sum(
        (slots[:, :, None] == jnp.arange(slot_total, dtype=jnp.int32)[None, None, :]).astype(
            jnp.bfloat16
        ),
        axis=1,
    )
    return tuple(
        (
            lax.dot_general(
                slot_table, member, (((0,), (0,)), ((), ())), preferred_element_type=jnp.float32
            ).astype(jnp.bfloat16)
            for member in sources
        )
    )


def combine_rows(residual, results, slots, route_weights):
    picked = results[slots].astype(jnp.float32)
    combined = residual.astype(jnp.float32) + jnp.sum(route_weights[:, :, None] * picked, axis=1)
    return combined.astype(jnp.bfloat16)


def forward_work(received, w_up, w_down):
    hidden = jax.nn.silu(
        jnp.einsum("scd,df->scf", received[0], w_up, preferred_element_type=jnp.float32)
    ).astype(jnp.bfloat16)
    return (jnp.einsum("scf,fd->scd", hidden, w_down, preferred_element_type=jnp.float32),)


def backward_work(received, w_up, w_down):
    pre_act = jnp.einsum("scd,df->scf", received[0], w_up, preferred_element_type=jnp.float32)
    upstream = jnp.einsum("scd,fd->scf", received[1], w_down, preferred_element_type=jnp.float32)
    hidden_grad = (silu_slope(pre_act) * upstream).astype(jnp.bfloat16)
    return (jnp.einsum("scf,df->scd", hidden_grad, w_up, preferred_element_type=jnp.float32),)


def pair_duplicate(outgoing, expert_work, expert_count, feature_count):

    def handle(received):
        partials = expert_work(received)
        rounded = tuple((member.astype(jnp.bfloat16) for member in partials))
        return jax.tree.map(
            lambda part, own: part.astype(own.dtype),
            lax.all_to_all(as_sent(rounded), "ep", split_axis=0, concat_axis=0, tiled=True),
            rounded,
        )

    returned = handle(
        jax.tree.map(
            lambda part, own: part.astype(own.dtype),
            lax.all_to_all(as_sent(outgoing), "ep", split_axis=0, concat_axis=0, tiled=True),
            outgoing,
        )
    )
    results = []
    for member in returned:
        paired = member.reshape(expert_count, 2, member.shape[1], feature_count).astype(jnp.float32)
        results.append(jnp.sum(paired, axis=1).astype(jnp.bfloat16).reshape(-1, feature_count))
    return tuple(results)


def on_device(
    fwd_tokens,
    fwd_routes,
    fwd_weights,
    bwd_tokens,
    bwd_grads,
    bwd_routes,
    bwd_weights,
    up_proj,
    down_proj,
):
    ep_count = lax.axis_size("ep")
    expert_count = ep_count // 2
    tok_rows = fwd_tokens.shape[1]
    feature_count = fwd_tokens.shape[2]
    route_count = fwd_routes.shape[2]
    capacity = 3 * tok_rows * route_count // ep_count
    slot_total = expert_count * capacity
    w_up = up_proj[0]
    w_down = down_proj[0]
    fwd_slots = slot_numbers(fwd_routes, expert_count, capacity)
    bwd_slots = slot_numbers(bwd_routes, expert_count, capacity)
    fwd_packed = pack_rows((fwd_tokens[0],), fwd_slots, slot_total)
    bwd_packed = pack_rows((bwd_tokens[0], bwd_grads[0]), bwd_slots, slot_total)

    def forward_fn(received):
        return forward_work(received, w_up, w_down)

    def backward_fn(received):
        return backward_work(received, w_up, w_down)

    def layout(packed):
        spread = []
        for member in packed:
            copies = jnp.broadcast_to(
                member.reshape(expert_count, 1, capacity, feature_count),
                (expert_count, 2, capacity, feature_count),
            )
            spread.append(copies.reshape(ep_count, capacity, feature_count))
        return tuple(spread)

    (fwd_results,) = pair_duplicate(layout(fwd_packed), forward_fn, expert_count, feature_count)
    (bwd_results,) = pair_duplicate(layout(bwd_packed), backward_fn, expert_count, feature_count)
    fwd_out = combine_rows(fwd_tokens[0], fwd_results, fwd_slots, fwd_weights[0])
    bwd_out = combine_rows(bwd_grads[0], bwd_results, bwd_slots, bwd_weights[0])
    next_input = from_behind(fwd_out[None], "pp", 1)
    prev_grad = from_behind(bwd_out[None], "pp", -1)
    return (next_input, prev_grad)


def solution(mesh):
    placed = (
        P("pp", "ep", None),
        P("pp", "ep", None),
        P("pp", "ep", None),
        P("pp", "ep", None),
        P("pp", "ep", None),
        P("pp", "ep", None),
        P("pp", "ep", None),
        P("pp", None, "ep"),
        P("pp", "ep", None),
    )
    return jax.shard_map(
        on_device,
        mesh=mesh,
        in_specs=placed,
        out_specs=(P("pp", "ep", None), P("pp", "ep", None)),
        check_vma=False,
    )
```

profile of v0, /device:TPU:29, one launch (start us, length us, event | category | flops | bytes accessed | tf_op | source)
XLA Modules:
  0.0 736.0 jit_solution(3275072012511017414)
XLA Ops:
  0.6 0.9 copy.29
  1.5 0.1 eq.93
  1.7 0.1 eq.89
  1.8 0.6 reduce-window.16
  2.4 0.2 slice_reduce_fusion
  2.7 0.1 reshape.166
  3.1 0.9 convolution_convert_fusion.3
  4.0 3.0 broadcast_in_dim.15
  7.0 10.9 %all-to-all-start.2 = ((bf16[16,48,3584]{2,1,0:T(8,128)(2,1)}), bf16[16,48,3584]{2,1,0:T(8,128)(2,1)}, u32[]{:S(2)}, u32[]{:S(2)}) async-start(bf16[16,48,3584]{2,1,0:T(8,128)(2,1)} %bitcast.95), calls=%async_computation.2 | async-start | bytes 11010048 | tf_op jit(solution)/shard_map/all_to_all | solution.py:88
  17.9 2.1 convolution_convert_fusion.2
  20.0 121.1 %all-to-all-done.2 = bf16[16,48,3584]{2,1,0:T(8,128)(2,1)} async-done(((bf16[16,48,3584]{2,1,0:T(8,128)(2,1)}), bf16[16,48,3584]{2,1,0:T(8,128)(2,1)}, u32[]{:S(2)}, u32[]{:S(2)}) %all-to-all-start.2) | async-done | bytes 5505056 | tf_op jit(solution)/shard_map/all_to_all | solution.py:88
  141.1 3.0 broadcast_in_dim.17
  144.1 6.6 all-to-all-start.3
  150.8 0.1 eq.82
  150.9 0.1 eq.78
  151.1 0.6 reduce-window.14
  151.7 0.2 slice_reduce_fusion.1
  152.0 0.1 reshape.160
  152.4 2.1 convolution_convert_fusion.4
  154.5 106.8 %all-to-all-done.3 = bf16[16,48,3584]{2,1,0:T(8,128)(2,1)} async-done(((bf16[16,48,3584]{2,1,0:T(8,128)(2,1)}), bf16[16,48,3584]{2,1,0:T(8,128)(2,1)}, u32[]{:S(2)}, u32[]{:S(2)}) %all-to-all-start.3) | async-done | bytes 5505056 | tf_op jit(solution)/shard_map/all_to_all | solution.py:88
  261.2 3.0 broadcast_in_dim.13
  264.2 24.5 %all-to-all-start = ((bf16[16,48,3584]{2,1,0:T(8,128)(2,1)}), bf16[16,48,3584]{2,1,0:T(8,128)(2,1)}, u32[]{:S(2)}, u32[]{:S(2)}) async-start(bf16[16,48,3584]{2,1,0:T(8,128)(2,1)} %bitcast.94), calls=%async_computation | async-start | bytes 11010048 | tf_op jit(solution)/shard_map/all_to_all | solution.py:88
  288.7 6.1 fusion.4
  294.8 13.2 %convolution_convert_fusion = bf16[16,48,3584]{2,1,0:T(8,128)(2,1)} fusion(bf16[1,3584,512]{2,1,0:T(8,128)(2,1)} %param.16, f32[16,48,512]{2,1,0:T(8,128)S(1)} %fusion.4, bf16[16,48,3584]{2,1,0:T(8,128)(2,1)} %all-to-all-done.3, bf16[1,512,3584]{2,1,0:T(8,128)(2,1)} %param.17), kind=kOutput, calls=%fused_computation.2 | convolution fusion | flops 5643436032 | bytes 19922944 | tf_op jit(solution)/shard_map/scf,df->scd/dot_general | solution.py:71
  308.0 97.5 %all-to-all-done = bf16[16,48,3584]{2,1,0:T(8,128)(2,1)} async-done(((bf16[16,48,3584]{2,1,0:T(8,128)(2,1)}), bf16[16,48,3584]{2,1,0:T(8,128)(2,1)}, u32[]{:S(2)}, u32[]{:S(2)}) %all-to-all-start) | async-done | bytes 5505056 | tf_op jit(solution)/shard_map/all_to_all | solution.py:88
  405.5 22.8 %all-to-all-start.4 = ((bf16[16,48,3584]{2,1,0:T(8,128)(2,1)}), bf16[16,48,3584]{2,1,0:T(8,128)(2,1)}, u32[]{:S(2)}, u32[]{:S(2)}) async-start(bf16[16,48,3584]{2,1,0:T(8,128)(2,1)} %convolution_convert_fusion), calls=%async_computation.4 | async-start | bytes 11010048 | tf_op jit(solution)/shard_map/all_to_all | solution.py:81
  428.4 13.2 %convolution_convert_fusion.1 = bf16[16,48,3584]{2,1,0:T(8,128)(2,1)} fusion(bf16[1,512,3584]{2,1,0:T(8,128)(2,1)} %param.17, bf16[16,48,3584]{2,1,0:T(8,128)(2,1)} %all-to-all-done, bf16[1,3584,512]{2,1,0:T(8,128)(2,1)} %param.16), kind=kOutput, calls=%fused_computation.3 | convolution fusion | flops 5641863168 | bytes 18350080 | tf_op jit(solution)/shard_map/scf,fd->scd/dot_general | solution.py:64
  441.5 95.3 %all-to-all-done.4 = bf16[16,48,3584]{2,1,0:T(8,128)(2,1)} async-done(((bf16[16,48,3584]{2,1,0:T(8,128)(2,1)}), bf16[16,48,3584]{2,1,0:T(8,128)(2,1)}, u32[]{:S(2)}, u32[]{:S(2)}) %all-to-all-start.4) | async-done | bytes 5505056 | tf_op jit(solution)/shard_map/all_to_all | solution.py:81
  536.8 19.9 %all-to-all-start.1 = ((bf16[16,48,3584]{2,1,0:T(8,128)(2,1)}), bf16[16,48,3584]{2,1,0:T(8,128)(2,1)}, u32[]{:S(2)}, u32[]{:S(2)}) async-start(bf16[16,48,3584]{2,1,0:T(8,128)(2,1)} %convolution_convert_fusion.1), calls=%async_computation.1 | async-start | bytes 11010048 | tf_op jit(solution)/shard_map/all_to_all | solution.py:81
  556.8 0.1 reshape.164
  557.0 0.1 reshape.182
  557.3 0.1 reshape.174
  557.6 3.8 bitcast_reduce_fusion
  561.4 3.0 gather_fusion.1
  564.4 5.2 reshape.191
  569.6 7.4 %multiply_reduce_fusion = f32[128,3584]{1,0:T(8,128)S(1)} fusion(f32[128,2,3584]{2,1,0:T(2,128)} %reshape.191, f32[128,2]{1,0:T(8,128)S(1)} %copy.28), kind=kLoop, calls=%fused_computation.17 | loop fusion | flops 1376256 | bytes 5506048 | tf_op jit(solution)/shard_map/reduce_sum | solution.py:56
  577.0 1.1 fusion.8
  578.1 4.3 collective-permute-start.1
  582.4 82.5 %all-to-all-done.1 = bf16[16,48,3584]{2,1,0:T(8,128)(2,1)} async-done(((bf16[16,48,3584]{2,1,0:T(8,128)(2,1)}), bf16[16,48,3584]{2,1,0:T(8,128)(2,1)}, u32[]{:S(2)}, u32[]{:S(2)}) %all-to-all-start.1) | async-done | bytes 5505056 | tf_op jit(solution)/shard_map/all_to_all | solution.py:81
  664.9 3.8 bitcast_reduce_fusion.1
  668.7 3.0 gather_fusion
  671.7 5.2 reshape.190
  676.9 7.5 %multiply_reduce_fusion.1 = f32[128,3584]{1,0:T(8,128)S(1)} fusion(f32[128,2,3584]{2,1,0:T(2,128)} %reshape.190, f32[128,2]{1,0:T(8,128)S(1)} %copy.23), kind=kLoop, calls=%fused_computation.18 | loop fusion | flops 1376256 | bytes 5506048 | tf_op jit(solution)/shard_map/reduce_sum | solution.py:56
  684.4 0.2 fusion.9
  684.6 38.0 %collective-permute-start = (bf16[1,128,3584]{2,1,0:T(8,128)(2,1)S(1)}, bf16[1,128,3584]{2,1,0:T(8,128)(2,1)S(1)}, u32[]{:S(2)}, u32[]{:S(2)}) collective-permute-start(bf16[1,128,3584]{2,1,0:T(8,128)(2,1)S(1)} %fusion.9), channel_id=1, source_target_pairs={{0,16},{16,32},{32,48},{48,64},{64,80},{80,96},{96,112},{112,128},... | collective-permute-start | bytes 2752520 | tf_op jit(solution)/shard_map/ppermute | solution.py:17
  722.6 10.3 %collective-permute-done = bf16[1,128,3584]{2,1,0:T(8,128)(2,1)S(1)} collective-permute-done((bf16[1,128,3584]{2,1,0:T(8,128)(2,1)S(1)}, bf16[1,128,3584]{2,1,0:T(8,128)(2,1)S(1)}, u32[]{:S(2)}, u32[]{:S(2)}) %collective-permute-start) | collective-permute-done | bytes 917536 | tf_op jit(solution)/shard_map/ppermute | solution.py:17
  732.9 0.9 copy.35
  733.8 2.2 copy.36
  (37 shorter events, 1.2 us)
Async XLA Ops:
  0.6 2.5 copy-start
  7.0 134.1 %all-to-all-start.2 = ((bf16[16,48,3584]{2,1,0:T(8,128)(2,1)}), bf16[16,48,3584]{2,1,0:T(8,128)(2,1)}, u32[]{:S(2)}, u32[]{:S(2)}) async-start(bf16[16,48,3584]{2,1,0:T(8,128)(2,1)} %bitcast.95), calls=%async_computation.2 | async-start | bytes 11010048 | tf_op jit(solution)/shard_map/all_to_all | solution.py:88
  144.1 6.6 copy-start.4
  144.1 117.2 %all-to-all-start.3 = ((bf16[16,48,3584]{2,1,0:T(8,128)(2,1)}), bf16[16,48,3584]{2,1,0:T(8,128)(2,1)}, u32[]{:S(2)}, u32[]{:S(2)}) async-start(bf16[16,48,3584]{2,1,0:T(8,128)(2,1)} %bitcast.93), calls=%async_computation.3 | async-start | bytes 11010048 | tf_op jit(solution)/shard_map/all_to_all | solution.py:88
  264.2 141.3 %all-to-all-start = ((bf16[16,48,3584]{2,1,0:T(8,128)(2,1)}), bf16[16,48,3584]{2,1,0:T(8,128)(2,1)}, u32[]{:S(2)}, u32[]{:S(2)}) async-start(bf16[16,48,3584]{2,1,0:T(8,128)(2,1)} %bitcast.94), calls=%async_computation | async-start | bytes 11010048 | tf_op jit(solution)/shard_map/all_to_all | solution.py:88
  405.5 131.2 %all-to-all-start.4 = ((bf16[16,48,3584]{2,1,0:T(8,128)(2,1)}), bf16[16,48,3584]{2,1,0:T(8,128)(2,1)}, u32[]{:S(2)}, u32[]{:S(2)}) async-start(bf16[16,48,3584]{2,1,0:T(8,128)(2,1)} %convolution_convert_fusion), calls=%async_computation.4 | async-start | bytes 11010048 | tf_op jit(solution)/shard_map/all_to_all | solution.py:81
  441.5 115.6 %copy-start.5 = (f32[1,128,2]{1,2,0:T(2,128)S(1)}, f32[1,128,2]{1,2,0:T(2,128)}, u32[]{:S(2)}) copy-start(f32[1,128,2]{1,2,0:T(2,128)} %param.15) | copy-start | bytes 3076
  441.5 115.9 %copy-start.6 = (f32[1,128,2]{1,2,0:T(2,128)S(1)}, f32[1,128,2]{1,2,0:T(2,128)}, u32[]{:S(2)}) copy-start(f32[1,128,2]{1,2,0:T(2,128)} %param.11) | copy-start | bytes 3076
  536.8 128.1 %all-to-all-start.1 = ((bf16[16,48,3584]{2,1,0:T(8,128)(2,1)}), bf16[16,48,3584]{2,1,0:T(8,128)(2,1)}, u32[]{:S(2)}, u32[]{:S(2)}) async-start(bf16[16,48,3584]{2,1,0:T(8,128)(2,1)} %convolution_convert_fusion.1), calls=%async_computation.1 | async-start | bytes 11010048 | tf_op jit(solution)/shard_map/all_to_all | solution.py:81
  569.6 7.4 %copy-start.2 = (bf16[1,128,3584]{2,1,0:T(8,128)(2,1)S(1)}, bf16[1,128,3584]{2,1,0:T(8,128)(2,1)}, u32[]{:S(2)}) copy-start(bf16[1,128,3584]{2,1,0:T(8,128)(2,1)} %param.13) | copy-start | bytes 2752516
  578.1 144.5 %collective-permute-start.1 = (bf16[1,128,3584]{2,1,0:T(8,128)(2,1)}, bf16[1,128,3584]{2,1,0:T(8,128)(2,1)}, u32[]{:S(2)}, u32[]{:S(2)}) collective-permute-start(bf16[1,128,3584]{2,1,0:T(8,128)(2,1)} %fusion.8), channel_id=1, source_target_pairs={{0,240},{16,0},{32,16},{48,32},{64,48},{80,64},{96,80},{112,96},{1... | collective-permute-start | bytes 2752520 | tf_op jit(solution)/shard_map/ppermute | solution.py:17
  676.9 7.5 %copy-start.3 = (bf16[1,128,3584]{2,1,0:T(8,128)(2,1)S(1)}, bf16[1,128,3584]{2,1,0:T(8,128)(2,1)}, u32[]{:S(2)}) copy-start(bf16[1,128,3584]{2,1,0:T(8,128)(2,1)} %param.9) | copy-start | bytes 2752516
  676.9 59.1 %copy-start.1 = (bf16[1,128,3584]{2,1,0:T(8,128)(2,1)S(1)}, bf16[1,128,3584]{2,1,0:T(8,128)(2,1)}, u32[]{:S(2)}) copy-start(bf16[1,128,3584]{2,1,0:T(8,128)(2,1)} %param.12) | copy-start | bytes 2752516
  684.6 48.4 %collective-permute-start = (bf16[1,128,3584]{2,1,0:T(8,128)(2,1)S(1)}, bf16[1,128,3584]{2,1,0:T(8,128)(2,1)S(1)}, u32[]{:S(2)}, u32[]{:S(2)}) collective-permute-start(bf16[1,128,3584]{2,1,0:T(8,128)(2,1)S(1)} %fusion.9), channel_id=1, source_target_pairs={{0,16},{16,32},{32,48},{48,64},{64,80},{80,96},{96,112},{112,128},... | collective-permute-start | bytes 2752520 | tf_op jit(solution)/shard_map/ppermute | solution.py:17
where the time goes:
time: 744 us; the launch traced here: 736 us
  waiting for transfers between devices  514 us (69%)
  starting transfers between devices  127 us (17%)
  matrix products  37.5 us (5%)
  local copies, waits for them, and re-layouts  31.5 us (4%)
  other arithmetic  25.5 us (3%)
    all_to_all x3, waiting for transfers between devices, pair_duplicate(): lax.all_to_all(as_sent(outgoing), 'ep', split_axis=0, concat_axis=0, tile...  325 us
    all_to_all x2, waiting for transfers between devices, handle(): lax.all_to_all(as_sent(rounded), 'ep', split_axis=0, concat_axis=0, tiled...  178 us
    all_to_all x2, starting transfers between devices, handle(): lax.all_to_all(as_sent(rounded), 'ep', split_axis=0, concat_axis=0, tiled...  42.8 us
    ppermute x2, starting transfers between devices, from_behind(): lax.ppermute(value, axis, [(i, (i + by) % size) for i in range(size)])  42.4 us
    all_to_all x3, starting transfers between devices, pair_duplicate(): lax.all_to_all(as_sent(outgoing), 'ep', split_axis=0, concat_axis=0, tile...  42 us
  transfers between devices with their start and end apart: 7, of which 6 were waited for; matrix products, arithmetic and copies ran while one was open for 11% of the time, Pallas kernels for 0%

commit v1 on v0

v1 whole, which is shorter than its diff:
```python
import jax
import jax.numpy as jnp
from jax import lax
from jax.sharding import Mesh
from jax.sharding import PartitionSpec as P

Z_PARTS = 4


def from_behind(value, axis, by):
    size = lax.axis_size(axis)
    return lax.ppermute(value, axis, [(i, (i + by) % size) for i in range(size)])


def silu_slope(pre_act):
    sigmoid_value = jax.nn.sigmoid(pre_act)
    return sigmoid_value * (1.0 + pre_act * (1.0 - sigmoid_value))


def slot_positions(chosen, expert_count):
    groups, tok_rows, route_count = chosen.shape
    onehot = (chosen[..., None] == jnp.arange(expert_count, dtype=jnp.int32)).astype(jnp.int32)
    flat_hot = onehot.reshape(groups, tok_rows * route_count, expert_count)
    earlier = jnp.cumsum(flat_hot, axis=1) - flat_hot
    return jnp.sum(earlier * flat_hot, axis=2).reshape(groups, tok_rows, route_count)


def local_slots(chosen, position, expert_class, class_count, capacity):
    column = chosen // class_count
    mine = (chosen % class_count) == expert_class
    return jnp.where(mine, column * capacity + position, -1)


def pack_rows(sources, slots, slot_total):
    table = jnp.sum(
        (slots[..., None] == jnp.arange(slot_total, dtype=jnp.int32)).astype(jnp.bfloat16), axis=2
    )
    return tuple(
        jnp.einsum("gts,gtd->gsd", table, member, preferred_element_type=jnp.float32).astype(jnp.bfloat16)
        for member in sources
    )


def weighted_partial(results, slots, route_weights):
    groups, tok_rows, route_count = slots.shape
    valid = slots >= 0
    index = jnp.where(valid, slots, 0)
    weight = jnp.where(valid, route_weights, 0.0)
    total = None
    for k in range(route_count):
        picked = jnp.take_along_axis(results, index[:, :, k, None], axis=1).astype(jnp.float32)
        term = weight[:, :, k, None] * picked
        total = term if total is None else total + term
    return total.astype(jnp.bfloat16)


def forward_work(rows, w_up, w_down):
    hidden = jax.nn.silu(jnp.dot(rows, w_up, preferred_element_type=jnp.float32)).astype(jnp.bfloat16)
    return jnp.dot(hidden, w_down, preferred_element_type=jnp.float32).astype(jnp.bfloat16)


def backward_work(rows, grad_rows, w_up, w_down):
    pre_act = jnp.dot(rows, w_up, preferred_element_type=jnp.float32)
    upstream = lax.dot_general(grad_rows, w_down, (((1,), (1,)), ((), ())), preferred_element_type=jnp.float32)
    hidden_grad = (silu_slope(pre_act) * upstream).astype(jnp.bfloat16)
    return lax.dot_general(
        hidden_grad, w_up, (((1,), (1,)), ((), ())), preferred_element_type=jnp.float32
    ).astype(jnp.bfloat16)


def to_experts(packed, x_count, capacity):
    groups, slot_total, features = packed.shape
    spread = packed.reshape(groups, x_count, capacity, features)
    got = lax.all_to_all(spread, "ex", split_axis=1, concat_axis=1, tiled=True)
    return got.reshape(groups * x_count * capacity, features)


def from_experts(rows, groups, x_count, capacity):
    features = rows.shape[-1]
    spread = rows.reshape(groups, x_count, capacity, features)
    back = lax.all_to_all(spread, "ex", split_axis=1, concat_axis=1, tiled=True)
    return back.reshape(groups, x_count * capacity, features)


def sum_back(residual, partial):
    got = lax.all_to_all(partial, "ez", split_axis=0, concat_axis=0, tiled=True)
    total = residual.astype(jnp.float32) + jnp.sum(got.astype(jnp.float32), axis=0)
    return total.astype(jnp.bfloat16)


def on_device(
    fwd_tokens,
    fwd_routes,
    fwd_weights,
    bwd_tokens,
    bwd_grads,
    bwd_routes,
    bwd_weights,
    up_proj,
    down_proj,
):
    x_count = lax.axis_size("ex")
    z_count = lax.axis_size("ez")
    ep_count = x_count * z_count
    expert_count = ep_count // 2
    class_count = expert_count // x_count
    tok_rows = fwd_tokens.shape[1]
    route_count = fwd_routes.shape[2]
    capacity = 3 * tok_rows * route_count // ep_count
    slot_total = x_count * capacity
    z_index = lax.axis_index("ez")
    expert_class = z_index // (z_count // class_count)
    w_up = up_proj[0]
    w_down = down_proj[0]

    def gather_z(value):
        return lax.all_gather(value[0], "ez", axis=0, tiled=False)

    with jax.named_scope("gather_along_z"):
        fwd_tok_z = gather_z(fwd_tokens)
        fwd_routes_z = gather_z(fwd_routes)
        fwd_weights_z = gather_z(fwd_weights)
        bwd_tok_z = gather_z(bwd_tokens)
        bwd_grads_z = gather_z(bwd_grads)
        bwd_routes_z = gather_z(bwd_routes)
        bwd_weights_z = gather_z(bwd_weights)

    with jax.named_scope("slots"):
        fwd_slots = local_slots(
            fwd_routes_z, slot_positions(fwd_routes_z, expert_count), expert_class, class_count, capacity
        )
        bwd_slots = local_slots(
            bwd_routes_z, slot_positions(bwd_routes_z, expert_count), expert_class, class_count, capacity
        )

    with jax.named_scope("forward_experts"):
        (fwd_packed,) = pack_rows((fwd_tok_z,), fwd_slots, slot_total)
        fwd_rows = to_experts(fwd_packed, x_count, capacity)
        fwd_res = forward_work(fwd_rows, w_up, w_down)
        fwd_back = from_experts(fwd_res, z_count, x_count, capacity)
        fwd_part = weighted_partial(fwd_back, fwd_slots, fwd_weights_z)
        fwd_out = sum_back(fwd_tokens[0], fwd_part)

    with jax.named_scope("backward_experts"):
        bwd_packed, grad_packed = pack_rows((bwd_tok_z, bwd_grads_z), bwd_slots, slot_total)
        bwd_rows = to_experts(bwd_packed, x_count, capacity)
        grad_rows = to_experts(grad_packed, x_count, capacity)
        bwd_res = backward_work(bwd_rows, grad_rows, w_up, w_down)
        bwd_back = from_experts(bwd_res, z_count, x_count, capacity)
        bwd_part = weighted_partial(bwd_back, bwd_slots, bwd_weights_z)
        bwd_out = sum_back(bwd_grads[0], bwd_part)

    next_input = from_behind(fwd_out[None], "pp", 1)
    prev_grad = from_behind(bwd_out[None], "pp", -1)
    return (next_input, prev_grad)


def solution(mesh):
    devices = mesh.devices
    pp_count, ep_count = devices.shape
    split_mesh = Mesh(devices.reshape(pp_count, ep_count // Z_PARTS, Z_PARTS), ("pp", "ex", "ez"))
    rows = P("pp", ("ex", "ez"), None)
    placed = (rows, rows, rows, rows, rows, rows, rows, P("pp", None, ("ex", "ez")), rows)
    return jax.shard_map(
        on_device,
        mesh=split_mesh,
        in_specs=placed,
        out_specs=(rows, rows),
        check_vma=False,
    )
```

time: 744 us -> 674 us (0.906)
  waiting for transfers between devices: 514 us -> 295 us
  local copies, waits for them, and re-layouts: 31.5 us -> 156 us
  blocking collectives: 0 us -> 38.7 us
  starting transfers between devices: 127 us -> 107 us
  between operations: 0.89 us -> 14 us
  matrix products: 37.5 us -> 26.9 us
    all_to_all x5 -> x7, waiting for transfers between devices: 503 us -> 131 us  [the longest x2 45.7 us: from_experts(): back = lax.all_to_all(spread, 'ex', split_axis=1, concat_axis=1, tiled=True)]
    all_gather x0 -> x3, waiting for transfers between devices: none -> 152 us  [gather_z(): return lax.all_gather(value[0], 'ez', axis=0, tiled=False)]
    gather x2 -> x4, local copies, waits for them, and re-layouts: 5.95 us -> 118 us  [weighted_partial(): jnp.take_along_axis(results, index[:, :, k, None], axis=1)]
    all_gather x0 -> x4, blocking collectives: none -> 38.7 us  [gather_z(): return lax.all_gather(value[0], 'ez', axis=0, tiled=False)]
    all_to_all x5 -> x7, starting transfers between devices: 84.7 us -> 62.7 us  [the longest x3 27.2 us: to_experts(): got = lax.all_to_all(spread, 'ex', split_axis=1, concat_axis=1, tiled=True)]
    all_to_all x0 -> x5, local copies, waits for them, and re-layouts: none -> 19.9 us  [the longest x2 10.9 us: from_experts(): back = lax.all_to_all(spread, 'ex', split_axis=1, concat_axis=1, tiled=True)]
    reduce_sum x8 -> x6, other arithmetic: 23 us -> 5.95 us  [the longest x2 5.54 us: sum_back(): jnp.sum(got.astype(jnp.float32), axis=0)]
    reshape x4 -> x7, local copies, waits for them, and re-layouts: 0.55 us -> 14.1 us  [the longest x3 8.37 us: to_experts(): spread = packed.reshape(groups, x_count, capacity, features)]
  transfers between devices with their start and end apart: 7 -> 12, of which waited for: 6 -> 8; matrix products, arithmetic and copies ran while one was open for 11% -> 31% of each run, Pallas kernels for 0% -> 0%
where the time goes in v1:
time: 674 us; the launch traced here: 662 us
  waiting for transfers between devices  295 us (44%)
  local copies, waits for them, and re-layouts  156 us (23%)
  starting transfers between devices  107 us (16%)
  blocking collectives  38.7 us (6%)
  matrix products  26.9 us (4%)
  other arithmetic  24.5 us (4%)
  between operations  14 us (2%)
    all_gather x3, waiting for transfers between devices, gather_z(): return lax.all_gather(value[0], 'ez', axis=0, tiled=False)  152 us
    gather x4, local copies, waits for them, and re-layouts, weighted_partial(): jnp.take_along_axis(results, index[:, :, k, None], axis=1)  118 us
    all_to_all x2, waiting for transfers between devices, from_experts(): back = lax.all_to_all(spread, 'ex', split_axis=1, concat_axis=1, tiled=True)  45.7 us
    all_to_all x2, waiting for transfers between devices, sum_back(): got = lax.all_to_all(partial, 'ez', split_axis=0, concat_axis=0, tiled=True)  44.3 us
    ppermute x2, starting transfers between devices, from_behind(): lax.ppermute(value, axis, [(i, (i + by) % size) for i in range(size)])  43.9 us
    all_to_all x3, waiting for transfers between devices, to_experts(): got = lax.all_to_all(spread, 'ex', split_axis=1, concat_axis=1, tiled=True)  40.8 us
    all_gather x4, blocking collectives, gather_z(): return lax.all_gather(value[0], 'ez', axis=0, tiled=False)  38.7 us
    all_to_all x3, starting transfers between devices, to_experts(): got = lax.all_to_all(spread, 'ex', split_axis=1, concat_axis=1, tiled=True)  27.2 us
  transfers between devices with their start and end apart: 12, of which 8 were waited for; matrix products, arithmetic and copies ran while one was open for 31% of the time, Pallas kernels for 0%

profile of v1, /device:TPU:29, one launch (start us, length us, event | category | flops | bytes accessed | tf_op | source)
XLA Modules:
  0.0 662.1 jit_solution(5652477622670695788)
XLA Ops:
  8.7 12.4 %all_gather.21 = s32[4,128,2]{1,2,0:T(2,128)S(1)} all-gather(s32[1,128,2]{1,2,0:T(2,128)} %param.12), channel_id=1, replica_groups=mesh['pp'=16,'ex'=4,'ez'=4] {'ez'}, dimensions={0}, use_global_device_ids=true | all-gather | bytes 5120 | tf_op jit(solution)/shard_map/gather_along_z/all_gather | solution.py:117
  24.2 8.5 %all_gather.24 = s32[4,128,2]{1,2,0:T(2,128)S(1)} all-gather(s32[1,128,2]{1,2,0:T(2,128)} %param.16), channel_id=1, replica_groups=mesh['pp'=16,'ex'=4,'ez'=4] {'ez'}, dimensions={0}, use_global_device_ids=true | all-gather | bytes 5120 | tf_op jit(solution)/shard_map/gather_along_z/all_gather | solution.py:117
  33.0 2.3 reduce-window.16
  35.9 7.6 %all_gather.22 = f32[4,128,2]{1,2,0:T(2,128)S(1)} all-gather(f32[1,128,2]{1,2,0:T(2,128)S(1)} %copy-done.2), channel_id=1, replica_groups=mesh['pp'=16,'ex'=4,'ez'=4] {'ez'}, dimensions={0}, use_global_device_ids=true | all-gather | bytes 5120 | tf_op jit(solution)/shard_map/gather_along_z/all_gather | solution.py:117
  43.5 10.3 %all_gather.25 = f32[4,128,2]{1,2,0:T(2,128)S(1)} all-gather(f32[1,128,2]{1,2,0:T(2,128)S(1)} %copy-done.3), channel_id=1, replica_groups=mesh['pp'=16,'ex'=4,'ez'=4] {'ez'}, dimensions={0}, use_global_device_ids=true | all-gather | bytes 5120 | tf_op jit(solution)/shard_map/gather_along_z/all_gather | solution.py:117
  53.9 26.6 %all-gather.6.cloned.1.call-done = bf16[4,128,3584]{2,1,0:T(8,128)(2,1)} async-done(((bf16[1,128,3584]{2,1,0:T(8,128)(2,1)}), bf16[4,128,3584]{2,1,0:T(8,128)(2,1)}) %all-gather.6.cloned.1.call-update) | async-done | bytes 3670032 | tf_op jit(solution)/shard_map/gather_along_z/all_gather | solution.py:117
  80.5 3.6 convolution_convert_fusion.3
  84.1 2.8 copy.256
  86.9 5.6 all-to-all-start.3
  93.3 63.7 %all-gather.8.cloned.1.call-done = bf16[4,128,3584]{2,1,0:T(8,128)(2,1)} async-done(((bf16[1,128,3584]{2,1,0:T(8,128)(2,1)}), bf16[4,128,3584]{2,1,0:T(8,128)(2,1)}) %all-gather.8.cloned.1.call-update) | async-done | bytes 3670032 | tf_op jit(solution)/shard_map/gather_along_z/all_gather | solution.py:117
  156.9 3.6 convolution_convert_fusion.2
  160.6 2.8 copy.258
  163.4 11.3 %all-to-all-start.4 = ((bf16[4,4,48,3584]{3,2,0,1:T(8,128)(2,1)}), bf16[4,4,48,3584]{3,2,0,1:T(8,128)(2,1)}, u32[]{:S(2)}, u32[]{:S(2)}) async-start(bf16[4,4,48,3584]{3,2,0,1:T(8,128)(2,1)} %copy.258), calls=%async_computation.4 | async-start | bytes 11010048 | tf_op jit(solution)/shard_map/backward_experts/all_to_all | solution.py:74
  174.8 61.6 %all-gather.4.cloned.1.call-done = bf16[4,128,3584]{2,1,0:T(8,128)(2,1)} async-done(((bf16[1,128,3584]{2,1,0:T(8,128)(2,1)}), bf16[4,128,3584]{2,1,0:T(8,128)(2,1)}) %all-gather.4.cloned.1.call-update) | async-done | bytes 3670032 | tf_op jit(solution)/shard_map/gather_along_z/all_gather | solution.py:117
  236.3 3.6 convolution_convert_fusion.4
  239.9 2.7 copy.238
  242.7 10.3 %all-to-all-start = ((bf16[4,4,48,3584]{3,2,0,1:T(8,128)(2,1)}), bf16[4,4,48,3584]{3,2,0,1:T(8,128)(2,1)}, u32[]{:S(2)}, u32[]{:S(2)}) async-start(bf16[4,4,48,3584]{3,2,0,1:T(8,128)(2,1)} %copy.238), calls=%async_computation | async-start | bytes 11010048 | tf_op jit(solution)/shard_map/forward_experts/all_to_all | solution.py:74
  252.9 2.9 copy.257
  255.9 3.1 copy.259
  259.5 3.0 fusion.4
  262.5 3.3 multiply_convert_fusion
  265.9 3.3 convolution_convert_fusion
  269.1 2.8 copy.260
  271.9 40.8 %all-to-all-done = bf16[4,4,48,3584]{3,2,0,1:T(8,128)(2,1)} async-done(((bf16[4,4,48,3584]{3,2,0,1:T(8,128)(2,1)}), bf16[4,4,48,3584]{3,2,0,1:T(8,128)(2,1)}, u32[]{:S(2)}, u32[]{:S(2)}) %all-to-all-start) | async-done | bytes 5505056 | tf_op jit(solution)/shard_map/forward_experts/all_to_all | solution.py:74
  312.8 7.5 %all-to-all-start.5 = ((bf16[4,4,48,3584]{3,2,0,1:T(8,128)(2,1)}), bf16[4,4,48,3584]{3,2,0,1:T(8,128)(2,1)}, u32[]{:S(2)}, u32[]{:S(2)}) async-start(bf16[4,4,48,3584]{3,2,0,1:T(8,128)(2,1)} %copy.260), calls=%async_computation.5 | async-start | bytes 11010048 | tf_op jit(solution)/shard_map/backward_experts/all_to_all | solution.py:81
  320.2 3.1 copy.239
  323.9 3.2 multiply_convert_fusion.1
  327.1 3.2 convolution_convert_fusion.1
  330.4 2.8 copy.240
  333.2 45.7 %all-to-all-done.5 = bf16[4,4,48,3584]{3,2,0,1:T(8,128)(2,1)} async-done(((bf16[4,4,48,3584]{3,2,0,1:T(8,128)(2,1)}), bf16[4,4,48,3584]{3,2,0,1:T(8,128)(2,1)}, u32[]{:S(2)}, u32[]{:S(2)}) %all-to-all-start.5) | async-done | bytes 5505056 | tf_op jit(solution)/shard_map/backward_experts/all_to_all | solution.py:81
  378.9 7.7 %all-to-all-start.1 = ((bf16[4,4,48,3584]{3,2,0,1:T(8,128)(2,1)}), bf16[4,4,48,3584]{3,2,0,1:T(8,128)(2,1)}, u32[]{:S(2)}, u32[]{:S(2)}) async-start(bf16[4,4,48,3584]{3,2,0,1:T(8,128)(2,1)} %copy.240), calls=%async_computation.1 | async-start | bytes 11010048 | tf_op jit(solution)/shard_map/forward_experts/all_to_all | solution.py:81
  386.6 5.4 copy.261
  392.0 29.7 %gather_fusion.2 = bf16[512,3584]{1,0:T(8,128)(2,1)} fusion(bf16[4,192,3584]{2,1,0:T(8,128)(2,1)} %bitcast.101, s32[512]{0:T(512)S(1)} %get-tuple-element.11), kind=kCustom, calls=%fused_computation.2.clone | custom fusion | bytes 7344128 | tf_op jit(solution)/shard_map/backward_experts/jit(take_along_axis)/gather | solution.py:51
  421.7 29.2 %gather_fusion.3 = bf16[512,3584]{1,0:T(8,128)(2,1)} fusion(bf16[4,192,3584]{2,1,0:T(8,128)(2,1)} %bitcast.102, s32[512]{0:T(512)S(1)} %get-tuple-element.12), kind=kCustom, calls=%fused_computation.3.clone | custom fusion | bytes 7344128 | tf_op jit(solution)/shard_map/backward_experts/jit(take_along_axis)/gather | solution.py:51
  450.9 6.8 %add_convert_fusion = bf16[4,128,3584]{2,1,0:T(8,128)(2,1)} fusion(bf16[4,128,3584]{2,1,0:T(8,128)(2,1)} %bitcast.110, bf16[4,128,3584]{2,1,0:T(8,128)(2,1)} %bitcast.108, f32[4,128]{1,0:T(4,128)S(1)} %get-tuple-element.10, f32[4,128]{1,0:T(4,128)S(1)} %get-tuple-element.9, pred[4,128]{1,0:T(4,128)(4,1)S(1)} %get-tuple-element.8, ...), kind=kLoop, calls=%fused_computation.5 | loop fusion | flops 14680064 | bytes 11015168 | tf_op jit(solution)/shard_map/backward_experts/convert_element_type | solution.py:54
  457.7 11.5 %all-to-all-start.6 = ((bf16[4,128,3584]{2,1,0:T(8,128)(2,1)}), bf16[4,128,3584]{2,1,0:T(8,128)(2,1)}, u32[]{:S(2)}, u32[]{:S(2)}) async-start(bf16[4,128,3584]{2,1,0:T(8,128)(2,1)} %add_convert_fusion), calls=%async_computation.6 | async-start | bytes 7340032 | tf_op jit(solution)/shard_map/backward_experts/all_to_all | solution.py:86
  469.2 5.5 copy.241
  474.7 29.9 %gather_fusion = bf16[512,3584]{1,0:T(8,128)(2,1)} fusion(bf16[4,192,3584]{2,1,0:T(8,128)(2,1)} %bitcast.103, s32[512]{0:T(512)S(1)} %get-tuple-element.17), kind=kCustom, calls=%fused_computation.clone | custom fusion | bytes 7344128 | tf_op jit(solution)/shard_map/forward_experts/jit(take_along_axis)/gather | solution.py:51
  504.6 29.1 %gather_fusion.1 = bf16[512,3584]{1,0:T(8,128)(2,1)} fusion(bf16[4,192,3584]{2,1,0:T(8,128)(2,1)} %bitcast.104, s32[512]{0:T(512)S(1)} %get-tuple-element.18), kind=kCustom, calls=%fused_computation.1.clone | custom fusion | bytes 7344128 | tf_op jit(solution)/shard_map/forward_experts/jit(take_along_axis)/gather | solution.py:51
  533.7 6.8 %add_convert_fusion.1 = bf16[4,128,3584]{2,1,0:T(8,128)(2,1)} fusion(bf16[4,128,3584]{2,1,0:T(8,128)(2,1)} %bitcast.111, bf16[4,128,3584]{2,1,0:T(8,128)(2,1)} %bitcast.109, f32[4,128]{1,0:T(4,128)S(1)} %get-tuple-element.16, f32[4,128]{1,0:T(4,128)S(1)} %get-tuple-element.15, pred[4,128]{1,0:T(4,128)(4,1)S(1)} %get-tuple-element.14, ...), kind=kLoop, calls=%fused_computation.7 | loop fusion | flops 14680064 | bytes 11015168 | tf_op jit(solution)/shard_map/forward_experts/convert_element_type | solution.py:54
  540.5 8.9 %all-to-all-start.2 = ((bf16[4,128,3584]{2,1,0:T(8,128)(2,1)}), bf16[4,128,3584]{2,1,0:T(8,128)(2,1)}, u32[]{:S(2)}, u32[]{:S(2)}) async-start(bf16[4,128,3584]{2,1,0:T(8,128)(2,1)} %add_convert_fusion.1), calls=%async_computation.2 | async-start | bytes 7340032 | tf_op jit(solution)/shard_map/forward_experts/all_to_all | solution.py:86
  549.4 2.8 convert_reduce_fusion
  552.4 7.8 %collective-permute-start.1 = (bf16[1,128,3584]{2,1,0:T(8,128)(2,1)S(1)}, bf16[1,128,3584]{2,1,0:T(8,128)(2,1)S(1)}, u32[]{:S(2)}, u32[]{:S(2)}) collective-permute-start(bf16[1,128,3584]{2,1,0:T(8,128)(2,1)S(1)} %fusion.8), channel_id=1, source_target_pairs={{0,240},{16,0},{32,16},{48,32},{64,48},{80,64},{96,80},{112,96},{1... | collective-permute-start | bytes 2752520 | tf_op jit(solution)/shard_map/ppermute | solution.py:12
  560.2 44.2 %all-to-all-done.2 = bf16[4,128,3584]{2,1,0:T(8,128)(2,1)} async-done(((bf16[4,128,3584]{2,1,0:T(8,128)(2,1)}), bf16[4,128,3584]{2,1,0:T(8,128)(2,1)}, u32[]{:S(2)}, u32[]{:S(2)}) %all-to-all-start.2) | async-done | bytes 3670048 | tf_op jit(solution)/shard_map/forward_experts/all_to_all | solution.py:86
  604.5 2.7 convert_reduce_fusion.1
  607.4 36.1 %collective-permute-start = (bf16[1,128,3584]{2,1,0:T(8,128)(2,1)S(1)}, bf16[1,128,3584]{2,1,0:T(8,128)(2,1)S(1)}, u32[]{:S(2)}, u32[]{:S(2)}) collective-permute-start(bf16[1,128,3584]{2,1,0:T(8,128)(2,1)S(1)} %fusion.9), channel_id=1, source_target_pairs={{0,16},{16,32},{32,48},{48,64},{64,80},{80,96},{96,112},{112,128},... | collective-permute-start | bytes 2752520 | tf_op jit(solution)/shard_map/ppermute | solution.py:12
  643.4 3.9 collective-permute-done.1
  647.4 6.4 collective-permute-done
  (68 shorter events, 9.8 us)
Async XLA Ops:
  7.2 28.7 %copy-start.2 = (f32[1,128,2]{1,2,0:T(2,128)S(1)}, f32[1,128,2]{1,2,0:T(2,128)}, u32[]{:S(2)}) copy-start(f32[1,128,2]{1,2,0:T(2,128)} %param.13) | copy-start | bytes 3076
  7.2 36.3 %copy-start.3 = (f32[1,128,2]{1,2,0:T(2,128)S(1)}, f32[1,128,2]{1,2,0:T(2,128)}, u32[]{:S(2)}) copy-start(f32[1,128,2]{1,2,0:T(2,128)} %param.17) | copy-start | bytes 3076
  7.2 73.3 %all-gather.6.cloned.1.call-start = ((), (), s32[]{:S(2)}) async-start(), calls=%async_computation.8 | async-start | bytes 4587520 | tf_op jit(solution)/shard_map/gather_along_z/all_gather | solution.py:117
  7.9 149.0 %all-gather.8.cloned.1.call-start = ((), (), s32[]{:S(2)}) async-start(), calls=%async_computation.9 | async-start | bytes 4587520 | tf_op jit(solution)/shard_map/gather_along_z/all_gather | solution.py:117
  86.9 76.5 %all-to-all-start.3 = ((bf16[4,4,48,3584]{3,2,0,1:T(8,128)(2,1)}), bf16[4,4,48,3584]{3,2,0,1:T(8,128)(2,1)}, u32[]{:S(2)}, u32[]{:S(2)}) async-start(bf16[4,4,48,3584]{3,2,0,1:T(8,128)(2,1)} %copy.256), calls=%async_computation.3 | async-start | bytes 11010048 | tf_op jit(solution)/shard_map/backward_experts/all_to_all | solution.py:74
  92.5 143.8 %all-gather.4.cloned.1.call-start = ((), (), s32[]{:S(2)}) async-start(), calls=%async_computation.7 | async-start | bytes 4587520 | tf_op jit(solution)/shard_map/gather_along_z/all_gather | solution.py:117
  163.4 79.3 %all-to-all-start.4 = ((bf16[4,4,48,3584]{3,2,0,1:T(8,128)(2,1)}), bf16[4,4,48,3584]{3,2,0,1:T(8,128)(2,1)}, u32[]{:S(2)}, u32[]{:S(2)}) async-start(bf16[4,4,48,3584]{3,2,0,1:T(8,128)(2,1)} %copy.258), calls=%async_computation.4 | async-start | bytes 11010048 | tf_op jit(solution)/shard_map/backward_experts/all_to_all | solution.py:74
  242.7 70.1 %all-to-all-start = ((bf16[4,4,48,3584]{3,2,0,1:T(8,128)(2,1)}), bf16[4,4,48,3584]{3,2,0,1:T(8,128)(2,1)}, u32[]{:S(2)}, u32[]{:S(2)}) async-start(bf16[4,4,48,3584]{3,2,0,1:T(8,128)(2,1)} %copy.238), calls=%async_computation | async-start | bytes 11010048 | tf_op jit(solution)/shard_map/forward_experts/all_to_all | solution.py:74
  255.9 3.7 copy-start.4
  259.5 3.0 copy-start.6
  312.8 66.2 %all-to-all-start.5 = ((bf16[4,4,48,3584]{3,2,0,1:T(8,128)(2,1)}), bf16[4,4,48,3584]{3,2,0,1:T(8,128)(2,1)}, u32[]{:S(2)}, u32[]{:S(2)}) async-start(bf16[4,4,48,3584]{3,2,0,1:T(8,128)(2,1)} %copy.260), calls=%async_computation.5 | async-start | bytes 11010048 | tf_op jit(solution)/shard_map/backward_experts/all_to_all | solution.py:81
  320.2 3.7 copy-start.5
  323.9 3.2 copy-start.7
  378.9 78.8 %all-to-all-start.1 = ((bf16[4,4,48,3584]{3,2,0,1:T(8,128)(2,1)}), bf16[4,4,48,3584]{3,2,0,1:T(8,128)(2,1)}, u32[]{:S(2)}, u32[]{:S(2)}) async-start(bf16[4,4,48,3584]{3,2,0,1:T(8,128)(2,1)} %copy.240), calls=%async_computation.1 | async-start | bytes 11010048 | tf_op jit(solution)/shard_map/forward_experts/all_to_all | solution.py:81
  457.7 82.8 %all-to-all-start.6 = ((bf16[4,128,3584]{2,1,0:T(8,128)(2,1)}), bf16[4,128,3584]{2,1,0:T(8,128)(2,1)}, u32[]{:S(2)}, u32[]{:S(2)}) async-start(bf16[4,128,3584]{2,1,0:T(8,128)(2,1)} %add_convert_fusion), calls=%async_computation.6 | async-start | bytes 7340032 | tf_op jit(solution)/shard_map/backward_experts/all_to_all | solution.py:86
  540.5 64.0 %all-to-all-start.2 = ((bf16[4,128,3584]{2,1,0:T(8,128)(2,1)}), bf16[4,128,3584]{2,1,0:T(8,128)(2,1)}, u32[]{:S(2)}, u32[]{:S(2)}) async-start(bf16[4,128,3584]{2,1,0:T(8,128)(2,1)} %add_convert_fusion.1), calls=%async_computation.2 | async-start | bytes 7340032 | tf_op jit(solution)/shard_map/forward_experts/all_to_all | solution.py:86
  549.4 2.8 copy-start
  552.2 55.0 %copy-start.1 = (bf16[1,128,3584]{2,1,0:T(8,128)(2,1)S(1)}, bf16[1,128,3584]{2,1,0:T(8,128)(2,1)}, u32[]{:S(2)}) copy-start(bf16[1,128,3584]{2,1,0:T(8,128)(2,1)} %param.11) | copy-start | bytes 2752516
  552.4 95.0 %collective-permute-start.1 = (bf16[1,128,3584]{2,1,0:T(8,128)(2,1)S(1)}, bf16[1,128,3584]{2,1,0:T(8,128)(2,1)S(1)}, u32[]{:S(2)}, u32[]{:S(2)}) collective-permute-start(bf16[1,128,3584]{2,1,0:T(8,128)(2,1)S(1)} %fusion.8), channel_id=1, source_target_pairs={{0,240},{16,0},{32,16},{48,32},{64,48},{80,64},{96,80},{112,96},{1... | collective-permute-start | bytes 2752520 | tf_op jit(solution)/shard_map/ppermute | solution.py:12
  607.4 46.4 %collective-permute-start = (bf16[1,128,3584]{2,1,0:T(8,128)(2,1)S(1)}, bf16[1,128,3584]{2,1,0:T(8,128)(2,1)S(1)}, u32[]{:S(2)}, u32[]{:S(2)}) collective-permute-start(bf16[1,128,3584]{2,1,0:T(8,128)(2,1)S(1)} %fusion.9), channel_id=1, source_target_pairs={{0,16},{16,32},{32,48},{48,64},{64,80},{80,96},{96,112},{112,128},... | collective-permute-start | bytes 2752520 | tf_op jit(solution)/shard_map/ppermute | solution.py:12
Sparse Core Ops, SparseCore 0:
  9.8 70.5 all-gather.5
  82.3 74.6 all-gather.7
  158.8 77.5 all-gather.3

commit v2 on v1

--- a/solution.py
+++ b/solution.py
@@ -42,14 +42,14 @@
 
 
 def weighted_partial(results, slots, route_weights):
-    groups, tok_rows, route_count = slots.shape
-    valid = slots >= 0
-    index = jnp.where(valid, slots, 0)
-    weight = jnp.where(valid, route_weights, 0.0)
+    groups, slot_total, features = results.shape
+    route_count = slots.shape[2]
+    places = jnp.arange(slot_total, dtype=jnp.int32)
     total = None
     for k in range(route_count):
-        picked = jnp.take_along_axis(results, index[:, :, k, None], axis=1).astype(jnp.float32)
-        term = weight[:, :, k, None] * picked
+        table = (slots[:, :, k, None] == places).astype(jnp.bfloat16)
+        picked = jnp.einsum("gts,gsd->gtd", table, results, preferred_element_type=jnp.float32)
+        term = route_weights[:, :, k, None] * picked
         total = term if total is None else total + term
     return total.astype(jnp.bfloat16)
 
@@ -118,12 +118,16 @@
 
     with jax.named_scope("gather_along_z"):
         fwd_tok_z = gather_z(fwd_tokens)
-        fwd_routes_z = gather_z(fwd_routes)
-        fwd_weights_z = gather_z(fwd_weights)
         bwd_tok_z = gather_z(bwd_tokens)
         bwd_grads_z = gather_z(bwd_grads)
-        bwd_routes_z = gather_z(bwd_routes)
-        bwd_weights_z = gather_z(bwd_weights)
+        meta = jnp.concatenate(
+            [fwd_routes.astype(jnp.float32), fwd_weights, bwd_routes.astype(jnp.float32), bwd_weights], axis=-1
+        )
+        meta_z = gather_z(meta)
+        fwd_routes_z = meta_z[:, :, 0:route_count].astype(jnp.int32)
+        fwd_weights_z = meta_z[:, :, route_count : 2 * route_count]
+        bwd_routes_z = meta_z[:, :, 2 * route_count : 3 * route_count].astype(jnp.int32)
+        bwd_weights_z = meta_z[:, :, 3 * route_count : 4 * route_count]
 
     with jax.named_scope("slots"):
         fwd_slots = local_slots(
@@ -136,8 +140,10 @@
     with jax.named_scope("forward_experts"):
         (fwd_packed,) = pack_rows((fwd_tok_z,), fwd_slots, slot_total)
         fwd_rows = to_experts(fwd_packed, x_count, capacity)
+        fwd_rows, bwd_tok_z = lax.optimization_barrier((fwd_rows, bwd_tok_z))
         fwd_res = forward_work(fwd_rows, w_up, w_down)
         fwd_back = from_experts(fwd_res, z_count, x_count, capacity)
+        fwd_back, bwd_grads_z = lax.optimization_barrier((fwd_back, bwd_grads_z))
         fwd_part = weighted_partial(fwd_back, fwd_slots, fwd_weights_z)
         fwd_out = sum_back(fwd_tokens[0], fwd_part)
 

time: 674 us -> 664 us (0.985)
  local copies, waits for them, and re-layouts: 156 us -> 34.1 us
  waiting for transfers between devices: 295 us -> 341 us
  blocking collectives: 38.7 us -> 78.3 us
  starting transfers between devices: 107 us -> 129 us
  matrix products: 26.9 us -> 42.5 us
  other arithmetic: 24.5 us -> 14.1 us
    gather x4 -> x0, local copies, waits for them, and re-layouts: 118 us -> none  [weighted_partial(): jnp.take_along_axis(results, index[:, :, k, None], axis=1)]
    all_gather x3, waiting for transfers between devices: 152 us -> 55.8 us  [gather_z(): return lax.all_gather(value[0], 'ez', axis=0, tiled=False)]
    all_to_all x0 -> x1, blocking collectives: none -> 63.8 us  [to_experts(): got = lax.all_to_all(spread, 'ex', split_axis=1, concat_axis=1, tiled=True)]
    all_to_all x3 -> x2, waiting for transfers between devices: 40.8 us -> 96.7 us  [to_experts(): got = lax.all_to_all(spread, 'ex', split_axis=1, concat_axis=1, tiled=True)]
    all_to_all x2, waiting for transfers between devices: 45.7 us -> 101 us  [from_experts(): back = lax.all_to_all(spread, 'ex', split_axis=1, concat_axis=1, tiled=True)]
    all_to_all x2, waiting for transfers between devices: 44.3 us -> 80.6 us  [sum_back(): got = lax.all_to_all(partial, 'ez', split_axis=0, concat_axis=0, tiled=True)]
    all_to_all x2, starting transfers between devices: 20.4 us -> 49.7 us  [sum_back(): got = lax.all_to_all(partial, 'ez', split_axis=0, concat_axis=0, tiled=True)]
    all_gather x4 -> x1, blocking collectives: 38.7 us -> 14.4 us  [gather_z(): return lax.all_gather(value[0], 'ez', axis=0, tiled=False)]
  transfers between devices with their start and end apart: 12 -> 11, of which waited for: 8 -> 10; matrix products, arithmetic and copies ran while one was open for 31% -> 9% of each run, Pallas kernels for 0% -> 0%
where the time goes in v2:
time: 664 us; the launch traced here: 652 us
  waiting for transfers between devices  341 us (51%)
  starting transfers between devices  129 us (19%)
  blocking collectives  78.3 us (12%)
  matrix products  42.5 us (6%)
  local copies, waits for them, and re-layouts  34.1 us (5%)
  other arithmetic  14.1 us (2%)
  between operations  14 us (2%)
    all_to_all x2, waiting for transfers between devices, from_experts(): back = lax.all_to_all(spread, 'ex', split_axis=1, concat_axis=1, tiled=True)  101 us
    all_to_all x2, waiting for transfers between devices, to_experts(): got = lax.all_to_all(spread, 'ex', split_axis=1, concat_axis=1, tiled=True)  96.7 us
    all_to_all x2, waiting for transfers between devices, sum_back(): got = lax.all_to_all(partial, 'ez', split_axis=0, concat_axis=0, tiled=True)  80.6 us
    all_to_all x1, blocking collectives, to_experts(): got = lax.all_to_all(spread, 'ex', split_axis=1, concat_axis=1, tiled=True)  63.8 us
    all_gather x3, waiting for transfers between devices, gather_z(): return lax.all_gather(value[0], 'ez', axis=0, tiled=False)  55.8 us
    all_to_all x2, starting transfers between devices, sum_back(): got = lax.all_to_all(partial, 'ez', split_axis=0, concat_axis=0, tiled=True)  49.7 us
    ppermute x2, starting transfers between devices, from_behind(): lax.ppermute(value, axis, [(i, (i + by) % size) for i in range(size)])  45.9 us
    all_to_all x2, starting transfers between devices, from_experts(): back = lax.all_to_all(spread, 'ex', split_axis=1, concat_axis=1, tiled=True)  18 us
  transfers between devices with their start and end apart: 11, of which 10 were waited for; matrix products, arithmetic and copies ran while one was open for 9% of the time, Pallas kernels for 0%

profile of v2, /device:TPU:29, one launch (start us, length us, event | category | flops | bytes accessed | tf_op | source)
XLA Modules:
  0.0 652.3 jit_solution(5818392602407395174)
XLA Ops:
  10.7 14.4 %all_gather.12 = f32[4,128,8]{1,2,0:T(8,128)S(1)} all-gather(f32[1,128,8]{1,2,0:T(8,128)S(1)} %pad_maximum_fusion), channel_id=1, replica_groups=mesh['pp'=16,'ex'=4,'ez'=4] {'ez'}, dimensions={0}, use_global_device_ids=true | all-gather | bytes 20480 | tf_op jit(solution)/shard_map/gather_along_z/all_gather | solution.py:117
  25.6 2.3 reduce-window.16
  28.7 2.3 reduce-window.14
  31.5 1.1 compare_select_fusion
  32.8 47.4 %all-gather.4.cloned.1.call-done = bf16[4,128,3584]{2,1,0:T(8,128)(2,1)} async-done(((bf16[1,128,3584]{2,1,0:T(8,128)(2,1)}), bf16[4,128,3584]{2,1,0:T(8,128)(2,1)}) %all-gather.4.cloned.1.call-update) | async-done | bytes 3670032 | tf_op jit(solution)/shard_map/gather_along_z/all_gather | solution.py:117
  80.1 3.6 convolution_convert_fusion.4
  84.2 63.8 %all_to_all.35 = bf16[4,4,48,3584]{3,2,0,1:T(8,128)(2,1)S(1)} all-to-all(bf16[4,4,48,3584]{3,2,0,1:T(8,128)(2,1)S(1)} %copy.99), channel_id=1, replica_groups=mesh['pp'=16,'ex'=4,'ez'=4] {'ex'}, dimensions={1} | all-to-all | bytes 11010048 | tf_op jit(solution)/shard_map/forward_experts/all_to_all | solution.py:74
  148.0 2.8 copy.100
  150.8 7.1 %all-gather.6.cloned.1.call-done = bf16[4,128,3584]{2,1,0:T(8,128)(2,1)} async-done(((bf16[1,128,3584]{2,1,0:T(8,128)(2,1)}), bf16[4,128,3584]{2,1,0:T(8,128)(2,1)}) %all-gather.6.cloned.1.call-update) | async-done | bytes 3670032 | tf_op jit(solution)/shard_map/gather_along_z/all_gather | solution.py:117
  157.9 7.0 %multiply_convert_fusion.1 = bf16[768,512]{1,0:T(8,128)(2,1)S(1)} fusion(bf16[768,3584]{1,0:T(8,128)(2,1)} %bitcast.94, bf16[1,3584,512]{2,1,0:T(8,128)(2,1)} %param.16), kind=kOutput, calls=%fused_computation.22 | convolution fusion | flops 2820538368 | bytes 9961472 | tf_op jit(solution)/shard_map/forward_experts/dot_general | solution.py:58
  164.9 3.2 convolution_convert_fusion.1
  168.2 2.8 copy.101
  171.0 10.3 %all-to-all-start.1 = ((bf16[4,4,48,3584]{3,2,0,1:T(8,128)(2,1)}), bf16[4,4,48,3584]{3,2,0,1:T(8,128)(2,1)}, u32[]{:S(2)}, u32[]{:S(2)}) async-start(bf16[4,4,48,3584]{3,2,0,1:T(8,128)(2,1)} %copy.101), calls=%async_computation.1 | async-start | bytes 11010048 | tf_op jit(solution)/shard_map/forward_experts/all_to_all | solution.py:81
  182.2 3.6 convolution_convert_fusion.3
  185.8 2.7 copy.112
  188.5 52.4 %all-to-all-done.1 = bf16[4,4,48,3584]{3,2,0,1:T(8,128)(2,1)} async-done(((bf16[4,4,48,3584]{3,2,0,1:T(8,128)(2,1)}), bf16[4,4,48,3584]{3,2,0,1:T(8,128)(2,1)}, u32[]{:S(2)}, u32[]{:S(2)}) %all-to-all-start.1) | async-done | bytes 5505056 | tf_op jit(solution)/shard_map/forward_experts/all_to_all | solution.py:81
  240.9 7.6 %all-to-all-start.3 = ((bf16[4,4,48,3584]{3,2,0,1:T(8,128)(2,1)}), bf16[4,4,48,3584]{3,2,0,1:T(8,128)(2,1)}, u32[]{:S(2)}, u32[]{:S(2)}) async-start(bf16[4,4,48,3584]{3,2,0,1:T(8,128)(2,1)} %copy.112), calls=%async_computation.3 | async-start | bytes 11010048 | tf_op jit(solution)/shard_map/backward_experts/all_to_all | solution.py:74
  248.5 5.4 copy.102
  254.0 1.3 all-gather.8.cloned.1.call-done
  255.3 3.6 convolution_convert_fusion.2
  258.9 2.8 copy.114
  261.8 45.6 %all-to-all-done.3 = bf16[4,4,48,3584]{3,2,0,1:T(8,128)(2,1)} async-done(((bf16[4,4,48,3584]{3,2,0,1:T(8,128)(2,1)}), bf16[4,4,48,3584]{3,2,0,1:T(8,128)(2,1)}, u32[]{:S(2)}, u32[]{:S(2)}) %all-to-all-start.3) | async-done | bytes 5505056 | tf_op jit(solution)/shard_map/backward_experts/all_to_all | solution.py:74
  307.4 7.5 %all-to-all-start.4 = ((bf16[4,4,48,3584]{3,2,0,1:T(8,128)(2,1)}), bf16[4,4,48,3584]{3,2,0,1:T(8,128)(2,1)}, u32[]{:S(2)}, u32[]{:S(2)}) async-start(bf16[4,4,48,3584]{3,2,0,1:T(8,128)(2,1)} %copy.114), calls=%async_computation.4 | async-start | bytes 11010048 | tf_op jit(solution)/shard_map/backward_experts/all_to_all | solution.py:74
  314.9 3.1 copy.113
  318.5 3.0 fusion.4
  321.5 51.1 %all-to-all-done.4 = bf16[4,4,48,3584]{3,2,0,1:T(8,128)(2,1)} async-done(((bf16[4,4,48,3584]{3,2,0,1:T(8,128)(2,1)}), bf16[4,4,48,3584]{3,2,0,1:T(8,128)(2,1)}, u32[]{:S(2)}, u32[]{:S(2)}) %all-to-all-start.4) | async-done | bytes 5505056 | tf_op jit(solution)/shard_map/backward_experts/all_to_all | solution.py:74
  372.7 3.1 copy.115
  376.3 3.3 multiply_convert_fusion
  379.7 3.3 convolution_convert_fusion
  382.9 2.7 copy.116
  385.6 7.7 %all-to-all-start.5 = ((bf16[4,4,48,3584]{3,2,0,1:T(8,128)(2,1)}), bf16[4,4,48,3584]{3,2,0,1:T(8,128)(2,1)}, u32[]{:S(2)}, u32[]{:S(2)}) async-start(bf16[4,4,48,3584]{3,2,0,1:T(8,128)(2,1)} %copy.116), calls=%async_computation.5 | async-start | bytes 11010048 | tf_op jit(solution)/shard_map/backward_experts/all_to_all | solution.py:81
  393.7 3.9 fusion.18
  397.8 3.4 add_convert_fusion.1
  401.2 49.0 %all-to-all-done.5 = bf16[4,4,48,3584]{3,2,0,1:T(8,128)(2,1)} async-done(((bf16[4,4,48,3584]{3,2,0,1:T(8,128)(2,1)}), bf16[4,4,48,3584]{3,2,0,1:T(8,128)(2,1)}, u32[]{:S(2)}, u32[]{:S(2)}) %all-to-all-start.5) | async-done | bytes 5505056 | tf_op jit(solution)/shard_map/backward_experts/all_to_all | solution.py:81
  450.2 11.3 %all-to-all-start.2 = ((bf16[4,128,3584]{2,1,0:T(8,128)(2,1)}), bf16[4,128,3584]{2,1,0:T(8,128)(2,1)}, u32[]{:S(2)}, u32[]{:S(2)}) async-start(bf16[4,128,3584]{2,1,0:T(8,128)(2,1)} %add_convert_fusion.1), calls=%async_computation.2 | async-start | bytes 7340032 | tf_op jit(solution)/shard_map/forward_experts/all_to_all | solution.py:86
  461.8 2.9 copy.117
  464.8 1.2 fusion.19
  465.9 3.4 add_convert_fusion
  469.3 38.5 %all-to-all-done.2 = bf16[4,128,3584]{2,1,0:T(8,128)(2,1)} async-done(((bf16[4,128,3584]{2,1,0:T(8,128)(2,1)}), bf16[4,128,3584]{2,1,0:T(8,128)(2,1)}, u32[]{:S(2)}, u32[]{:S(2)}) %all-to-all-start.2) | async-done | bytes 3670048 | tf_op jit(solution)/shard_map/forward_experts/all_to_all | solution.py:86
  507.8 38.4 %all-to-all-start.6 = ((bf16[4,128,3584]{2,1,0:T(8,128)(2,1)}), bf16[4,128,3584]{2,1,0:T(8,128)(2,1)}, u32[]{:S(2)}, u32[]{:S(2)}) async-start(bf16[4,128,3584]{2,1,0:T(8,128)(2,1)} %add_convert_fusion), calls=%async_computation.6 | async-start | bytes 7340032 | tf_op jit(solution)/shard_map/backward_experts/all_to_all | solution.py:86
  546.2 2.7 convert_reduce_fusion.1
  549.1 5.4 collective-permute-start
  554.5 42.2 %all-to-all-done.6 = bf16[4,128,3584]{2,1,0:T(8,128)(2,1)} async-done(((bf16[4,128,3584]{2,1,0:T(8,128)(2,1)}), bf16[4,128,3584]{2,1,0:T(8,128)(2,1)}, u32[]{:S(2)}, u32[]{:S(2)}) %all-to-all-start.6) | async-done | bytes 3670048 | tf_op jit(solution)/shard_map/backward_experts/all_to_all | solution.py:86
  596.7 2.7 convert_reduce_fusion
  599.6 40.5 %collective-permute-start.1 = (bf16[1,128,3584]{2,1,0:T(8,128)(2,1)S(1)}, bf16[1,128,3584]{2,1,0:T(8,128)(2,1)S(1)}, u32[]{:S(2)}, u32[]{:S(2)}) collective-permute-start(bf16[1,128,3584]{2,1,0:T(8,128)(2,1)S(1)} %fusion.8), channel_id=1, source_target_pairs={{0,240},{16,0},{32,16},{48,32},{64,48},{80,64},{96,80},{112,96},{1... | collective-permute-start | bytes 2752520 | tf_op jit(solution)/shard_map/ppermute | solution.py:12
  640.1 3.9 collective-permute-done.1
  644.0 0.9 copy.121
  644.9 0.9 copy.122
  (66 shorter events, 9.0 us)
Async XLA Ops:
  7.2 73.0 %all-gather.4.cloned.1.call-start = ((), (), s32[]{:S(2)}) async-start(), calls=%async_computation.7 | async-start | bytes 4587520 | tf_op jit(solution)/shard_map/gather_along_z/all_gather | solution.py:117
  7.9 150.0 %all-gather.6.cloned.1.call-start = ((), (), s32[]{:S(2)}) async-start(), calls=%async_computation.8 | async-start | bytes 4587520 | tf_op jit(solution)/shard_map/gather_along_z/all_gather | solution.py:117
  157.9 7.0 %copy-start.2 = (bf16[1,512,3584]{2,1,0:T(8,128)(2,1)S(1)}, bf16[1,512,3584]{2,1,0:T(8,128)(2,1)}, u32[]{:S(2)}) copy-start(bf16[1,512,3584]{2,1,0:T(8,128)(2,1)} %param.17) | copy-start | bytes 11010052
  171.0 69.9 %all-to-all-start.1 = ((bf16[4,4,48,3584]{3,2,0,1:T(8,128)(2,1)}), bf16[4,4,48,3584]{3,2,0,1:T(8,128)(2,1)}, u32[]{:S(2)}, u32[]{:S(2)}) async-start(bf16[4,4,48,3584]{3,2,0,1:T(8,128)(2,1)} %copy.101), calls=%async_computation.1 | async-start | bytes 11010048 | tf_op jit(solution)/shard_map/forward_experts/all_to_all | solution.py:81
  181.2 74.1 %all-gather.8.cloned.1.call-start = ((), (), s32[]{:S(2)}) async-start(), calls=%async_computation.9 | async-start | bytes 4587520 | tf_op jit(solution)/shard_map/gather_along_z/all_gather | solution.py:117
  240.9 66.5 %all-to-all-start.3 = ((bf16[4,4,48,3584]{3,2,0,1:T(8,128)(2,1)}), bf16[4,4,48,3584]{3,2,0,1:T(8,128)(2,1)}, u32[]{:S(2)}, u32[]{:S(2)}) async-start(bf16[4,4,48,3584]{3,2,0,1:T(8,128)(2,1)} %copy.112), calls=%async_computation.3 | async-start | bytes 11010048 | tf_op jit(solution)/shard_map/backward_experts/all_to_all | solution.py:74
  307.4 65.3 %all-to-all-start.4 = ((bf16[4,4,48,3584]{3,2,0,1:T(8,128)(2,1)}), bf16[4,4,48,3584]{3,2,0,1:T(8,128)(2,1)}, u32[]{:S(2)}, u32[]{:S(2)}) async-start(bf16[4,4,48,3584]{3,2,0,1:T(8,128)(2,1)} %copy.114), calls=%async_computation.4 | async-start | bytes 11010048 | tf_op jit(solution)/shard_map/backward_experts/all_to_all | solution.py:74
  314.9 3.7 copy-start.4
  372.7 3.7 copy-start.3
  376.3 3.3 copy-start.5
  385.6 64.6 %all-to-all-start.5 = ((bf16[4,4,48,3584]{3,2,0,1:T(8,128)(2,1)}), bf16[4,4,48,3584]{3,2,0,1:T(8,128)(2,1)}, u32[]{:S(2)}, u32[]{:S(2)}) async-start(bf16[4,4,48,3584]{3,2,0,1:T(8,128)(2,1)} %copy.116), calls=%async_computation.5 | async-start | bytes 11010048 | tf_op jit(solution)/shard_map/backward_experts/all_to_all | solution.py:81
  393.6 3.9 slice-start
  393.7 4.2 slice-start.1
  450.2 57.6 %all-to-all-start.2 = ((bf16[4,128,3584]{2,1,0:T(8,128)(2,1)}), bf16[4,128,3584]{2,1,0:T(8,128)(2,1)}, u32[]{:S(2)}, u32[]{:S(2)}) async-start(bf16[4,128,3584]{2,1,0:T(8,128)(2,1)} %add_convert_fusion.1), calls=%async_computation.2 | async-start | bytes 7340032 | tf_op jit(solution)/shard_map/forward_experts/all_to_all | solution.py:86
  469.3 79.6 %copy-start = (bf16[1,128,3584]{2,1,0:T(8,128)(2,1)S(1)}, bf16[1,128,3584]{2,1,0:T(8,128)(2,1)}, u32[]{:S(2)}) copy-start(bf16[1,128,3584]{2,1,0:T(8,128)(2,1)} %param.9) | copy-start | bytes 2752516
  507.8 88.9 %all-to-all-start.6 = ((bf16[4,128,3584]{2,1,0:T(8,128)(2,1)}), bf16[4,128,3584]{2,1,0:T(8,128)(2,1)}, u32[]{:S(2)}, u32[]{:S(2)}) async-start(bf16[4,128,3584]{2,1,0:T(8,128)(2,1)} %add_convert_fusion), calls=%async_computation.6 | async-start | bytes 7340032 | tf_op jit(solution)/shard_map/backward_experts/all_to_all | solution.py:86
  548.9 50.5 %copy-start.1 = (bf16[1,128,3584]{2,1,0:T(8,128)(2,1)S(1)}, bf16[1,128,3584]{2,1,0:T(8,128)(2,1)}, u32[]{:S(2)}) copy-start(bf16[1,128,3584]{2,1,0:T(8,128)(2,1)} %param.13) | copy-start | bytes 2752516
  549.1 91.0 %collective-permute-start = (bf16[1,128,3584]{2,1,0:T(8,128)(2,1)S(1)}, bf16[1,128,3584]{2,1,0:T(8,128)(2,1)S(1)}, u32[]{:S(2)}, u32[]{:S(2)}) collective-permute-start(bf16[1,128,3584]{2,1,0:T(8,128)(2,1)S(1)} %fusion.9), channel_id=1, source_target_pairs={{0,16},{16,32},{32,48},{48,64},{64,80},{80,96},{96,112},{112,128},... | collective-permute-start | bytes 2752520 | tf_op jit(solution)/shard_map/ppermute | solution.py:12
  599.6 44.3 %collective-permute-start.1 = (bf16[1,128,3584]{2,1,0:T(8,128)(2,1)S(1)}, bf16[1,128,3584]{2,1,0:T(8,128)(2,1)S(1)}, u32[]{:S(2)}, u32[]{:S(2)}) collective-permute-start(bf16[1,128,3584]{2,1,0:T(8,128)(2,1)S(1)} %fusion.8), channel_id=1, source_target_pairs={{0,240},{16,0},{32,16},{48,32},{64,48},{80,64},{96,80},{112,96},{1... | collective-permute-start | bytes 2752520 | tf_op jit(solution)/shard_map/ppermute | solution.py:12
Sparse Core Ops, SparseCore 0:
  9.8 70.2 all-gather.3
  81.9 75.8 all-gather.5
  183.9 71.3 all-gather.7

commit v3 on v2

--- a/solution.py
+++ b/solution.py
@@ -51,7 +51,7 @@
         picked = jnp.einsum("gts,gsd->gtd", table, results, preferred_element_type=jnp.float32)
         term = route_weights[:, :, k, None] * picked
         total = term if total is None else total + term
-    return total.astype(jnp.bfloat16)
+    return total
 
 
 def forward_work(rows, w_up, w_down):
@@ -82,9 +82,10 @@
     return back.reshape(groups, x_count * capacity, features)
 
 
-def sum_back(residual, partial):
-    got = lax.all_to_all(partial, "ez", split_axis=0, concat_axis=0, tiled=True)
-    total = residual.astype(jnp.float32) + jnp.sum(got.astype(jnp.float32), axis=0)
+def sum_back(residual, partial, z_index):
+    own = (jnp.arange(partial.shape[0]) == z_index)[:, None, None]
+    partial = partial + jnp.where(own, residual.astype(jnp.float32)[None], 0.0)
+    total = lax.psum_scatter(partial, "ez", scatter_dimension=0, tiled=False)
     return total.astype(jnp.bfloat16)
 
 
@@ -145,7 +146,7 @@
         fwd_back = from_experts(fwd_res, z_count, x_count, capacity)
         fwd_back, bwd_grads_z = lax.optimization_barrier((fwd_back, bwd_grads_z))
         fwd_part = weighted_partial(fwd_back, fwd_slots, fwd_weights_z)
-        fwd_out = sum_back(fwd_tokens[0], fwd_part)
+        fwd_out = sum_back(fwd_tokens[0], fwd_part, z_index)
 
     with jax.named_scope("backward_experts"):
         bwd_packed, grad_packed = pack_rows((bwd_tok_z, bwd_grads_z), bwd_slots, slot_total)
@@ -154,7 +155,7 @@
         bwd_res = backward_work(bwd_rows, grad_rows, w_up, w_down)
         bwd_back = from_experts(bwd_res, z_count, x_count, capacity)
         bwd_part = weighted_partial(bwd_back, bwd_slots, bwd_weights_z)
-        bwd_out = sum_back(bwd_grads[0], bwd_part)
+        bwd_out = sum_back(bwd_grads[0], bwd_part, z_index)
 
     next_input = from_behind(fwd_out[None], "pp", 1)
     prev_grad = from_behind(bwd_out[None], "pp", -1)

time: 664 us -> 634 us (0.955); the launches traced: 652 us -> 632 us
  waiting for transfers between devices: 341 us -> 457 us
  starting transfers between devices: 129 us -> 48.5 us
  blocking collectives: 78.3 us -> 14.4 us
    reduce_scatter x0 -> x2, waiting for transfers between devices: none -> 136 us  [sum_back(): total = lax.psum_scatter(partial, 'ez', scatter_dimension=0, tiled=False)]
    all_to_all x2 -> x0, waiting for transfers between devices: 80.6 us -> none  [sum_back(): got = lax.all_to_all(partial, 'ez', split_axis=0, concat_axis=0, tiled=True)]
    all_to_all x1 -> x0, blocking collectives: 63.8 us -> none  [to_experts(): got = lax.all_to_all(spread, 'ex', split_axis=1, concat_axis=1, tiled=True)]
    all_to_all x2 -> x0, starting transfers between devices: 49.7 us -> none  [sum_back(): got = lax.all_to_all(partial, 'ez', split_axis=0, concat_axis=0, tiled=True)]
    all_to_all x2 -> x3, waiting for transfers between devices: 96.7 us -> 146 us  [to_experts(): got = lax.all_to_all(spread, 'ex', split_axis=1, concat_axis=1, tiled=True)]
    ppermute x2, starting transfers between devices: 45.9 us -> 8.41 us  [from_behind(): lax.ppermute(value, axis, [(i, (i + by) % size) for i in range(size)])]
    ppermute x2, waiting for transfers between devices: 3.86 us -> 14.5 us  [from_behind(): lax.ppermute(value, axis, [(i, (i + by) % size) for i in range(size)])]
    all_to_all x2, waiting for transfers between devices: 101 us -> 109 us  [from_experts(): back = lax.all_to_all(spread, 'ex', split_axis=1, concat_axis=1, tiled=True)]
  transfers between devices with their start and end apart: 11 -> 12, of which waited for: 10 -> 9; matrix products, arithmetic and copies ran while one was open for 9% -> 15% of each run, Pallas kernels for 0% -> 0%
where the time goes in v3:
time: 634 us; the launch traced here: 632 us
  waiting for transfers between devices  457 us (72%)
  starting transfers between devices  48.5 us (8%)
  matrix products  46.8 us (7%)
  local copies, waits for them, and re-layouts  39.1 us (6%)
  blocking collectives  14.4 us (2%)
  between operations  14 us (2%)
  other arithmetic  11.8 us (2%)
    all_to_all x3, waiting for transfers between devices, to_experts(): got = lax.all_to_all(spread, 'ex', split_axis=1, concat_axis=1, tiled=True)  146 us
    reduce_scatter x2, waiting for transfers between devices, sum_back(): total = lax.psum_scatter(partial, 'ez', scatter_dimension=0, tiled=False)  136 us
    all_to_all x2, waiting for transfers between devices, from_experts(): back = lax.all_to_all(spread, 'ex', split_axis=1, concat_axis=1, tiled=True)  109 us
    all_gather x3, waiting for transfers between devices, gather_z(): return lax.all_gather(value[0], 'ez', axis=0, tiled=False)  49 us
    all_to_all x3, starting transfers between devices, to_experts(): got = lax.all_to_all(spread, 'ex', split_axis=1, concat_axis=1, tiled=True)  20.5 us
    all_to_all x2, starting transfers between devices, from_experts(): back = lax.all_to_all(spread, 'ex', split_axis=1, concat_axis=1, tiled=True)  19.5 us
    dot_general x4, matrix products, weighted_partial(): jnp.einsum('gts,gsd->gtd', table, results, preferred_element_type=jnp.flo...  15.9 us
    ppermute x2, waiting for transfers between devices, from_behind(): lax.ppermute(value, axis, [(i, (i + by) % size) for i in range(size)])  14.5 us
  transfers between devices with their start and end apart: 12, of which 9 were waited for; matrix products, arithmetic and copies ran while one was open for 15% of the time, Pallas kernels for 0%

profile of v3, /device:TPU:29, one launch (start us, length us, event | category | flops | bytes accessed | tf_op | source)
XLA Modules:
  0.0 631.5 jit_solution(12607121215746934315)
XLA Ops:
  7.9 0.7 all-gather.6.cloned.1.call-update
  8.7 0.7 convert_element_type.76
  10.0 0.7 pad_maximum_fusion
  10.7 14.4 %all_gather.12 = f32[4,128,8]{1,2,0:T(8,128)S(1)} all-gather(f32[1,128,8]{1,2,0:T(8,128)S(1)} %pad_maximum_fusion), channel_id=1, replica_groups=mesh['pp'=16,'ex'=4,'ez'=4] {'ez'}, dimensions={0}, use_global_device_ids=true | all-gather | bytes 20480 | tf_op jit(solution)/shard_map/gather_along_z/all_gather | solution.py:118
  25.5 2.3 reduce-window.16
  28.6 2.3 reduce-window.14
  31.5 1.1 compare_select_fusion
  32.7 46.3 %all-gather.4.cloned.1.call-done = bf16[4,128,3584]{2,1,0:T(8,128)(2,1)} async-done(((bf16[1,128,3584]{2,1,0:T(8,128)(2,1)}), bf16[4,128,3584]{2,1,0:T(8,128)(2,1)}) %all-gather.4.cloned.1.call-update) | async-done | bytes 3670032 | tf_op jit(solution)/shard_map/gather_along_z/all_gather | solution.py:118
  79.0 3.6 convolution_convert_fusion.4
  82.6 2.8 copy.99
  85.5 5.1 all-to-all-start
  91.3 57.7 %all-to-all-done = bf16[4,4,48,3584]{3,2,0,1:T(8,128)(2,1)} async-done(((bf16[4,4,48,3584]{3,2,0,1:T(8,128)(2,1)}), bf16[4,4,48,3584]{3,2,0,1:T(8,128)(2,1)}, u32[]{:S(2)}, u32[]{:S(2)}) %all-to-all-start) | async-done | bytes 5505056 | tf_op jit(solution)/shard_map/forward_experts/all_to_all | solution.py:74
  149.0 5.5 copy.100
  154.4 2.7 all-gather.6.cloned.1.call-done
  157.2 7.0 %multiply_convert_fusion.1 = bf16[768,512]{1,0:T(8,128)(2,1)S(1)} fusion(bf16[768,3584]{1,0:T(8,128)(2,1)} %bitcast.92, bf16[1,3584,512]{2,1,0:T(8,128)(2,1)} %param.16), kind=kOutput, calls=%fused_computation.16 | convolution fusion | flops 2820538368 | bytes 9961472 | tf_op jit(solution)/shard_map/forward_experts/dot_general | solution.py:58
  164.2 3.2 convolution_convert_fusion.1
  167.5 2.8 copy.101
  170.3 11.4 %all-to-all-start.1 = ((bf16[4,4,48,3584]{3,2,0,1:T(8,128)(2,1)}), bf16[4,4,48,3584]{3,2,0,1:T(8,128)(2,1)}, u32[]{:S(2)}, u32[]{:S(2)}) async-start(bf16[4,4,48,3584]{3,2,0,1:T(8,128)(2,1)} %copy.101), calls=%async_computation.1 | async-start | bytes 11010048 | tf_op jit(solution)/shard_map/forward_experts/all_to_all | solution.py:81
  182.4 3.9 convolution_convert_fusion.3
  186.3 2.7 copy.112
  189.0 52.4 %all-to-all-done.1 = bf16[4,4,48,3584]{3,2,0,1:T(8,128)(2,1)} async-done(((bf16[4,4,48,3584]{3,2,0,1:T(8,128)(2,1)}), bf16[4,4,48,3584]{3,2,0,1:T(8,128)(2,1)}, u32[]{:S(2)}, u32[]{:S(2)}) %all-to-all-start.1) | async-done | bytes 5505056 | tf_op jit(solution)/shard_map/forward_experts/all_to_all | solution.py:81
  241.4 7.7 %all-to-all-start.2 = ((bf16[4,4,48,3584]{3,2,0,1:T(8,128)(2,1)}), bf16[4,4,48,3584]{3,2,0,1:T(8,128)(2,1)}, u32[]{:S(2)}, u32[]{:S(2)}) async-start(bf16[4,4,48,3584]{3,2,0,1:T(8,128)(2,1)} %copy.112), calls=%async_computation.3 | async-start | bytes 11010048 | tf_op jit(solution)/shard_map/backward_experts/all_to_all | solution.py:74
  249.1 5.5 copy.102
  254.5 3.9 fusion.16
  258.7 5.4 select_add_fusion.1
  264.2 3.6 convolution_convert_fusion.2
  267.8 2.8 copy.114
  270.6 37.2 %all-to-all-done.2 = bf16[4,4,48,3584]{3,2,0,1:T(8,128)(2,1)} async-done(((bf16[4,4,48,3584]{3,2,0,1:T(8,128)(2,1)}), bf16[4,4,48,3584]{3,2,0,1:T(8,128)(2,1)}, u32[]{:S(2)}, u32[]{:S(2)}) %all-to-all-start.2) | async-done | bytes 5505056 | tf_op jit(solution)/shard_map/backward_experts/all_to_all | solution.py:74
  307.8 7.7 %all-to-all-start.3 = ((bf16[4,4,48,3584]{3,2,0,1:T(8,128)(2,1)}), bf16[4,4,48,3584]{3,2,0,1:T(8,128)(2,1)}, u32[]{:S(2)}, u32[]{:S(2)}) async-start(bf16[4,4,48,3584]{3,2,0,1:T(8,128)(2,1)} %copy.114), calls=%async_computation.4 | async-start | bytes 11010048 | tf_op jit(solution)/shard_map/backward_experts/all_to_all | solution.py:74
  315.5 3.1 copy.113
  319.1 3.0 fusion.4
  322.1 51.1 %all-to-all-done.3 = bf16[4,4,48,3584]{3,2,0,1:T(8,128)(2,1)} async-done(((bf16[4,4,48,3584]{3,2,0,1:T(8,128)(2,1)}), bf16[4,4,48,3584]{3,2,0,1:T(8,128)(2,1)}, u32[]{:S(2)}, u32[]{:S(2)}) %all-to-all-start.3) | async-done | bytes 5505056 | tf_op jit(solution)/shard_map/backward_experts/all_to_all | solution.py:74
  373.2 3.1 copy.115
  376.9 3.3 multiply_convert_fusion
  380.2 3.3 convolution_convert_fusion
  383.5 2.7 copy.116
  386.2 8.1 %all-to-all-start.4 = ((bf16[4,4,48,3584]{3,2,0,1:T(8,128)(2,1)}), bf16[4,4,48,3584]{3,2,0,1:T(8,128)(2,1)}, u32[]{:S(2)}, u32[]{:S(2)}) async-start(bf16[4,4,48,3584]{3,2,0,1:T(8,128)(2,1)} %copy.116), calls=%async_computation.5 | async-start | bytes 11010048 | tf_op jit(solution)/shard_map/backward_experts/all_to_all | solution.py:81
  394.8 56.5 %all-to-all-done.4 = bf16[4,4,48,3584]{3,2,0,1:T(8,128)(2,1)} async-done(((bf16[4,4,48,3584]{3,2,0,1:T(8,128)(2,1)}), bf16[4,4,48,3584]{3,2,0,1:T(8,128)(2,1)}, u32[]{:S(2)}, u32[]{:S(2)}) %all-to-all-start.4) | async-done | bytes 5505056 | tf_op jit(solution)/shard_map/backward_experts/all_to_all | solution.py:81
  451.3 2.9 copy.117
  454.2 1.2 fusion.17
  455.4 5.5 select_add_fusion
  460.9 1.6 convert_element_type.84
  462.5 7.9 %collective-permute-start = (bf16[1,128,3584]{2,1,0:T(8,128)(2,1)S(1)}, bf16[1,128,3584]{2,1,0:T(8,128)(2,1)S(1)}, u32[]{:S(2)}, u32[]{:S(2)}) collective-permute-start(bf16[1,128,3584]{2,1,0:T(8,128)(2,1)S(1)} %convert_element_type.84), channel_id=1, source_target_pairs={{0,16},{16,32},{32,48},{48,64},{64,80},{80,96},{96,112},{112,128},... | collective-permute-start | bytes 2752520 | tf_op jit(solution)/shard_map/ppermute | solution.py:12
  470.4 136.1 %reduce-scatter.5.cloned.1.call-done = f32[1,128,3584]{2,1,0:T(8,128)} async-done(((f32[4,128,3584]{2,1,0:T(8,128)}), f32[1,128,3584]{2,1,0:T(8,128)}) %reduce-scatter.5.cloned.1.call-update) | async-done | bytes 1835024 | tf_op jit(solution)/shard_map/backward_experts/reduce_scatter | solution.py:88
  606.5 1.6 convert_element_type.93
  608.6 14.5 %collective-permute-done.1 = bf16[1,128,3584]{2,1,0:T(8,128)(2,1)S(1)} collective-permute-done((bf16[1,128,3584]{2,1,0:T(8,128)(2,1)S(1)}, bf16[1,128,3584]{2,1,0:T(8,128)(2,1)S(1)}, u32[]{:S(2)}, u32[]{:S(2)}) %collective-permute-start.1) | collective-permute-done | bytes 917536 | tf_op jit(solution)/shard_map/ppermute | solution.py:12
  623.1 0.9 copy.121
  624.1 0.9 copy.122
  (70 shorter events, 7.1 us)
Async XLA Ops:
  7.2 71.9 %all-gather.4.cloned.1.call-start = ((), (), s32[]{:S(2)}) async-start(), calls=%async_computation.7 | async-start | bytes 4587520 | tf_op jit(solution)/shard_map/gather_along_z/all_gather | solution.py:118
  7.9 149.3 %all-gather.6.cloned.1.call-start = ((), (), s32[]{:S(2)}) async-start(), calls=%async_computation.8 | async-start | bytes 4587520 | tf_op jit(solution)/shard_map/gather_along_z/all_gather | solution.py:118
  85.5 63.5 %all-to-all-start = ((bf16[4,4,48,3584]{3,2,0,1:T(8,128)(2,1)}), bf16[4,4,48,3584]{3,2,0,1:T(8,128)(2,1)}, u32[]{:S(2)}, u32[]{:S(2)}) async-start(bf16[4,4,48,3584]{3,2,0,1:T(8,128)(2,1)} %copy.99), calls=%async_computation | async-start | bytes 11010048 | tf_op jit(solution)/shard_map/forward_experts/all_to_all | solution.py:74
  90.5 164.0 %all-gather.8.cloned.1.call-start = ((), (), s32[]{:S(2)}) async-start(), calls=%async_computation.9 | async-start | bytes 4587520 | tf_op jit(solution)/shard_map/gather_along_z/all_gather | solution.py:118
  157.2 7.0 %copy-start.2 = (bf16[1,512,3584]{2,1,0:T(8,128)(2,1)S(1)}, bf16[1,512,3584]{2,1,0:T(8,128)(2,1)}, u32[]{:S(2)}) copy-start(bf16[1,512,3584]{2,1,0:T(8,128)(2,1)} %param.17) | copy-start | bytes 11010052
  170.3 11.9 %copy-start = (bf16[1,128,3584]{2,1,0:T(8,128)(2,1)S(1)}, bf16[1,128,3584]{2,1,0:T(8,128)(2,1)}, u32[]{:S(2)}) copy-start(bf16[1,128,3584]{2,1,0:T(8,128)(2,1)} %param.9) | copy-start | bytes 2752516
  170.3 71.1 %all-to-all-start.1 = ((bf16[4,4,48,3584]{3,2,0,1:T(8,128)(2,1)}), bf16[4,4,48,3584]{3,2,0,1:T(8,128)(2,1)}, u32[]{:S(2)}, u32[]{:S(2)}) async-start(bf16[4,4,48,3584]{3,2,0,1:T(8,128)(2,1)} %copy.101), calls=%async_computation.1 | async-start | bytes 11010048 | tf_op jit(solution)/shard_map/forward_experts/all_to_all | solution.py:81
  241.4 66.4 %all-to-all-start.2 = ((bf16[4,4,48,3584]{3,2,0,1:T(8,128)(2,1)}), bf16[4,4,48,3584]{3,2,0,1:T(8,128)(2,1)}, u32[]{:S(2)}, u32[]{:S(2)}) async-start(bf16[4,4,48,3584]{3,2,0,1:T(8,128)(2,1)} %copy.112), calls=%async_computation.3 | async-start | bytes 11010048 | tf_op jit(solution)/shard_map/backward_experts/all_to_all | solution.py:74
  249.1 211.8 %reduce-scatter.3.cloned.1.call-start = ((), (), s32[]{:S(2)}) async-start(), calls=%async_computation.10 | async-start | bytes 9175040 | tf_op jit(solution)/shard_map/forward_experts/reduce_scatter | solution.py:88
  254.5 3.9 slice-start
  254.5 4.2 slice-start.1
  307.8 65.5 %all-to-all-start.3 = ((bf16[4,4,48,3584]{3,2,0,1:T(8,128)(2,1)}), bf16[4,4,48,3584]{3,2,0,1:T(8,128)(2,1)}, u32[]{:S(2)}, u32[]{:S(2)}) async-start(bf16[4,4,48,3584]{3,2,0,1:T(8,128)(2,1)} %copy.114), calls=%async_computation.4 | async-start | bytes 11010048 | tf_op jit(solution)/shard_map/backward_experts/all_to_all | solution.py:74
  315.5 3.7 copy-start.4
  373.2 3.7 copy-start.3
  376.9 3.3 copy-start.5
  386.2 8.3 %copy-start.1 = (bf16[1,128,3584]{2,1,0:T(8,128)(2,1)S(1)}, bf16[1,128,3584]{2,1,0:T(8,128)(2,1)}, u32[]{:S(2)}) copy-start(bf16[1,128,3584]{2,1,0:T(8,128)(2,1)} %param.13) | copy-start | bytes 2752516
  386.2 65.1 %all-to-all-start.4 = ((bf16[4,4,48,3584]{3,2,0,1:T(8,128)(2,1)}), bf16[4,4,48,3584]{3,2,0,1:T(8,128)(2,1)}, u32[]{:S(2)}, u32[]{:S(2)}) async-start(bf16[4,4,48,3584]{3,2,0,1:T(8,128)(2,1)} %copy.116), calls=%async_computation.5 | async-start | bytes 11010048 | tf_op jit(solution)/shard_map/backward_experts/all_to_all | solution.py:81
  394.3 212.2 %reduce-scatter.5.cloned.1.call-start = ((), (), s32[]{:S(2)}) async-start(), calls=%async_computation.11 | async-start | bytes 9175040 | tf_op jit(solution)/shard_map/backward_experts/reduce_scatter | solution.py:88
  462.5 146.1 %collective-permute-start = (bf16[1,128,3584]{2,1,0:T(8,128)(2,1)S(1)}, bf16[1,128,3584]{2,1,0:T(8,128)(2,1)S(1)}, u32[]{:S(2)}, u32[]{:S(2)}) collective-permute-start(bf16[1,128,3584]{2,1,0:T(8,128)(2,1)S(1)} %convert_element_type.84), channel_id=1, source_target_pairs={{0,16},{16,32},{32,48},{48,64},{64,80},{80,96},{96,112},{112,128},... | collective-permute-start | bytes 2752520 | tf_op jit(solution)/shard_map/ppermute | solution.py:12
  608.1 15.0 %collective-permute-start.1 = (bf16[1,128,3584]{2,1,0:T(8,128)(2,1)S(1)}, bf16[1,128,3584]{2,1,0:T(8,128)(2,1)S(1)}, u32[]{:S(2)}, u32[]{:S(2)}) collective-permute-start(bf16[1,128,3584]{2,1,0:T(8,128)(2,1)S(1)} %convert_element_type.93), channel_id=1, source_target_pairs={{0,240},{16,0},{32,16},{48,32},{64,48},{80,64},{96,80},{112,96},{1... | collective-permute-start | bytes 2752520 | tf_op jit(solution)/shard_map/ppermute | solution.py:12
Sparse Core Ops, SparseCore 0:
  9.8 69.1 all-gather.3
  80.8 76.3 all-gather.5
  159.0 76.5 all-gather.7
  264.3 142.0 reduce-scatter.2
  461.0 145.5 reduce-scatter.4

commit v4 on v2

--- a/solution.py
+++ b/solution.py
@@ -26,32 +26,35 @@
 
 
 def local_slots(chosen, position, expert_class, class_count, capacity):
+    groups = chosen.shape[0]
     column = chosen // class_count
     mine = (chosen % class_count) == expert_class
-    return jnp.where(mine, column * capacity + position, -1)
+    group = jnp.arange(groups, dtype=jnp.int32)[:, None, None]
+    return jnp.where(mine, (column * groups + group) * capacity + position, -1)
 
 
-def pack_rows(sources, slots, slot_total):
-    table = jnp.sum(
-        (slots[..., None] == jnp.arange(slot_total, dtype=jnp.int32)).astype(jnp.bfloat16), axis=2
-    )
-    return tuple(
-        jnp.einsum("gts,gtd->gsd", table, member, preferred_element_type=jnp.float32).astype(jnp.bfloat16)
-        for member in sources
-    )
+def slot_table(slots, slot_total):
+    flat = slots.reshape(-1, slots.shape[-1])
+    return jnp.sum((flat[..., None] == jnp.arange(slot_total, dtype=jnp.int32)).astype(jnp.bfloat16), axis=1)
 
 
-def weighted_partial(results, slots, route_weights):
-    groups, slot_total, features = results.shape
-    route_count = slots.shape[2]
+def pack_rows(member, table):
+    flat = member.reshape(-1, member.shape[-1])
+    return lax.dot_general(
+        table, flat, (((0,), (0,)), ((), ())), preferred_element_type=jnp.float32
+    ).astype(jnp.bfloat16)
+
+
+def weighted_partial(results, slots, route_weights, slot_total):
+    groups, tok_rows, route_count = slots.shape
     places = jnp.arange(slot_total, dtype=jnp.int32)
     total = None
     for k in range(route_count):
-        table = (slots[:, :, k, None] == places).astype(jnp.bfloat16)
-        picked = jnp.einsum("gts,gsd->gtd", table, results, preferred_element_type=jnp.float32)
-        term = route_weights[:, :, k, None] * picked
+        table = (slots[:, :, k].reshape(-1, 1) == places).astype(jnp.bfloat16)
+        picked = jnp.dot(table, results, preferred_element_type=jnp.float32)
+        term = route_weights[:, :, k].reshape(-1, 1) * picked
         total = term if total is None else total + term
-    return total.astype(jnp.bfloat16)
+    return total.reshape(groups, tok_rows, -1)
 
 
 def forward_work(rows, w_up, w_down):
@@ -68,23 +71,20 @@
     ).astype(jnp.bfloat16)
 
 
-def to_experts(packed, x_count, capacity):
-    groups, slot_total, features = packed.shape
-    spread = packed.reshape(groups, x_count, capacity, features)
-    got = lax.all_to_all(spread, "ex", split_axis=1, concat_axis=1, tiled=True)
-    return got.reshape(groups * x_count * capacity, features)
+def swap_x(rows, x_count):
+    spread = rows.reshape((x_count, -1) + rows.shape[1:])
+    got = lax.all_to_all(spread, "ex", split_axis=0, concat_axis=0, tiled=True)
+    return got.reshape(rows.shape)
 
 
-def from_experts(rows, groups, x_count, capacity):
-    features = rows.shape[-1]
-    spread = rows.reshape(groups, x_count, capacity, features)
-    back = lax.all_to_all(spread, "ex", split_axis=1, concat_axis=1, tiled=True)
-    return back.reshape(groups, x_count * capacity, features)
-
-
-def sum_back(residual, partial):
-    got = lax.all_to_all(partial, "ez", split_axis=0, concat_axis=0, tiled=True)
-    total = residual.astype(jnp.float32) + jnp.sum(got.astype(jnp.float32), axis=0)
+def sum_back(residual, partial, z_index, wire_type):
+    if wire_type == jnp.float32:
+        own = (jnp.arange(partial.shape[0]) == z_index)[:, None, None]
+        partial = partial + jnp.where(own, residual.astype(jnp.float32)[None], 0.0)
+        total = lax.psum_scatter(partial, "ez", scatter_dimension=0, tiled=False)
+    else:
+        summed = lax.psum_scatter(partial.astype(wire_type), "ez", scatter_dimension=0, tiled=False)
+        total = residual.astype(jnp.float32) + summed.astype(jnp.float32)
     return total.astype(jnp.bfloat16)
 
 
@@ -107,7 +107,7 @@
     tok_rows = fwd_tokens.shape[1]
     route_count = fwd_routes.shape[2]
     capacity = 3 * tok_rows * route_count // ep_count
-    slot_total = x_count * capacity
+    slot_total = x_count * z_count * capacity
     z_index = lax.axis_index("ez")
     expert_class = z_index // (z_count // class_count)
     w_up = up_proj[0]
@@ -138,23 +138,32 @@
         )
 
     with jax.named_scope("forward_experts"):
-        (fwd_packed,) = pack_rows((fwd_tok_z,), fwd_slots, slot_total)
-        fwd_rows = to_experts(fwd_packed, x_count, capacity)
+        fwd_table = slot_table(fwd_slots, slot_total)
+        fwd_rows = swap_x(pack_rows(fwd_tok_z, fwd_table), x_count)
         fwd_rows, bwd_tok_z = lax.optimization_barrier((fwd_rows, bwd_tok_z))
         fwd_res = forward_work(fwd_rows, w_up, w_down)
-        fwd_back = from_experts(fwd_res, z_count, x_count, capacity)
+        fwd_back = swap_x(fwd_res, x_count)
         fwd_back, bwd_grads_z = lax.optimization_barrier((fwd_back, bwd_grads_z))
-        fwd_part = weighted_partial(fwd_back, fwd_slots, fwd_weights_z)
-        fwd_out = sum_back(fwd_tokens[0], fwd_part)
+        fwd_part = weighted_partial(fwd_back, fwd_slots, fwd_weights_z, slot_total)
+        fwd_out = sum_back(fwd_tokens[0], fwd_part, z_index, jnp.float32)
 
     with jax.named_scope("backward_experts"):
-        bwd_packed, grad_packed = pack_rows((bwd_tok_z, bwd_grads_z), bwd_slots, slot_total)
-        bwd_rows = to_experts(bwd_packed, x_count, capacity)
-        grad_rows = to_experts(grad_packed, x_count, capacity)
+        bwd_table = slot_table(bwd_slots, slot_total)
+        features = bwd_tok_z.shape[-1]
+        both = jnp.stack(
+            [
+                pack_rows(bwd_tok_z, bwd_table).reshape(x_count, -1, features),
+                pack_rows(bwd_grads_z, bwd_table).reshape(x_count, -1, features),
+            ],
+            axis=1,
+        )
+        both = swap_x(both, x_count)
+        bwd_rows = both[:, 0].reshape(-1, features)
+        grad_rows = both[:, 1].reshape(-1, features)
         bwd_res = backward_work(bwd_rows, grad_rows, w_up, w_down)
-        bwd_back = from_experts(bwd_res, z_count, x_count, capacity)
-        bwd_part = weighted_partial(bwd_back, bwd_slots, bwd_weights_z)
-        bwd_out = sum_back(bwd_grads[0], bwd_part)
+        bwd_back = swap_x(bwd_res, x_count)
+        bwd_part = weighted_partial(bwd_back, bwd_slots, bwd_weights_z, slot_total)
+        bwd_out = sum_back(bwd_grads[0], bwd_part, z_index, jnp.bfloat16)
 
     next_input = from_behind(fwd_out[None], "pp", 1)
     prev_grad = from_behind(bwd_out[None], "pp", -1)

time: 664 us -> 591 us (0.89); the launches traced: 652 us -> 590 us
  starting transfers between devices: 129 us -> 42.6 us
  waiting for transfers between devices: 341 us -> 415 us
  blocking collectives: 78.3 us -> 14.4 us
  matrix products: 42.5 us -> 69.2 us
  local copies, waits for them, and re-layouts: 34.1 us -> 13.9 us
  other arithmetic: 14.1 us -> 20.9 us
    all_to_all x6 -> x4, waiting for transfers between devices: 279 us -> 162 us  [swap_x(): got = lax.all_to_all(spread, 'ex', split_axis=0, concat_axis=0, tiled=True)]
    all_gather x3, waiting for transfers between devices: 55.8 us -> 162 us  [gather_z(): return lax.all_gather(value[0], 'ez', axis=0, tiled=False)]
    reduce_scatter x0 -> x2, waiting for transfers between devices: none -> 75 us  [the longest x1 75 us: sum_back(): lax.psum_scatter(partial.astype(wire_type), 'ez', scatter_dimension=0, ti...]
    all_to_all x1 -> x0, blocking collectives: 63.8 us -> none  [to_experts(): got = lax.all_to_all(spread, 'ex', split_axis=1, concat_axis=1, tiled=True)]
    all_to_all x6 -> x4, starting transfers between devices: 82.9 us -> 32.4 us  [swap_x(): got = lax.all_to_all(spread, 'ex', split_axis=0, concat_axis=0, tiled=True)]
    ppermute x2, starting transfers between devices: 45.9 us -> 10 us  [from_behind(): lax.ppermute(value, axis, [(i, (i + by) % size) for i in range(size)])]
    dot_general x7, matrix products: 22.6 us -> 43 us  [the longest x4 23.7 us: weighted_partial(): picked = jnp.dot(table, results, preferred_element_type=jnp.float32)]
    all_to_all x5 -> x0, local copies, waits for them, and re-layouts: 17.3 us -> none  [the longest x3 8.92 us: to_experts(): got = lax.all_to_all(spread, 'ex', split_axis=1, concat_axis=1, tiled=True)]
  transfers between devices with their start and end apart: 11 -> 11, of which waited for: 10 -> 7; matrix products, arithmetic and copies ran while one was open for 9% -> 15% of each run, Pallas kernels for 0% -> 0%
where the time goes in v4:
time: 591 us; the launch traced here: 590 us
  waiting for transfers between devices  415 us (70%)
  matrix products  69.2 us (12%)
  starting transfers between devices  42.6 us (7%)
  other arithmetic  20.9 us (4%)
  blocking collectives  14.4 us (2%)
  between operations  14 us (2%)
  local copies, waits for them, and re-layouts  13.9 us (2%)
    all_to_all x4, waiting for transfers between devices, swap_x(): got = lax.all_to_all(spread, 'ex', split_axis=0, concat_axis=0, tiled=True)  162 us
    all_gather x3, waiting for transfers between devices, gather_z(): return lax.all_gather(value[0], 'ez', axis=0, tiled=False)  162 us
    reduce_scatter x1, waiting for transfers between devices, sum_back(): lax.psum_scatter(partial.astype(wire_type), 'ez', scatter_dimension=0, ti...  75 us
    all_to_all x4, starting transfers between devices, swap_x(): got = lax.all_to_all(spread, 'ex', split_axis=0, concat_axis=0, tiled=True)  32.4 us
    dot_general x4, matrix products, weighted_partial(): picked = jnp.dot(table, results, preferred_element_type=jnp.float32)  23.7 us
    dot_general x3, matrix products, pack_rows(): lax.dot_general(table, flat, (((0,), (0,)), ((), ())), preferred_element_...  19.3 us
    ppermute x2, waiting for transfers between devices, from_behind(): lax.ppermute(value, axis, [(i, (i + by) % size) for i in range(size)])  14.5 us
    all_gather x1, blocking collectives, gather_z(): return lax.all_gather(value[0], 'ez', axis=0, tiled=False)  14.4 us
  transfers between devices with their start and end apart: 11, of which 7 were waited for; matrix products, arithmetic and copies ran while one was open for 15% of the time, Pallas kernels for 0%

profile of v4, /device:TPU:29, one launch (start us, length us, event | category | flops | bytes accessed | tf_op | source)
XLA Modules:
  0.0 590.5 jit_solution(9834440840620299154)
XLA Ops:
  7.2 0.7 all-gather.4.cloned.1.call-update
  7.9 0.7 all-gather.6.cloned.1.call-update
  8.7 0.7 convert_element_type.88
  9.3 0.7 convert_element_type.87
  10.0 0.7 pad_maximum_fusion
  10.7 14.4 %all_gather.12 = f32[4,128,8]{1,2,0:T(8,128)S(1)} all-gather(f32[1,128,8]{1,2,0:T(8,128)S(1)} %pad_maximum_fusion), channel_id=1, replica_groups=mesh['pp'=16,'ex'=4,'ez'=4] {'ez'}, dimensions={0}, use_global_device_ids=true | all-gather | bytes 20480 | tf_op jit(solution)/shard_map/gather_along_z/all_gather | solution.py:117
  25.2 0.2 copy.86
  25.5 2.3 reduce-window.16
  28.6 2.3 reduce-window.14
  31.5 1.2 compare_select_fusion
  32.7 0.4 fusion.11
  33.1 45.9 %all-gather.4.cloned.1.call-done = bf16[4,128,3584]{2,1,0:T(8,128)(2,1)} async-done(((bf16[1,128,3584]{2,1,0:T(8,128)(2,1)}), bf16[4,128,3584]{2,1,0:T(8,128)(2,1)}) %all-gather.4.cloned.1.call-update) | async-done | bytes 3670032 | tf_op jit(solution)/shard_map/gather_along_z/all_gather | solution.py:117
  79.0 6.9 %convolution_convert_fusion.4 = bf16[768,3584]{1,0:T(8,128)(2,1)} fusion(bf16[512,768]{1,0:T(8,128)(2,1)S(1)} %fusion.11, bf16[512,3584]{1,0:T(8,128)(2,1)} %bitcast.132), kind=kOutput, calls=%fused_computation.8 | convolution fusion | flops 2821324800 | bytes 9961472 | tf_op jit(solution)/shard_map/forward_experts/dot_general | solution.py:43
  85.9 5.2 all-to-all-start
  91.2 0.7 all-gather.8.cloned.1.call-update
  91.8 65.3 %all-gather.6.cloned.1.call-done = bf16[4,128,3584]{2,1,0:T(8,128)(2,1)} async-done(((bf16[1,128,3584]{2,1,0:T(8,128)(2,1)}), bf16[4,128,3584]{2,1,0:T(8,128)(2,1)}) %all-gather.6.cloned.1.call-update) | async-done | bytes 3670032 | tf_op jit(solution)/shard_map/gather_along_z/all_gather | solution.py:117
  157.1 7.0 %multiply_convert_fusion.1 = bf16[768,512]{1,0:T(8,128)(2,1)S(1)} fusion(bf16[768,3584]{1,0:T(8,128)(2,1)} %bitcast.10, bf16[1,3584,512]{2,1,0:T(8,128)(2,1)} %param.16), kind=kOutput, calls=%fused_computation.28 | convolution fusion | flops 2820538368 | bytes 9961472 | tf_op jit(solution)/shard_map/forward_experts/dot_general | solution.py:61
  164.2 4.8 convolution_convert_fusion.3
  169.0 7.6 %all-to-all-start.1 = ((bf16[4,192,3584]{2,1,0:T(8,128)(2,1)}), bf16[4,192,3584]{2,1,0:T(8,128)(2,1)}, u32[]{:S(2)}, u32[]{:S(2)}) async-start(bf16[4,192,3584]{2,1,0:T(8,128)(2,1)} %bitcast.105), calls=%async_computation.1 | async-start | bytes 11010048 | tf_op jit(solution)/shard_map/forward_experts/all_to_all | solution.py:76
  176.9 0.4 fusion.10
  177.3 0.2 bitcast_convert_fusion
  177.5 0.7 copy-done.4
  178.2 6.9 %convolution_convert_fusion.2 = bf16[768,3584]{1,0:T(8,128)(2,1)} fusion(bf16[512,768]{1,0:T(8,128)(2,1)S(1)} %fusion.10, bf16[512,3584]{1,0:T(8,128)(2,1)} %bitcast.131), kind=kOutput, calls=%fused_computation.6 | convolution fusion | flops 2821324800 | bytes 9961472 | tf_op jit(solution)/shard_map/backward_experts/dot_general | solution.py:43
  185.1 50.5 %all-gather.8.cloned.1.call-done = bf16[4,128,3584]{2,1,0:T(8,128)(2,1)} async-done(((bf16[1,128,3584]{2,1,0:T(8,128)(2,1)}), bf16[4,128,3584]{2,1,0:T(8,128)(2,1)}) %all-gather.8.cloned.1.call-update) | async-done | bytes 3670032 | tf_op jit(solution)/shard_map/gather_along_z/all_gather | solution.py:117
  235.6 5.5 convolution_convert_fusion.1
  241.1 4.8 maximum_bitcast_fusion
  245.9 12.0 %all-to-all-start.2 = ((bf16[4,1,2,192,3584]{4,3,2,1,0:T(8,128)(2,1)}), bf16[4,1,2,192,3584]{4,3,2,1,0:T(8,128)(2,1)}, u32[]{:S(2)}, u32[]{:S(2)}) async-start(bf16[4,1,2,192,3584]{4,3,2,1,0:T(8,128)(2,1)} %maximum_bitcast_fusion), calls=%async_computation.3 | async-start | bytes 22020096 | tf_op jit(solution)/shard_map/backward_experts/all_to_all | solution.py:76
  258.0 5.2 fusion.12
  263.2 5.9 multiply_add_fusion
  269.0 4.0 select_add_fusion
  273.0 103.6 %all-to-all-done.2 = bf16[4,1,2,192,3584]{4,3,2,1,0:T(8,128)(2,1)} async-done(((bf16[4,1,2,192,3584]{4,3,2,1,0:T(8,128)(2,1)}), bf16[4,1,2,192,3584]{4,3,2,1,0:T(8,128)(2,1)}, u32[]{:S(2)}, u32[]{:S(2)}) %all-to-all-start.2) | async-done | bytes 11010080 | tf_op jit(solution)/shard_map/backward_experts/all_to_all | solution.py:76
  376.6 9.1 %fusion.32 = (bf16[4,1,192,3584]{3,2,1,0:T(8,128)(2,1)}, bf16[4,1,192,3584]{3,2,1,0:T(8,128)(2,1)}) fusion(bf16[4,2,192,3584]{3,2,1,0:T(8,128)(2,1)} %bitcast.34), kind=kLoop, calls=%fused_computation.69 | loop fusion | bytes 22020096 | tf_op jit(solution)/shard_map/backward_experts/slice | solution.py:162
  385.7 6.2 %fusion.4 = f32[768,512]{1,0:T(8,128)S(1)} fusion(bf16[768,3584]{1,0:T(8,128)(2,1)} %bitcast.111, bf16[1,3584,512]{2,1,0:T(8,128)(2,1)} %param.16), kind=kOutput, calls=%fused_computation.13 | convolution fusion | flops 2818572288 | bytes 10747904 | tf_op jit(solution)/shard_map/backward_experts/dot_general | solution.py:66
  391.9 0.3 copy-done.6
  392.2 3.3 multiply_convert_fusion
  395.5 4.9 convolution_convert_fusion
  400.4 7.7 %all-to-all-start.3 = ((bf16[4,192,3584]{2,1,0:T(8,128)(2,1)}), bf16[4,192,3584]{2,1,0:T(8,128)(2,1)}, u32[]{:S(2)}, u32[]{:S(2)}) async-start(bf16[4,192,3584]{2,1,0:T(8,128)(2,1)} %bitcast.107), calls=%async_computation.4 | async-start | bytes 11010048 | tf_op jit(solution)/shard_map/backward_experts/all_to_all | solution.py:76
  408.3 58.5 %all-to-all-done.3 = bf16[4,192,3584]{2,1,0:T(8,128)(2,1)} async-done(((bf16[4,192,3584]{2,1,0:T(8,128)(2,1)}), bf16[4,192,3584]{2,1,0:T(8,128)(2,1)}, u32[]{:S(2)}, u32[]{:S(2)}) %all-to-all-start.3) | async-done | bytes 5505056 | tf_op jit(solution)/shard_map/backward_experts/all_to_all | solution.py:76
  466.8 5.2 fusion.13
  471.9 7.5 %add_convert_fusion = bf16[512,3584]{1,0:T(8,128)(2,1)} fusion(f32[512,3584]{1,0:T(8,128)S(1)} %fusion.13, bf16[768,3584]{1,0:T(8,128)(2,1)} %bitcast.38, f32[512]{0:T(512)S(1)} %bitcast.128, f32[512]{0:T(512)S(1)} %bitcast.127, s32[512]{0:T(512)S(1)} %bitcast.125), kind=kOutput, calls=%fused_computation.1 | convolution fusion | flops 2826305536 | bytes 16521216 | tf_op jit(solution)/shard_map/backward_experts/dot_general | solution.py:54
  479.5 1.7 convert_element_type.96
  481.1 9.6 %collective-permute-start = (bf16[1,128,3584]{2,1,0:T(8,128)(2,1)S(1)}, bf16[1,128,3584]{2,1,0:T(8,128)(2,1)S(1)}, u32[]{:S(2)}, u32[]{:S(2)}) collective-permute-start(bf16[1,128,3584]{2,1,0:T(8,128)(2,1)S(1)} %convert_element_type.96), channel_id=1, source_target_pairs={{0,16},{16,32},{32,48},{48,64},{64,80},{80,96},{96,112},{112,128},... | collective-permute-start | bytes 2752520 | tf_op jit(solution)/shard_map/ppermute | solution.py:12
  490.7 75.0 %reduce-scatter.5.cloned.1.call-done = bf16[1,128,3584]{2,1,0:T(8,128)(2,1)} async-done(((bf16[4,128,3584]{2,1,0:T(8,128)(2,1)}), bf16[1,128,3584]{2,1,0:T(8,128)(2,1)}) %reduce-scatter.5.cloned.1.call-update) | async-done | bytes 917520 | tf_op jit(solution)/shard_map/backward_experts/reduce_scatter | solution.py:86
  565.7 1.4 add_convert_fusion.1
  567.1 0.5 collective-permute-start.1
  567.6 14.5 %collective-permute-done.1 = bf16[1,128,3584]{2,1,0:T(8,128)(2,1)S(1)} collective-permute-done((bf16[1,128,3584]{2,1,0:T(8,128)(2,1)S(1)}, bf16[1,128,3584]{2,1,0:T(8,128)(2,1)S(1)}, u32[]{:S(2)}, u32[]{:S(2)}) %collective-permute-start.1) | collective-permute-done | bytes 917536 | tf_op jit(solution)/shard_map/ppermute | solution.py:12
  582.1 0.9 copy.105
  583.0 0.9 copy.106
  (61 shorter events, 2.4 us)
Async XLA Ops:
  7.2 71.9 %all-gather.4.cloned.1.call-start = ((), (), s32[]{:S(2)}) async-start(), calls=%async_computation.6 | async-start | bytes 4587520 | tf_op jit(solution)/shard_map/gather_along_z/all_gather | solution.py:117
  7.9 149.2 %all-gather.6.cloned.1.call-start = ((), (), s32[]{:S(2)}) async-start(), calls=%async_computation.7 | async-start | bytes 4587520 | tf_op jit(solution)/shard_map/gather_along_z/all_gather | solution.py:117
  85.9 71.2 %all-to-all-start = ((bf16[4,192,3584]{2,1,0:T(8,128)(2,1)}), bf16[4,192,3584]{2,1,0:T(8,128)(2,1)}, u32[]{:S(2)}, u32[]{:S(2)}) async-start(bf16[4,192,3584]{2,1,0:T(8,128)(2,1)} %bitcast.106), calls=%async_computation | async-start | bytes 11010048 | tf_op jit(solution)/shard_map/forward_experts/all_to_all | solution.py:76
  91.1 144.5 %all-gather.8.cloned.1.call-start = ((), (), s32[]{:S(2)}) async-start(), calls=%async_computation.8 | async-start | bytes 4587520 | tf_op jit(solution)/shard_map/gather_along_z/all_gather | solution.py:117
  157.1 7.0 %copy-start.5 = (bf16[1,512,3584]{2,1,0:T(8,128)(2,1)S(1)}, bf16[1,512,3584]{2,1,0:T(8,128)(2,1)}, u32[]{:S(2)}) copy-start(bf16[1,512,3584]{2,1,0:T(8,128)(2,1)} %param.17) | copy-start | bytes 11010052
  169.0 8.3 %copy-start.2 = (bf16[1,128,3584]{2,1,0:T(8,128)(2,1)S(1)}, bf16[1,128,3584]{2,1,0:T(8,128)(2,1)}, u32[]{:S(2)}) copy-start(bf16[1,128,3584]{2,1,0:T(8,128)(2,1)} %param.9) | copy-start | bytes 2752516
  169.0 66.6 %all-to-all-start.1 = ((bf16[4,192,3584]{2,1,0:T(8,128)(2,1)}), bf16[4,192,3584]{2,1,0:T(8,128)(2,1)}, u32[]{:S(2)}, u32[]{:S(2)}) async-start(bf16[4,192,3584]{2,1,0:T(8,128)(2,1)} %bitcast.105), calls=%async_computation.1 | async-start | bytes 11010048 | tf_op jit(solution)/shard_map/forward_experts/all_to_all | solution.py:76
  177.3 0.9 copy-start.4
  235.6 5.5 copy-start
  245.9 130.7 %all-to-all-start.2 = ((bf16[4,1,2,192,3584]{4,3,2,1,0:T(8,128)(2,1)}), bf16[4,1,2,192,3584]{4,3,2,1,0:T(8,128)(2,1)}, u32[]{:S(2)}, u32[]{:S(2)}) async-start(bf16[4,1,2,192,3584]{4,3,2,1,0:T(8,128)(2,1)} %maximum_bitcast_fusion), calls=%async_computation.3 | async-start | bytes 22020096 | tf_op jit(solution)/shard_map/backward_experts/all_to_all | solution.py:76
  258.0 221.5 %reduce-scatter.3.cloned.1.call-start = ((), (), s32[]{:S(2)}) async-start(), calls=%async_computation.9 | async-start | bytes 9175040 | tf_op jit(solution)/shard_map/forward_experts/reduce_scatter | solution.py:84
  385.7 6.2 %copy-start.1 = (bf16[4,1,192,3584]{3,2,1,0:T(8,128)(2,1)S(1)}, bf16[4,1,192,3584]{3,2,1,0:T(8,128)(2,1)}, u32[]{:S(2)}) copy-start(bf16[4,1,192,3584]{3,2,1,0:T(8,128)(2,1)} %get-tuple-element.10) | copy-start | bytes 16515076
  385.7 6.5 %copy-start.6 = (bf16[1,512,3584]{2,1,0:T(8,128)(2,1)S(1)}, bf16[1,512,3584]{2,1,0:T(8,128)(2,1)}, u32[]{:S(2)}) copy-start(bf16[1,512,3584]{2,1,0:T(8,128)(2,1)} %param.17) | copy-start | bytes 11010052
  392.2 3.3 copy-start.7
  400.4 66.4 %all-to-all-start.3 = ((bf16[4,192,3584]{2,1,0:T(8,128)(2,1)}), bf16[4,192,3584]{2,1,0:T(8,128)(2,1)}, u32[]{:S(2)}, u32[]{:S(2)}) async-start(bf16[4,192,3584]{2,1,0:T(8,128)(2,1)} %bitcast.107), calls=%async_computation.4 | async-start | bytes 11010048 | tf_op jit(solution)/shard_map/backward_experts/all_to_all | solution.py:76
  408.0 157.7 %reduce-scatter.5.cloned.1.call-start = ((), (), s32[]{:S(2)}) async-start(), calls=%async_computation.10 | async-start | bytes 4587520 | tf_op jit(solution)/shard_map/backward_experts/reduce_scatter | solution.py:86
  479.4 86.3 %copy-start.3 = (bf16[1,128,3584]{2,1,0:T(8,128)(2,1)S(1)}, bf16[1,128,3584]{2,1,0:T(8,128)(2,1)}, u32[]{:S(2)}) copy-start(bf16[1,128,3584]{2,1,0:T(8,128)(2,1)} %param.13) | copy-start | bytes 2752516
  481.1 86.5 %collective-permute-start = (bf16[1,128,3584]{2,1,0:T(8,128)(2,1)S(1)}, bf16[1,128,3584]{2,1,0:T(8,128)(2,1)S(1)}, u32[]{:S(2)}, u32[]{:S(2)}) collective-permute-start(bf16[1,128,3584]{2,1,0:T(8,128)(2,1)S(1)} %convert_element_type.96), channel_id=1, source_target_pairs={{0,16},{16,32},{32,48},{48,64},{64,80},{80,96},{96,112},{112,128},... | collective-permute-start | bytes 2752520 | tf_op jit(solution)/shard_map/ppermute | solution.py:12
  567.1 15.0 %collective-permute-start.1 = (bf16[1,128,3584]{2,1,0:T(8,128)(2,1)S(1)}, bf16[1,128,3584]{2,1,0:T(8,128)(2,1)S(1)}, u32[]{:S(2)}, u32[]{:S(2)}) collective-permute-start(bf16[1,128,3584]{2,1,0:T(8,128)(2,1)S(1)} %add_convert_fusion.1), channel_id=1, source_target_pairs={{0,240},{16,0},{32,16},{48,32},{64,48},{80,64},{96,80},{112,96},{1... | collective-permute-start | bytes 2752520 | tf_op jit(solution)/shard_map/ppermute | solution.py:12
Sparse Core Ops, SparseCore 0:
  9.8 69.1 all-gather.3
  80.8 76.2 all-gather.5
  159.0 76.6 all-gather.7
  273.2 139.1 reduce-scatter.2
  479.5 86.1 reduce-scatter.4

commit v5 on v4

--- a/solution.py
+++ b/solution.py
@@ -5,6 +5,7 @@
 from jax.sharding import PartitionSpec as P
 
 Z_PARTS = 4
+D_PARTS = 2
 
 
 def from_behind(value, axis, by):
@@ -57,18 +58,25 @@
     return total.reshape(groups, tok_rows, -1)
 
 
-def forward_work(rows, w_up, w_down):
-    hidden = jax.nn.silu(jnp.dot(rows, w_up, preferred_element_type=jnp.float32)).astype(jnp.bfloat16)
+def forward_work(row_parts, w_up_parts, w_down):
+    pre_act = None
+    for rows, w_up in zip(row_parts, w_up_parts):
+        term = jnp.dot(rows, w_up, preferred_element_type=jnp.float32)
+        pre_act = term if pre_act is None else pre_act + term
+    hidden = jax.nn.silu(pre_act).astype(jnp.bfloat16)
     return jnp.dot(hidden, w_down, preferred_element_type=jnp.float32).astype(jnp.bfloat16)
 
 
-def backward_work(rows, grad_rows, w_up, w_down):
+def backward_work(rows, grad_rows, w_up, w_down, w_up_parts):
     pre_act = jnp.dot(rows, w_up, preferred_element_type=jnp.float32)
     upstream = lax.dot_general(grad_rows, w_down, (((1,), (1,)), ((), ())), preferred_element_type=jnp.float32)
     hidden_grad = (silu_slope(pre_act) * upstream).astype(jnp.bfloat16)
-    return lax.dot_general(
-        hidden_grad, w_up, (((1,), (1,)), ((), ())), preferred_element_type=jnp.float32
-    ).astype(jnp.bfloat16)
+    return [
+        lax.dot_general(hidden_grad, part, (((1,), (1,)), ((), ())), preferred_element_type=jnp.float32).astype(
+            jnp.bfloat16
+        )
+        for part in w_up_parts
+    ]
 
 
 def swap_x(rows, x_count):
@@ -116,8 +124,12 @@
     def gather_z(value):
         return lax.all_gather(value[0], "ez", axis=0, tiled=False)
 
+    features = fwd_tokens.shape[-1]
+    cuts = [(i * features // D_PARTS, (i + 1) * features // D_PARTS) for i in range(D_PARTS)]
+    w_up_parts = [w_up[lo:hi] for lo, hi in cuts]
+
     with jax.named_scope("gather_along_z"):
-        fwd_tok_z = gather_z(fwd_tokens)
+        fwd_tok_parts = [gather_z(fwd_tokens[:, :, lo:hi]) for lo, hi in cuts]
         bwd_tok_z = gather_z(bwd_tokens)
         bwd_grads_z = gather_z(bwd_grads)
         meta = jnp.concatenate(
@@ -139,17 +151,15 @@
 
     with jax.named_scope("forward_experts"):
         fwd_table = slot_table(fwd_slots, slot_total)
-        fwd_rows = swap_x(pack_rows(fwd_tok_z, fwd_table), x_count)
-        fwd_rows, bwd_tok_z = lax.optimization_barrier((fwd_rows, bwd_tok_z))
-        fwd_res = forward_work(fwd_rows, w_up, w_down)
+        fwd_row_parts = [swap_x(pack_rows(part, fwd_table), x_count) for part in fwd_tok_parts]
+        fwd_row_parts, bwd_tok_z = lax.optimization_barrier((fwd_row_parts, bwd_tok_z))
+        fwd_res = forward_work(fwd_row_parts, w_up_parts, w_down)
         fwd_back = swap_x(fwd_res, x_count)
         fwd_back, bwd_grads_z = lax.optimization_barrier((fwd_back, bwd_grads_z))
         fwd_part = weighted_partial(fwd_back, fwd_slots, fwd_weights_z, slot_total)
-        fwd_out = sum_back(fwd_tokens[0], fwd_part, z_index, jnp.float32)
 
     with jax.named_scope("backward_experts"):
         bwd_table = slot_table(bwd_slots, slot_total)
-        features = bwd_tok_z.shape[-1]
         both = jnp.stack(
             [
                 pack_rows(bwd_tok_z, bwd_table).reshape(x_count, -1, features),
@@ -157,16 +167,22 @@
             ],
             axis=1,
         )
+        fwd_part, both = lax.optimization_barrier((fwd_part, both))
         both = swap_x(both, x_count)
         bwd_rows = both[:, 0].reshape(-1, features)
         grad_rows = both[:, 1].reshape(-1, features)
-        bwd_res = backward_work(bwd_rows, grad_rows, w_up, w_down)
-        bwd_back = swap_x(bwd_res, x_count)
-        bwd_part = weighted_partial(bwd_back, bwd_slots, bwd_weights_z, slot_total)
-        bwd_out = sum_back(bwd_grads[0], bwd_part, z_index, jnp.bfloat16)
-
-    next_input = from_behind(fwd_out[None], "pp", 1)
-    prev_grad = from_behind(bwd_out[None], "pp", -1)
+        fwd_out = sum_back(fwd_tokens[0], fwd_part, z_index, jnp.float32)
+        bwd_res_parts = backward_work(bwd_rows, grad_rows, w_up, w_down, w_up_parts)
+        fwd_out, bwd_res_parts = lax.optimization_barrier((fwd_out, bwd_res_parts))
+        next_input = from_behind(fwd_out[None], "pp", 1)
+        prev_parts = []
+        for (lo, hi), bwd_res in zip(cuts, bwd_res_parts):
+            bwd_back = swap_x(bwd_res, x_count)
+            bwd_part = weighted_partial(bwd_back, bwd_slots, bwd_weights_z, slot_total)
+            bwd_out = sum_back(bwd_grads[0][:, lo:hi], bwd_part, z_index, jnp.bfloat16)
+            prev_parts.append(from_behind(bwd_out[None], "pp", -1))
+        prev_grad = jnp.concatenate(prev_parts, axis=-1)
+
     return (next_input, prev_grad)
 
 

time: 591 us -> 621 us (1.051); the launches traced: 590 us -> 613 us
  blocking collectives: 14.4 us -> 176 us
  waiting for transfers between devices: 415 us -> 270 us
  matrix products: 69.2 us -> 75.8 us
    all_to_all x0 -> x2, blocking collectives: none -> 162 us  [swap_x(): got = lax.all_to_all(spread, 'ex', split_axis=0, concat_axis=0, tiled=True)]
    all_to_all x4, waiting for transfers between devices: 162 us -> 64.8 us  [swap_x(): got = lax.all_to_all(spread, 'ex', split_axis=0, concat_axis=0, tiled=True)]
    all_gather x3 -> x4, waiting for transfers between devices: 162 us -> 136 us  [gather_z(): return lax.all_gather(value[0], 'ez', axis=0, tiled=False)]
    reduce_scatter x1 -> x2, waiting for transfers between devices: 75 us -> 52.5 us  [sum_back(): lax.psum_scatter(partial.astype(wire_type), 'ez', scatter_dimension=0, ti...]
    ppermute x2 -> x3, starting transfers between devices: 10 us -> 13.1 us  [from_behind(): lax.ppermute(value, axis, [(i, (i + by) % size) for i in range(size)])]
    dot_general x3 -> x4, matrix products: 19.3 us -> 22 us  [pack_rows(): lax.dot_general(table, flat, (((0,), (0,)), ((), ())), preferred_element_...]
    ppermute x2 -> x3, waiting for transfers between devices: 14.5 us -> 14 us  [from_behind(): lax.ppermute(value, axis, [(i, (i + by) % size) for i in range(size)])]
    dot_general x4 -> x6, matrix products: 23.7 us -> 24.2 us  [weighted_partial(): picked = jnp.dot(table, results, preferred_element_type=jnp.float32)]
  transfers between devices with their start and end apart: 11 -> 14, of which waited for: 7 -> 11; matrix products, arithmetic and copies ran while one was open for 15% -> 11% of each run, Pallas kernels for 0% -> 0%
where the time goes in v5:
time: 621 us; the launch traced here: 613 us
  waiting for transfers between devices  270 us (43%)
  blocking collectives  176 us (28%)
  matrix products  75.8 us (12%)
  starting transfers between devices  40.9 us (7%)
  other arithmetic  20.7 us (3%)
  local copies, waits for them, and re-layouts  15.1 us (2%)
  between operations  14.9 us (2%)
    all_to_all x2, blocking collectives, swap_x(): got = lax.all_to_all(spread, 'ex', split_axis=0, concat_axis=0, tiled=True)  162 us
    all_gather x4, waiting for transfers between devices, gather_z(): return lax.all_gather(value[0], 'ez', axis=0, tiled=False)  136 us
    all_to_all x4, waiting for transfers between devices, swap_x(): got = lax.all_to_all(spread, 'ex', split_axis=0, concat_axis=0, tiled=True)  64.8 us
    reduce_scatter x2, waiting for transfers between devices, sum_back(): lax.psum_scatter(partial.astype(wire_type), 'ez', scatter_dimension=0, ti...  52.5 us
    all_to_all x4, starting transfers between devices, swap_x(): got = lax.all_to_all(spread, 'ex', split_axis=0, concat_axis=0, tiled=True)  27.5 us
    dot_general x6, matrix products, weighted_partial(): picked = jnp.dot(table, results, preferred_element_type=jnp.float32)  24.2 us
    dot_general x4, matrix products, pack_rows(): lax.dot_general(table, flat, (((0,), (0,)), ((), ())), preferred_element_...  22 us
    all_gather x1, blocking collectives, gather_z(): return lax.all_gather(value[0], 'ez', axis=0, tiled=False)  14.5 us
  transfers between devices with their start and end apart: 14, of which 11 were waited for; matrix products, arithmetic and copies ran while one was open for 11% of the time, Pallas kernels for 0%

profile of v5, /device:TPU:29, one launch (start us, length us, event | category | flops | bytes accessed | tf_op | source)
XLA Modules:
  0.0 613.0 jit_solution(2881816823570746336)
XLA Ops:
  7.3 2.1 fusion.51
  9.5 0.7 all-gather.7.cloned.1.call-update
  11.0 14.5 %all_gather.15 = f32[4,128,8]{1,2,0:T(8,128)S(1)} all-gather(f32[1,128,8]{1,2,0:T(8,128)S(1)} %pad_maximum_fusion.2), channel_id=1, replica_groups=mesh['pp'=16,'ex'=4,'ez'=4] {'ez'}, dimensions={0}, use_global_device_ids=true | all-gather | bytes 20480 | tf_op jit(solution)/shard_map/gather_along_z/all_gather | solution.py:125
  25.8 2.3 reduce-window.16
  29.0 2.3 reduce-window.14
  31.7 1.2 compare_select_fusion
  33.4 24.2 %all-gather.5.cloned.1.call-done = bf16[4,128,1792]{2,1,0:T(8,128)(2,1)} async-done(((bf16[1,128,1792]{2,1,0:T(8,128)(2,1)}), bf16[4,128,1792]{2,1,0:T(8,128)(2,1)}) %all-gather.5.cloned.1.call-update) | async-done | bytes 1835024 | tf_op jit(solution)/shard_map/gather_along_z/all_gather | solution.py:125
  57.5 4.7 convolution_convert_fusion.6
  62.2 5.1 all-to-all-start
  67.3 39.5 %all-gather.7.cloned.1.call-done = bf16[4,128,1792]{2,1,0:T(8,128)(2,1)} async-done(((bf16[1,128,1792]{2,1,0:T(8,128)(2,1)}), bf16[4,128,1792]{2,1,0:T(8,128)(2,1)}) %all-gather.7.cloned.1.call-update) | async-done | bytes 1835024 | tf_op jit(solution)/shard_map/gather_along_z/all_gather | solution.py:125
  106.8 4.9 convolution_convert_fusion.5
  111.8 4.8 all-to-all-start.1
  117.1 29.7 %all-to-all-done.1 = bf16[4,192,1792]{2,1,0:T(8,128)(2,1)} async-done(((bf16[4,192,1792]{2,1,0:T(8,128)(2,1)}), bf16[4,192,1792]{2,1,0:T(8,128)(2,1)}, u32[]{:S(2)}, u32[]{:S(2)}) %all-to-all-start.1) | async-done | bytes 2752544 | tf_op jit(solution)/shard_map/forward_experts/all_to_all | solution.py:84
  146.8 28.9 %all-gather.9.cloned.1.call-done = bf16[4,128,3584]{2,1,0:T(8,128)(2,1)} async-done(((bf16[1,128,3584]{2,1,0:T(8,128)(2,1)}), bf16[4,128,3584]{2,1,0:T(8,128)(2,1)}) %all-gather.9.cloned.1.call-update) | async-done | bytes 3670032 | tf_op jit(solution)/shard_map/gather_along_z/all_gather | solution.py:125
  175.7 5.1 fusion.8
  180.8 10.1 %convolution_convert_fusion.2 = bf16[768,3584]{1,0:T(8,128)(2,1)} fusion(bf16[1,512,3584]{2,1,0:T(8,128)(2,1)} %param.17, f32[768,512]{1,0:T(8,128)} %fusion.8, bf16[768,1792]{1,0:T(8,128)(2,1)S(1)} %bitcast.148, bf16[1,3584,512]{2,1,0:T(8,128)(2,1)} %param.16), kind=kOutput, calls=%fused_computation.5 | convolution fusion | flops 4232970240 | bytes 15335424 | tf_op jit(solution)/shard_map/forward_experts/dot_general | solution.py:67
  190.9 10.5 %all-to-all-start.2 = ((bf16[4,192,3584]{2,1,0:T(8,128)(2,1)}), bf16[4,192,3584]{2,1,0:T(8,128)(2,1)}, u32[]{:S(2)}, u32[]{:S(2)}) async-start(bf16[4,192,3584]{2,1,0:T(8,128)(2,1)} %bitcast.139), calls=%async_computation.2 | async-start | bytes 11010048 | tf_op jit(solution)/shard_map/forward_experts/all_to_all | solution.py:84
  203.2 6.9 %convolution_convert_fusion.1 = bf16[768,3584]{1,0:T(8,128)(2,1)} fusion(bf16[512,768]{1,0:T(8,128)(2,1)S(1)} %fusion.17, bf16[512,3584]{1,0:T(8,128)(2,1)} %bitcast.179), kind=kOutput, calls=%fused_computation.4 | convolution fusion | flops 2821324800 | bytes 9961472 | tf_op jit(solution)/shard_map/backward_experts/dot_general | solution.py:44
  210.1 43.8 %all-gather.11.cloned.1.call-done = bf16[4,128,3584]{2,1,0:T(8,128)(2,1)} async-done(((bf16[1,128,3584]{2,1,0:T(8,128)(2,1)}), bf16[4,128,3584]{2,1,0:T(8,128)(2,1)}) %all-gather.11.cloned.1.call-update) | async-done | bytes 3670032 | tf_op jit(solution)/shard_map/gather_along_z/all_gather | solution.py:125
  253.9 7.1 %all-to-all-done.2 = bf16[4,192,3584]{2,1,0:T(8,128)(2,1)} async-done(((bf16[4,192,3584]{2,1,0:T(8,128)(2,1)}), bf16[4,192,3584]{2,1,0:T(8,128)(2,1)}, u32[]{:S(2)}, u32[]{:S(2)}) %all-to-all-start.2) | async-done | bytes 5505056 | tf_op jit(solution)/shard_map/forward_experts/all_to_all | solution.py:84
  261.0 5.5 convolution_convert_fusion
  266.5 4.9 pad_maximum_fusion
  271.4 5.2 fusion.21
  276.6 5.9 multiply_add_fusion
  282.5 4.0 select_add_fusion
  286.4 128.9 %all_to_all.30 = bf16[4,1,2,192,3584]{4,3,2,1,0:T(8,128)(2,1)} all-to-all(bf16[4,1,2,192,3584]{4,3,2,1,0:T(8,128)(2,1)} %bitcast.136), channel_id=1, replica_groups=mesh['pp'=16,'ex'=4,'ez'=4] {'ex'}, dimensions={0} | all-to-all | bytes 22020096 | tf_op jit(solution)/shard_map/backward_experts/all_to_all | solution.py:84
  415.3 9.2 %fusion.50 = (bf16[4,1,192,3584]{3,2,1,0:T(8,128)(2,1)}, bf16[4,1,192,3584]{3,2,1,0:T(8,128)(2,1)}) fusion(bf16[4,2,192,3584]{3,2,1,0:T(8,128)(2,1)} %bitcast.137), kind=kLoop, calls=%fused_computation.91 | loop fusion | bytes 22020096 | tf_op jit(solution)/shard_map/backward_experts/slice | solution.py:173
  424.5 6.4 %fusion = f32[768,512]{1,0:T(8,128)S(1)} fusion(bf16[768,3584]{1,0:T(8,128)(2,1)} %bitcast.145, bf16[1,3584,512]{2,1,0:T(8,128)(2,1)} %param.16), kind=kOutput, calls=%fused_computation.6 | convolution fusion | flops 2818572288 | bytes 10747904 | tf_op jit(solution)/shard_map/backward_experts/dot_general | solution.py:71
  431.0 3.3 multiply_convert_fusion
  434.4 3.2 convolution_convert_fusion.3
  437.5 1.6 convolution_convert_fusion.4
  439.2 2.5 convert_bitcast_fusion
  441.7 7.1 %all-to-all-start.5 = ((bf16[4,192,1792]{2,1,0:T(8,128)(2,1)}), bf16[4,192,1792]{2,1,0:T(8,128)(2,1)}, u32[]{:S(2)}, u32[]{:S(2)}) async-start(bf16[4,192,1792]{2,1,0:T(8,128)(2,1)} %bitcast.149), calls=%async_computation.7 | async-start | bytes 5505024 | tf_op jit(solution)/shard_map/backward_experts/all_to_all | solution.py:84
  449.1 28.0 %all-to-all-done.5 = bf16[4,192,1792]{2,1,0:T(8,128)(2,1)} async-done(((bf16[4,192,1792]{2,1,0:T(8,128)(2,1)}), bf16[4,192,1792]{2,1,0:T(8,128)(2,1)}, u32[]{:S(2)}, u32[]{:S(2)}) %all-to-all-start.5) | async-done | bytes 2752544 | tf_op jit(solution)/shard_map/backward_experts/all_to_all | solution.py:84
  477.0 3.5 fusion.19
  480.5 4.9 add_convert_fusion
  485.5 32.6 %all_to_all.31 = bf16[4,192,1792]{2,1,0:T(8,128)(2,1)S(1)} all-to-all(bf16[4,192,1792]{2,1,0:T(8,128)(2,1)S(1)} %bitcast.147), channel_id=1, replica_groups=mesh['pp'=16,'ex'=4,'ez'=4] {'ex'}, dimensions={0} | all-to-all | bytes 5505024 | tf_op jit(solution)/shard_map/backward_experts/all_to_all | solution.py:84
  518.1 1.7 fusion.20
  519.8 3.1 add_convert_fusion.1
  523.0 12.0 %collective-permute-start = (bf16[1,128,3584]{2,1,0:T(8,128)(2,1)S(1)}, bf16[1,128,3584]{2,1,0:T(8,128)(2,1)S(1)}, u32[]{:S(2)}, u32[]{:S(2)}) collective-permute-start(bf16[1,128,3584]{2,1,0:T(8,128)(2,1)S(1)} %bitcast.160), channel_id=1, source_target_pairs={{0,16},{16,32},{32,48},{48,64},{64,80},{80,96},{96,112},{112,128},... | collective-permute-start | bytes 2752520 | tf_op jit(solution)/shard_map/backward_experts/ppermute | solution.py:13
  535.0 5.8 reduce-scatter.8.cloned.1.call-done
  540.8 46.7 %reduce-scatter.6.cloned.1.call-done = bf16[1,128,1792]{2,1,0:T(8,128)(2,1)} async-done(((bf16[4,128,1792]{2,1,0:T(8,128)(2,1)}), bf16[1,128,1792]{2,1,0:T(8,128)(2,1)}) %reduce-scatter.6.cloned.1.call-update) | async-done | bytes 458768 | tf_op jit(solution)/shard_map/backward_experts/reduce_scatter | solution.py:94
  587.5 1.4 fusion.37
  588.8 0.7 collective-permute-start.1
  589.9 9.1 %collective-permute-done.1 = bf16[1,128,1792]{2,1,0:T(8,128)(2,1)S(1)} collective-permute-done((bf16[1,128,1792]{2,1,0:T(8,128)(2,1)S(1)}, bf16[1,128,1792]{2,1,0:T(8,128)(2,1)S(1)}, u32[]{:S(2)}, u32[]{:S(2)}) %collective-permute-start.1) | collective-permute-done | bytes 458784 | tf_op jit(solution)/shard_map/backward_experts/ppermute | solution.py:13
  598.9 4.9 collective-permute-done.2
  603.8 1.0 pad_maximum_fusion.1
  604.8 0.9 copy.104
  (89 shorter events, 6.1 us)
Async XLA Ops:
  7.2 3.7 copy-start.6
  7.2 3.8 copy-start.7
  7.2 3.8 copy-start.8
  7.2 3.8 copy-start.9
  7.2 50.3 %all-gather.5.cloned.1.call-start = ((), (), s32[]{:S(2)}) async-start(), calls=%async_computation.9 | async-start | bytes 2293760 | tf_op jit(solution)/shard_map/gather_along_z/all_gather | solution.py:125
  9.4 97.4 %all-gather.7.cloned.1.call-start = ((), (), s32[]{:S(2)}) async-start(), calls=%async_computation.10 | async-start | bytes 2293760 | tf_op jit(solution)/shard_map/gather_along_z/all_gather | solution.py:125
  10.2 165.5 %all-gather.9.cloned.1.call-start = ((), (), s32[]{:S(2)}) async-start(), calls=%async_computation.11 | async-start | bytes 4587520 | tf_op jit(solution)/shard_map/gather_along_z/all_gather | solution.py:125
  33.4 28.9 %copy-start.5 = (bf16[512,768]{1,0:T(8,128)(2,1)}, bf16[512,768]{1,0:T(8,128)(2,1)S(1)}, u32[]{:S(2)}) copy-start(bf16[512,768]{1,0:T(8,128)(2,1)S(1)} %fusion.18) | copy-start | bytes 2359300
  62.2 49.5 %all-to-all-start = ((bf16[4,192,1792]{2,1,0:T(8,128)(2,1)}), bf16[4,192,1792]{2,1,0:T(8,128)(2,1)S(1)}, u32[]{:S(2)}, u32[]{:S(2)}) async-start(bf16[4,192,1792]{2,1,0:T(8,128)(2,1)} %bitcast.151), calls=%async_computation | async-start | bytes 5505024 | tf_op jit(solution)/shard_map/forward_experts/all_to_all | solution.py:84
  111.8 35.0 %all-to-all-start.1 = ((bf16[4,192,1792]{2,1,0:T(8,128)(2,1)}), bf16[4,192,1792]{2,1,0:T(8,128)(2,1)}, u32[]{:S(2)}, u32[]{:S(2)}) async-start(bf16[4,192,1792]{2,1,0:T(8,128)(2,1)} %bitcast.150), calls=%async_computation.1 | async-start | bytes 5505024 | tf_op jit(solution)/shard_map/forward_experts/all_to_all | solution.py:84
  116.5 137.4 %all-gather.11.cloned.1.call-start = ((), (), s32[]{:S(2)}) async-start(), calls=%async_computation.12 | async-start | bytes 4587520 | tf_op jit(solution)/shard_map/gather_along_z/all_gather | solution.py:125
  190.9 11.5 %copy-start.1 = (bf16[1,128,3584]{2,1,0:T(8,128)(2,1)S(1)}, bf16[1,128,3584]{2,1,0:T(8,128)(2,1)}, u32[]{:S(2)}) copy-start(bf16[1,128,3584]{2,1,0:T(8,128)(2,1)} %param.9) | copy-start | bytes 2752516
  190.9 70.2 %all-to-all-start.2 = ((bf16[4,192,3584]{2,1,0:T(8,128)(2,1)}), bf16[4,192,3584]{2,1,0:T(8,128)(2,1)}, u32[]{:S(2)}, u32[]{:S(2)}) async-start(bf16[4,192,3584]{2,1,0:T(8,128)(2,1)} %bitcast.139), calls=%async_computation.2 | async-start | bytes 11010048 | tf_op jit(solution)/shard_map/forward_experts/all_to_all | solution.py:84
  201.4 237.8 %reduce-scatter.4.cloned.1.call-start = ((), (), s32[]{:S(2)}) async-start(), calls=%async_computation.13 | async-start | bytes 9175040 | tf_op jit(solution)/shard_map/backward_experts/reduce_scatter | solution.py:92
  202.3 0.9 copy-start.4
  261.0 5.5 slice-start
  261.0 5.5 slice-start.1
  424.5 6.4 %copy-start = (bf16[4,1,192,3584]{3,2,1,0:T(8,128)(2,1)S(1)}, bf16[4,1,192,3584]{3,2,1,0:T(8,128)(2,1)}, u32[]{:S(2)}) copy-start(bf16[4,1,192,3584]{3,2,1,0:T(8,128)(2,1)} %get-tuple-element.22) | copy-start | bytes 16515076
  424.5 6.5 %copy-start.10 = (bf16[1,512,3584]{2,1,0:T(8,128)(2,1)S(1)}, bf16[1,512,3584]{2,1,0:T(8,128)(2,1)}, u32[]{:S(2)}) copy-start(bf16[1,512,3584]{2,1,0:T(8,128)(2,1)} %param.17) | copy-start | bytes 11010052
  431.0 3.3 copy-start.11
  441.7 35.3 %all-to-all-start.5 = ((bf16[4,192,1792]{2,1,0:T(8,128)(2,1)}), bf16[4,192,1792]{2,1,0:T(8,128)(2,1)}, u32[]{:S(2)}, u32[]{:S(2)}) async-start(bf16[4,192,1792]{2,1,0:T(8,128)(2,1)} %bitcast.149), calls=%async_computation.7 | async-start | bytes 5505024 | tf_op jit(solution)/shard_map/backward_experts/all_to_all | solution.py:84
  448.8 91.9 %reduce-scatter.8.cloned.1.call-start = ((), (), s32[]{:S(2)}) async-start(), calls=%async_computation.15 | async-start | bytes 2293760 | tf_op jit(solution)/shard_map/backward_experts/reduce_scatter | solution.py:94
  485.4 102.0 %reduce-scatter.6.cloned.1.call-start = ((), (), s32[]{:S(2)}) async-start(), calls=%async_computation.14 | async-start | bytes 2293760 | tf_op jit(solution)/shard_map/backward_experts/reduce_scatter | solution.py:94
  519.8 3.2 copy-start.3
  519.8 67.7 %copy-start.2 = (bf16[1,128,3584]{2,1,0:T(8,128)(2,1)S(1)}, bf16[1,128,3584]{2,1,0:T(8,128)(2,1)}, u32[]{:S(2)}) copy-start(bf16[1,128,3584]{2,1,0:T(8,128)(2,1)} %param.13) | copy-start | bytes 2752516
  523.0 66.9 %collective-permute-start = (bf16[1,128,3584]{2,1,0:T(8,128)(2,1)S(1)}, bf16[1,128,3584]{2,1,0:T(8,128)(2,1)S(1)}, u32[]{:S(2)}, u32[]{:S(2)}) collective-permute-start(bf16[1,128,3584]{2,1,0:T(8,128)(2,1)S(1)} %bitcast.160), channel_id=1, source_target_pairs={{0,16},{16,32},{32,48},{48,64},{64,80},{80,96},{96,112},{112,128},... | collective-permute-start | bytes 2752520 | tf_op jit(solution)/shard_map/backward_experts/ppermute | solution.py:13
  588.8 10.1 %collective-permute-start.1 = (bf16[1,128,1792]{2,1,0:T(8,128)(2,1)S(1)}, bf16[1,128,1792]{2,1,0:T(8,128)(2,1)S(1)}, u32[]{:S(2)}, u32[]{:S(2)}) collective-permute-start(bf16[1,128,1792]{2,1,0:T(8,128)(2,1)S(1)} %get-tuple-element.24), channel_id=1, source_target_pairs={{0,240},{16,0},{32,16},{48,32},{64,48},{80,64},{96,80},{112,96},{1... | collective-permute-start | bytes 1376264 | tf_op jit(solution)/shard_map/backward_experts/ppermute | solution.py:13
  589.5 14.3 %collective-permute-start.2 = (bf16[1,128,1792]{2,1,0:T(8,128)(2,1)S(1)}, bf16[1,128,1792]{2,1,0:T(8,128)(2,1)S(1)}, u32[]{:S(2)}, u32[]{:S(2)}) collective-permute-start(bf16[1,128,1792]{2,1,0:T(8,128)(2,1)S(1)} %get-tuple-element.25), channel_id=1, source_target_pairs={{0,240},{16,0},{32,16},{48,32},{64,48},{80,64},{96,80},{112,96},{1... | collective-permute-start | bytes 1376264 | tf_op jit(solution)/shard_map/backward_experts/ppermute | solution.py:13
Sparse Core Ops, SparseCore 0:
  9.8 47.6 all-gather.4
  59.9 46.8 all-gather.6
  108.6 67.0 all-gather.8
  177.4 76.4 all-gather.10
  286.6 140.0 reduce-scatter.3
  485.5 55.1 reduce-scatter.7
  543.3 44.1 reduce-scatter.5

commit v6 on v4

--- a/solution.py
+++ b/solution.py
@@ -5,6 +5,7 @@
 from jax.sharding import PartitionSpec as P
 
 Z_PARTS = 4
+D_PARTS = 2
 
 
 def from_behind(value, axis, by):
@@ -57,9 +58,9 @@
     return total.reshape(groups, tok_rows, -1)
 
 
-def forward_work(rows, w_up, w_down):
+def forward_work(rows, w_up, w_down_parts):
     hidden = jax.nn.silu(jnp.dot(rows, w_up, preferred_element_type=jnp.float32)).astype(jnp.bfloat16)
-    return jnp.dot(hidden, w_down, preferred_element_type=jnp.float32).astype(jnp.bfloat16)
+    return [jnp.dot(hidden, part, preferred_element_type=jnp.float32).astype(jnp.bfloat16) for part in w_down_parts]
 
 
 def backward_work(rows, grad_rows, w_up, w_down):
@@ -116,10 +117,14 @@
     def gather_z(value):
         return lax.all_gather(value[0], "ez", axis=0, tiled=False)
 
+    features = fwd_tokens.shape[-1]
+    cuts = [(i * features // D_PARTS, (i + 1) * features // D_PARTS) for i in range(D_PARTS)]
+
     with jax.named_scope("gather_along_z"):
-        fwd_tok_z = gather_z(fwd_tokens)
         bwd_tok_z = gather_z(bwd_tokens)
         bwd_grads_z = gather_z(bwd_grads)
+        fwd_tokens_in, bwd_grads_z = lax.optimization_barrier((fwd_tokens, bwd_grads_z))
+        fwd_tok_z = gather_z(fwd_tokens_in)
         meta = jnp.concatenate(
             [fwd_routes.astype(jnp.float32), fwd_weights, bwd_routes.astype(jnp.float32), bwd_weights], axis=-1
         )
@@ -137,36 +142,34 @@
             bwd_routes_z, slot_positions(bwd_routes_z, expert_count), expert_class, class_count, capacity
         )
 
+    with jax.named_scope("backward_experts"):
+        bwd_table = slot_table(bwd_slots, slot_total)
+        bwd_rows = swap_x(pack_rows(bwd_tok_z, bwd_table), x_count)
+        grad_rows = swap_x(pack_rows(bwd_grads_z, bwd_table), x_count)
+        bwd_res = backward_work(bwd_rows, grad_rows, w_up, w_down)
+
     with jax.named_scope("forward_experts"):
         fwd_table = slot_table(fwd_slots, slot_total)
         fwd_rows = swap_x(pack_rows(fwd_tok_z, fwd_table), x_count)
-        fwd_rows, bwd_tok_z = lax.optimization_barrier((fwd_rows, bwd_tok_z))
-        fwd_res = forward_work(fwd_rows, w_up, w_down)
-        fwd_back = swap_x(fwd_res, x_count)
-        fwd_back, bwd_grads_z = lax.optimization_barrier((fwd_back, bwd_grads_z))
-        fwd_part = weighted_partial(fwd_back, fwd_slots, fwd_weights_z, slot_total)
-        fwd_out = sum_back(fwd_tokens[0], fwd_part, z_index, jnp.float32)
+        fwd_rows, bwd_res = lax.optimization_barrier((fwd_rows, bwd_res))
 
     with jax.named_scope("backward_experts"):
-        bwd_table = slot_table(bwd_slots, slot_total)
-        features = bwd_tok_z.shape[-1]
-        both = jnp.stack(
-            [
-                pack_rows(bwd_tok_z, bwd_table).reshape(x_count, -1, features),
-                pack_rows(bwd_grads_z, bwd_table).reshape(x_count, -1, features),
-            ],
-            axis=1,
-        )
-        both = swap_x(both, x_count)
-        bwd_rows = both[:, 0].reshape(-1, features)
-        grad_rows = both[:, 1].reshape(-1, features)
-        bwd_res = backward_work(bwd_rows, grad_rows, w_up, w_down)
         bwd_back = swap_x(bwd_res, x_count)
         bwd_part = weighted_partial(bwd_back, bwd_slots, bwd_weights_z, slot_total)
         bwd_out = sum_back(bwd_grads[0], bwd_part, z_index, jnp.bfloat16)
+        prev_grad = from_behind(bwd_out[None], "pp", -1)
 
-    next_input = from_behind(fwd_out[None], "pp", 1)
-    prev_grad = from_behind(bwd_out[None], "pp", -1)
+    with jax.named_scope("forward_experts"):
+        w_down_parts = [w_down[:, lo:hi] for lo, hi in cuts]
+        fwd_res_parts = forward_work(fwd_rows, w_up, w_down_parts)
+        next_parts = []
+        for (lo, hi), fwd_res in zip(cuts, fwd_res_parts):
+            fwd_back = swap_x(fwd_res, x_count)
+            fwd_part = weighted_partial(fwd_back, fwd_slots, fwd_weights_z, slot_total)
+            fwd_out = sum_back(fwd_tokens[0][:, lo:hi], fwd_part, z_index, jnp.bfloat16)
+            next_parts.append(from_behind(fwd_out[None], "pp", 1))
+        next_input = jnp.concatenate(next_parts, axis=-1)
+
     return (next_input, prev_grad)
 
 

time: 591 us -> 587 us (level)
  starting transfers between devices: 42.6 us -> 54.2 us
  matrix products: 69.2 us -> 79.2 us
  local copies, waits for them, and re-layouts: 13.9 us -> 4.61 us
  waiting for transfers between devices: 415 us -> 406 us
  other arithmetic: 20.9 us -> 12.6 us
    all_to_all x4 -> x6, waiting for transfers between devices: 162 us -> 138 us  [swap_x(): got = lax.all_to_all(spread, 'ex', split_axis=0, concat_axis=0, tiled=True)]
    all_gather x3, waiting for transfers between devices: 162 us -> 178 us  [gather_z(): return lax.all_gather(value[0], 'ez', axis=0, tiled=False)]
    all_to_all x4 -> x6, starting transfers between devices: 32.4 us -> 41.7 us  [swap_x(): got = lax.all_to_all(spread, 'ex', split_axis=0, concat_axis=0, tiled=True)]
    slice x3 -> x2, local copies, waits for them, and re-layouts: 9.27 us -> 0.19 us  [the longest x1 9.08 us: on_device(): grad_rows = both[:, 1].reshape(-1, features)]
    dot_general x1, matrix products: 4.86 us -> 13.3 us  [backward_work(): lax.dot_general(hidden_grad, w_up, (((1,), (1,)), ((), ())), preferred_el...]
    ppermute x2 -> x3, starting transfers between devices: 10 us -> 12.4 us  [from_behind(): lax.ppermute(value, axis, [(i, (i + by) % size) for i in range(size)])]
    ppermute x2 -> x3, waiting for transfers between devices: 14.5 us -> 13.4 us  [from_behind(): lax.ppermute(value, axis, [(i, (i + by) % size) for i in range(size)])]
    reduce_scatter x1 -> x3, waiting for transfers between devices: 75 us -> 75.6 us  [sum_back(): lax.psum_scatter(partial.astype(wire_type), 'ez', scatter_dimension=0, ti...]
  transfers between devices with their start and end apart: 11 -> 15, of which waited for: 7 -> 10; matrix products, arithmetic and copies ran while one was open for 15% -> 14% of each run, Pallas kernels for 0% -> 0%
where the time goes in v6:
time: 587 us; the launch traced here: 585 us
  waiting for transfers between devices  406 us (69%)
  matrix products  79.2 us (13%)
  starting transfers between devices  54.2 us (9%)
  blocking collectives  14.4 us (2%)
  between operations  14.3 us (2%)
  other arithmetic  12.6 us (2%)
    all_gather x3, waiting for transfers between devices, gather_z(): return lax.all_gather(value[0], 'ez', axis=0, tiled=False)  178 us
    all_to_all x6, waiting for transfers between devices, swap_x(): got = lax.all_to_all(spread, 'ex', split_axis=0, concat_axis=0, tiled=True)  138 us
    reduce_scatter x3, waiting for transfers between devices, sum_back(): lax.psum_scatter(partial.astype(wire_type), 'ez', scatter_dimension=0, ti...  75.6 us
    all_to_all x6, starting transfers between devices, swap_x(): got = lax.all_to_all(spread, 'ex', split_axis=0, concat_axis=0, tiled=True)  41.7 us
    dot_general x6, matrix products, weighted_partial(): picked = jnp.dot(table, results, preferred_element_type=jnp.float32)  24.2 us
    dot_general x3, matrix products, pack_rows(): lax.dot_general(table, flat, (((0,), (0,)), ((), ())), preferred_element_...  20.6 us
    all_gather x1, blocking collectives, gather_z(): return lax.all_gather(value[0], 'ez', axis=0, tiled=False)  14.4 us
    ppermute x3, waiting for transfers between devices, from_behind(): lax.ppermute(value, axis, [(i, (i + by) % size) for i in range(size)])  13.4 us
  transfers between devices with their start and end apart: 15, of which 10 were waited for; matrix products, arithmetic and copies ran while one was open for 14% of the time, Pallas kernels for 0%

profile of v6, /device:TPU:29, one launch (start us, length us, event | category | flops | bytes accessed | tf_op | source)
XLA Modules:
  0.0 585.5 jit_solution(18081054919414381138)
XLA Ops:
  7.2 0.7 all-gather.8.cloned.1.call-update
  7.9 0.7 all-gather.4.cloned.1.call-update
  8.7 0.7 convert_element_type.124
  9.3 0.7 convert_element_type.123
  10.0 0.7 pad_maximum_fusion.1
  10.7 14.4 %all_gather.12 = f32[4,128,8]{1,2,0:T(8,128)S(1)} all-gather(f32[1,128,8]{1,2,0:T(8,128)S(1)} %pad_maximum_fusion.1), channel_id=1, replica_groups=mesh['pp'=16,'ex'=4,'ez'=4] {'ez'}, dimensions={0}, use_global_device_ids=true | all-gather | bytes 20480 | tf_op jit(solution)/shard_map/gather_along_z/all_gather | solution.py:118
  25.5 2.3 reduce-window.16
  28.6 2.3 reduce-window.14
  31.5 1.2 compare_select_fusion
  32.7 0.4 fusion.9
  33.1 45.9 %all-gather.8.cloned.1.call-done = bf16[4,128,3584]{2,1,0:T(8,128)(2,1)} async-done(((bf16[1,128,3584]{2,1,0:T(8,128)(2,1)}), bf16[4,128,3584]{2,1,0:T(8,128)(2,1)}) %all-gather.8.cloned.1.call-update) | async-done | bytes 3670032 | tf_op jit(solution)/shard_map/gather_along_z/all_gather | solution.py:118
  79.0 6.9 %convolution_convert_fusion.2 = bf16[768,3584]{1,0:T(8,128)(2,1)} fusion(bf16[512,768]{1,0:T(8,128)(2,1)S(1)} %fusion.9, bf16[512,3584]{1,0:T(8,128)(2,1)} %bitcast.146), kind=kOutput, calls=%fused_computation.3 | convolution fusion | flops 2821324800 | bytes 9961472 | tf_op jit(solution)/shard_map/backward_experts/dot_general | solution.py:44
  85.9 5.1 all-to-all-start.1
  91.1 67.2 %all-gather.4.cloned.1.call-done = bf16[4,128,3584]{2,1,0:T(8,128)(2,1)} async-done(((bf16[1,128,3584]{2,1,0:T(8,128)(2,1)}), bf16[4,128,3584]{2,1,0:T(8,128)(2,1)}) %all-gather.4.cloned.1.call-update) | async-done | bytes 3670032 | tf_op jit(solution)/shard_map/gather_along_z/all_gather | solution.py:118
  158.3 6.9 %convolution_convert_fusion.1 = bf16[768,3584]{1,0:T(8,128)(2,1)} fusion(bf16[512,768]{1,0:T(8,128)(2,1)S(1)} %fusion.9, bf16[512,3584]{1,0:T(8,128)(2,1)} %bitcast.145), kind=kOutput, calls=%fused_computation.2 | convolution fusion | flops 2821324800 | bytes 9961472 | tf_op jit(solution)/shard_map/backward_experts/dot_general | solution.py:44
  165.2 6.2 %all-to-all-start.2 = ((bf16[4,192,3584]{2,1,0:T(8,128)(2,1)}), bf16[4,192,3584]{2,1,0:T(8,128)(2,1)}, u32[]{:S(2)}, u32[]{:S(2)}) async-start(bf16[4,192,3584]{2,1,0:T(8,128)(2,1)} %bitcast.108), calls=%async_computation.2 | async-start | bytes 11010048 | tf_op jit(solution)/shard_map/backward_experts/all_to_all | solution.py:77
  171.5 0.4 fusion.10
  171.9 64.7 %all-gather.6.cloned.1.call-done = bf16[4,128,3584]{2,1,0:T(8,128)(2,1)} async-done(((bf16[1,128,3584]{2,1,0:T(8,128)(2,1)}), bf16[4,128,3584]{2,1,0:T(8,128)(2,1)}) %all-gather.6.cloned.1.call-update) | async-done | bytes 3670032 | tf_op jit(solution)/shard_map/gather_along_z/all_gather | solution.py:118
  236.6 6.8 %convolution_convert_fusion.3 = bf16[768,3584]{1,0:T(8,128)(2,1)} fusion(bf16[512,768]{1,0:T(8,128)(2,1)S(1)} %fusion.10, bf16[512,3584]{1,0:T(8,128)(2,1)} %bitcast.147), kind=kOutput, calls=%fused_computation.4 | convolution fusion | flops 2821324800 | bytes 9961472 | tf_op jit(solution)/shard_map/forward_experts/dot_general | solution.py:44
  243.5 10.3 %all-to-all-start = ((bf16[4,192,3584]{2,1,0:T(8,128)(2,1)}), bf16[4,192,3584]{2,1,0:T(8,128)(2,1)}, u32[]{:S(2)}, u32[]{:S(2)}) async-start(bf16[4,192,3584]{2,1,0:T(8,128)(2,1)} %bitcast.110), calls=%async_computation | async-start | bytes 11010048 | tf_op jit(solution)/shard_map/forward_experts/all_to_all | solution.py:77
  253.7 6.1 %fusion.3 = f32[768,512]{1,0:T(8,128)S(1)} fusion(bf16[768,3584]{1,0:T(8,128)(2,1)} %bitcast.20, bf16[1,3584,512]{2,1,0:T(8,128)(2,1)} %param.16), kind=kOutput, calls=%fused_computation.8 | convolution fusion | flops 2818572288 | bytes 10747904 | tf_op jit(solution)/shard_map/backward_experts/dot_general | solution.py:67
  259.8 13.3 %convolution_convert_fusion = bf16[768,3584]{1,0:T(8,128)(2,1)} fusion(bf16[1,3584,512]{2,1,0:T(8,128)(2,1)} %param.16, f32[768,512]{1,0:T(8,128)S(1)} %fusion.3, bf16[768,3584]{1,0:T(8,128)(2,1)} %bitcast.24, bf16[1,512,3584]{2,1,0:T(8,128)(2,1)} %param.17), kind=kOutput, calls=%fused_computation.1 | convolution fusion | flops 5643436032 | bytes 19922944 | tf_op jit(solution)/shard_map/backward_experts/dot_general | solution.py:70
  273.0 40.5 %all-to-all-done = bf16[4,192,3584]{2,1,0:T(8,128)(2,1)} async-done(((bf16[4,192,3584]{2,1,0:T(8,128)(2,1)}), bf16[4,192,3584]{2,1,0:T(8,128)(2,1)}, u32[]{:S(2)}, u32[]{:S(2)}) %all-to-all-start) | async-done | bytes 5505056 | tf_op jit(solution)/shard_map/forward_experts/all_to_all | solution.py:77
  313.5 7.0 %multiply_convert_fusion = bf16[768,512]{1,0:T(8,128)(2,1)S(1)} fusion(bf16[768,3584]{1,0:T(8,128)(2,1)} %bitcast.11, bf16[1,3584,512]{2,1,0:T(8,128)(2,1)} %param.16), kind=kOutput, calls=%fused_computation.26 | convolution fusion | flops 2820538368 | bytes 9961472 | tf_op jit(solution)/shard_map/forward_experts/dot_general | solution.py:62
  320.6 3.2 convolution_convert_fusion.5
  323.8 6.1 %all-to-all-start.3 = ((bf16[4,192,1792]{2,1,0:T(8,128)(2,1)}), bf16[4,192,1792]{2,1,0:T(8,128)(2,1)S(1)}, u32[]{:S(2)}, u32[]{:S(2)}) async-start(bf16[4,192,1792]{2,1,0:T(8,128)(2,1)} %bitcast.118), calls=%async_computation.3 | async-start | bytes 5505024 | tf_op jit(solution)/shard_map/forward_experts/all_to_all | solution.py:77
  330.1 4.9 convolution_convert_fusion.4
  335.0 23.9 %all-to-all-done.3 = bf16[4,192,1792]{2,1,0:T(8,128)(2,1)S(1)} async-done(((bf16[4,192,1792]{2,1,0:T(8,128)(2,1)}), bf16[4,192,1792]{2,1,0:T(8,128)(2,1)S(1)}, u32[]{:S(2)}, u32[]{:S(2)}) %all-to-all-start.3) | async-done | bytes 2752544 | tf_op jit(solution)/shard_map/forward_experts/all_to_all | solution.py:77
  358.9 1.6 copy-done.2
  360.5 6.3 %all-to-all-start.4 = ((bf16[4,192,1792]{2,1,0:T(8,128)(2,1)}), bf16[4,192,1792]{2,1,0:T(8,128)(2,1)S(1)}, u32[]{:S(2)}, u32[]{:S(2)}) async-start(bf16[4,192,1792]{2,1,0:T(8,128)(2,1)} %bitcast.117), calls=%async_computation.5 | async-start | bytes 5505024 | tf_op jit(solution)/shard_map/forward_experts/all_to_all | solution.py:77
  366.8 3.6 fusion.12
  370.4 3.2 add_convert_fusion.2
  373.6 21.3 %all-to-all-done.4 = bf16[4,192,1792]{2,1,0:T(8,128)(2,1)S(1)} async-done(((bf16[4,192,1792]{2,1,0:T(8,128)(2,1)}), bf16[4,192,1792]{2,1,0:T(8,128)(2,1)S(1)}, u32[]{:S(2)}, u32[]{:S(2)}) %all-to-all-start.4) | async-done | bytes 2752544 | tf_op jit(solution)/shard_map/forward_experts/all_to_all | solution.py:77
  395.0 7.8 %all-to-all-start.5 = ((bf16[4,192,3584]{2,1,0:T(8,128)(2,1)}), bf16[4,192,3584]{2,1,0:T(8,128)(2,1)}, u32[]{:S(2)}, u32[]{:S(2)}) async-start(bf16[4,192,3584]{2,1,0:T(8,128)(2,1)} %bitcast.107), calls=%async_computation.7 | async-start | bytes 11010048 | tf_op jit(solution)/shard_map/backward_experts/all_to_all | solution.py:77
  402.8 1.7 fusion.11
  404.5 3.1 add_convert_fusion.1
  407.9 51.9 %all-to-all-done.5 = bf16[4,192,3584]{2,1,0:T(8,128)(2,1)} async-done(((bf16[4,192,3584]{2,1,0:T(8,128)(2,1)}), bf16[4,192,3584]{2,1,0:T(8,128)(2,1)}, u32[]{:S(2)}, u32[]{:S(2)}) %all-to-all-start.5) | async-done | bytes 5505056 | tf_op jit(solution)/shard_map/backward_experts/all_to_all | solution.py:77
  459.7 5.2 fusion.13
  465.0 7.4 %add_convert_fusion = bf16[512,3584]{1,0:T(8,128)(2,1)} fusion(f32[512,3584]{1,0:T(8,128)S(1)} %fusion.13, bf16[768,3584]{1,0:T(8,128)(2,1)} %bitcast.41, f32[512]{0:T(512)S(1)} %bitcast.138, f32[512]{0:T(512)S(1)} %bitcast.137, s32[512]{0:T(512)S(1)} %bitcast.135), kind=kOutput, calls=%fused_computation | convolution fusion | flops 2826305536 | bytes 16521216 | tf_op jit(solution)/shard_map/backward_experts/dot_general | solution.py:55
  472.4 1.0 reduce-scatter.6.cloned.1.call-done
  473.6 1.4 fusion.24
  474.9 11.7 %collective-permute-start.1 = (bf16[1,128,1792]{2,1,0:T(8,128)(2,1)S(1)}, bf16[1,128,1792]{2,1,0:T(8,128)(2,1)S(1)}, u32[]{:S(2)}, u32[]{:S(2)}) collective-permute-start(bf16[1,128,1792]{2,1,0:T(8,128)(2,1)S(1)} %get-tuple-element.11), channel_id=1, source_target_pairs={{0,16},{16,32},{32,48},{48,64},{64,80},{80,96},{96,112},{112,128},... | collective-permute-start | bytes 1376264 | tf_op jit(solution)/shard_map/forward_experts/ppermute | solution.py:13
  486.7 74.6 %reduce-scatter.8.cloned.1.call-done = bf16[1,128,3584]{2,1,0:T(8,128)(2,1)} async-done(((bf16[4,128,3584]{2,1,0:T(8,128)(2,1)}), bf16[1,128,3584]{2,1,0:T(8,128)(2,1)}) %reduce-scatter.8.cloned.1.call-update) | async-done | bytes 917520 | tf_op jit(solution)/shard_map/backward_experts/reduce_scatter | solution.py:87
  561.3 1.4 add_convert_fusion.3
  562.7 0.6 collective-permute-start.2
  563.3 1.0 pad_maximum_fusion
  564.3 13.4 %collective-permute-done.2 = bf16[1,128,3584]{2,1,0:T(8,128)(2,1)S(1)} collective-permute-done((bf16[1,128,3584]{2,1,0:T(8,128)(2,1)S(1)}, bf16[1,128,3584]{2,1,0:T(8,128)(2,1)S(1)}, u32[]{:S(2)}, u32[]{:S(2)}) %collective-permute-start.2) | collective-permute-done | bytes 917536 | tf_op jit(solution)/shard_map/backward_experts/ppermute | solution.py:13
  577.7 0.9 copy.100
  (63 shorter events, 2.8 us)
Async XLA Ops:
  7.2 71.9 %all-gather.8.cloned.1.call-start = ((), (), s32[]{:S(2)}) async-start(), calls=%async_computation.11 | async-start | bytes 4587520 | tf_op jit(solution)/shard_map/gather_along_z/all_gather | solution.py:118
  7.9 150.4 %all-gather.4.cloned.1.call-start = ((), (), s32[]{:S(2)}) async-start(), calls=%async_computation.9 | async-start | bytes 4587520 | tf_op jit(solution)/shard_map/gather_along_z/all_gather | solution.py:118
  85.9 79.3 %all-to-all-start.1 = ((bf16[4,192,3584]{2,1,0:T(8,128)(2,1)}), bf16[4,192,3584]{2,1,0:T(8,128)(2,1)}, u32[]{:S(2)}, u32[]{:S(2)}) async-start(bf16[4,192,3584]{2,1,0:T(8,128)(2,1)} %bitcast.109), calls=%async_computation.1 | async-start | bytes 11010048 | tf_op jit(solution)/shard_map/backward_experts/all_to_all | solution.py:77
  91.0 145.6 %all-gather.6.cloned.1.call-start = ((), (), s32[]{:S(2)}) async-start(), calls=%async_computation.10 | async-start | bytes 4587520 | tf_op jit(solution)/shard_map/gather_along_z/all_gather | solution.py:118
  165.2 78.3 %all-to-all-start.2 = ((bf16[4,192,3584]{2,1,0:T(8,128)(2,1)}), bf16[4,192,3584]{2,1,0:T(8,128)(2,1)}, u32[]{:S(2)}, u32[]{:S(2)}) async-start(bf16[4,192,3584]{2,1,0:T(8,128)(2,1)} %bitcast.108), calls=%async_computation.2 | async-start | bytes 11010048 | tf_op jit(solution)/shard_map/backward_experts/all_to_all | solution.py:77
  243.5 70.1 %all-to-all-start = ((bf16[4,192,3584]{2,1,0:T(8,128)(2,1)}), bf16[4,192,3584]{2,1,0:T(8,128)(2,1)}, u32[]{:S(2)}, u32[]{:S(2)}) async-start(bf16[4,192,3584]{2,1,0:T(8,128)(2,1)} %bitcast.110), calls=%async_computation | async-start | bytes 11010048 | tf_op jit(solution)/shard_map/forward_experts/all_to_all | solution.py:77
  313.5 7.0 %copy-start.4 = (bf16[1,512,3584]{2,1,0:T(8,128)(2,1)S(1)}, bf16[1,512,3584]{2,1,0:T(8,128)(2,1)}, u32[]{:S(2)}) copy-start(bf16[1,512,3584]{2,1,0:T(8,128)(2,1)} %param.17) | copy-start | bytes 11010052
  320.6 3.2 copy-start.5
  323.8 35.2 %all-to-all-start.3 = ((bf16[4,192,1792]{2,1,0:T(8,128)(2,1)}), bf16[4,192,1792]{2,1,0:T(8,128)(2,1)S(1)}, u32[]{:S(2)}, u32[]{:S(2)}) async-start(bf16[4,192,1792]{2,1,0:T(8,128)(2,1)} %bitcast.118), calls=%async_computation.3 | async-start | bytes 5505024 | tf_op jit(solution)/shard_map/forward_experts/all_to_all | solution.py:77
  358.9 1.6 copy-start.2
  360.5 34.4 %all-to-all-start.4 = ((bf16[4,192,1792]{2,1,0:T(8,128)(2,1)}), bf16[4,192,1792]{2,1,0:T(8,128)(2,1)S(1)}, u32[]{:S(2)}, u32[]{:S(2)}) async-start(bf16[4,192,1792]{2,1,0:T(8,128)(2,1)} %bitcast.117), calls=%async_computation.5 | async-start | bytes 5505024 | tf_op jit(solution)/shard_map/forward_experts/all_to_all | solution.py:77
  366.8 105.6 %reduce-scatter.4.cloned.1.call-start = ((), (), s32[]{:S(2)}) async-start(), calls=%async_computation.12 | async-start | bytes 2293760 | tf_op jit(solution)/shard_map/forward_experts/reduce_scatter | solution.py:87
  366.8 3.6 copy-start.3
  395.0 64.8 %all-to-all-start.5 = ((bf16[4,192,3584]{2,1,0:T(8,128)(2,1)}), bf16[4,192,3584]{2,1,0:T(8,128)(2,1)}, u32[]{:S(2)}, u32[]{:S(2)}) async-start(bf16[4,192,3584]{2,1,0:T(8,128)(2,1)} %bitcast.107), calls=%async_computation.7 | async-start | bytes 11010048 | tf_op jit(solution)/shard_map/backward_experts/all_to_all | solution.py:77
  402.8 70.7 %reduce-scatter.6.cloned.1.call-start = ((), (), s32[]{:S(2)}) async-start(), calls=%async_computation.13 | async-start | bytes 2293760 | tf_op jit(solution)/shard_map/forward_experts/reduce_scatter | solution.py:87
  407.6 153.7 %reduce-scatter.8.cloned.1.call-start = ((), (), s32[]{:S(2)}) async-start(), calls=%async_computation.14 | async-start | bytes 4587520 | tf_op jit(solution)/shard_map/backward_experts/reduce_scatter | solution.py:87
  472.4 1.2 copy-start
  472.4 88.9 %copy-start.1 = (bf16[1,128,3584]{2,1,0:T(8,128)(2,1)S(1)}, bf16[1,128,3584]{2,1,0:T(8,128)(2,1)}, u32[]{:S(2)}) copy-start(bf16[1,128,3584]{2,1,0:T(8,128)(2,1)} %param.13) | copy-start | bytes 2752516
  474.9 88.4 %collective-permute-start.1 = (bf16[1,128,1792]{2,1,0:T(8,128)(2,1)S(1)}, bf16[1,128,1792]{2,1,0:T(8,128)(2,1)S(1)}, u32[]{:S(2)}, u32[]{:S(2)}) collective-permute-start(bf16[1,128,1792]{2,1,0:T(8,128)(2,1)S(1)} %get-tuple-element.11), channel_id=1, source_target_pairs={{0,16},{16,32},{32,48},{48,64},{64,80},{80,96},{96,112},{112,128},... | collective-permute-start | bytes 1376264 | tf_op jit(solution)/shard_map/forward_experts/ppermute | solution.py:13
  486.6 76.7 %collective-permute-start = (bf16[1,128,1792]{2,1,0:T(8,128)(2,1)S(1)}, bf16[1,128,1792]{2,1,0:T(8,128)(2,1)S(1)}, u32[]{:S(2)}, u32[]{:S(2)}) collective-permute-start(bf16[1,128,1792]{2,1,0:T(8,128)(2,1)S(1)} %get-tuple-element.10), channel_id=1, source_target_pairs={{0,16},{16,32},{32,48},{48,64},{64,80},{80,96},{96,112},{112,128},... | collective-permute-start | bytes 1376264 | tf_op jit(solution)/shard_map/forward_experts/ppermute | solution.py:13
  562.7 15.0 %collective-permute-start.2 = (bf16[1,128,3584]{2,1,0:T(8,128)(2,1)S(1)}, bf16[1,128,3584]{2,1,0:T(8,128)(2,1)S(1)}, u32[]{:S(2)}, u32[]{:S(2)}) collective-permute-start(bf16[1,128,3584]{2,1,0:T(8,128)(2,1)S(1)} %add_convert_fusion.3), channel_id=1, source_target_pairs={{0,240},{16,0},{32,16},{48,32},{64,48},{80,64},{96,80},{112,96},{1... | collective-permute-start | bytes 2752520 | tf_op jit(solution)/shard_map/backward_experts/ppermute | solution.py:13
Sparse Core Ops, SparseCore 0:
  9.8 69.1 all-gather.7
  80.8 77.4 all-gather.3
  160.1 76.4 all-gather.5
  373.8 52.9 reduce-scatter.3
  429.2 44.2 reduce-scatter.5
  475.9 85.3 reduce-scatter.7

commit v7 on v6

--- a/solution.py
+++ b/solution.py
@@ -153,19 +153,24 @@
         fwd_rows = swap_x(pack_rows(fwd_tok_z, fwd_table), x_count)
         fwd_rows, bwd_res = lax.optimization_barrier((fwd_rows, bwd_res))
 
+    with jax.named_scope("forward_experts"):
+        w_down_parts = [w_down[:, lo:hi] for lo, hi in cuts]
+        fwd_res_parts = forward_work(fwd_rows, w_up, w_down_parts)
+
     with jax.named_scope("backward_experts"):
         bwd_back = swap_x(bwd_res, x_count)
         bwd_part = weighted_partial(bwd_back, bwd_slots, bwd_weights_z, slot_total)
+        bwd_part, fwd_res_parts = lax.optimization_barrier((bwd_part, fwd_res_parts))
         bwd_out = sum_back(bwd_grads[0], bwd_part, z_index, jnp.bfloat16)
-        prev_grad = from_behind(bwd_out[None], "pp", -1)
 
     with jax.named_scope("forward_experts"):
-        w_down_parts = [w_down[:, lo:hi] for lo, hi in cuts]
-        fwd_res_parts = forward_work(fwd_rows, w_up, w_down_parts)
         next_parts = []
         for (lo, hi), fwd_res in zip(cuts, fwd_res_parts):
             fwd_back = swap_x(fwd_res, x_count)
             fwd_part = weighted_partial(fwd_back, fwd_slots, fwd_weights_z, slot_total)
+            if not next_parts:
+                bwd_out, fwd_part = lax.optimization_barrier((bwd_out, fwd_part))
+                prev_grad = from_behind(bwd_out[None], "pp", -1)
             fwd_out = sum_back(fwd_tokens[0][:, lo:hi], fwd_part, z_index, jnp.bfloat16)
             next_parts.append(from_behind(fwd_out[None], "pp", 1))
         next_input = jnp.concatenate(next_parts, axis=-1)

time: 587 us -> 598 us (1.019)
  waiting for transfers between devices: 406 us -> 418 us
    reduce_scatter x3, waiting for transfers between devices: 75.6 us -> 98.9 us  [sum_back(): lax.psum_scatter(partial.astype(wire_type), 'ez', scatter_dimension=0, ti...]
    ppermute x3, starting transfers between devices: 12.4 us -> 2.08 us  [from_behind(): lax.ppermute(value, axis, [(i, (i + by) % size) for i in range(size)])]
  transfers between devices with their start and end apart: 15 -> 15, of which waited for: 10 -> 12; matrix products, arithmetic and copies ran while one was open for 14% -> 14% of each run, Pallas kernels for 0% -> 0%
where the time goes in v7:
time: 598 us; the launch traced here: 593 us
  waiting for transfers between devices  418 us (70%)
  matrix products  79.3 us (13%)
  starting transfers between devices  48.7 us (8%)
  blocking collectives  14.4 us (2%)
  between operations  14.3 us (2%)
  other arithmetic  12.6 us (2%)
  local copies, waits for them, and re-layouts  6 us (1%)
    all_gather x3, waiting for transfers between devices, gather_z(): return lax.all_gather(value[0], 'ez', axis=0, tiled=False)  172 us
    all_to_all x6, waiting for transfers between devices, swap_x(): got = lax.all_to_all(spread, 'ex', split_axis=0, concat_axis=0, tiled=True)  134 us
    reduce_scatter x3, waiting for transfers between devices, sum_back(): lax.psum_scatter(partial.astype(wire_type), 'ez', scatter_dimension=0, ti...  98.9 us
    all_to_all x6, starting transfers between devices, swap_x(): got = lax.all_to_all(spread, 'ex', split_axis=0, concat_axis=0, tiled=True)  46.3 us
    dot_general x6, matrix products, weighted_partial(): picked = jnp.dot(table, results, preferred_element_type=jnp.float32)  26 us
    dot_general x3, matrix products, pack_rows(): lax.dot_general(table, flat, (((0,), (0,)), ((), ())), preferred_element_...  20.7 us
    all_gather x1, blocking collectives, gather_z(): return lax.all_gather(value[0], 'ez', axis=0, tiled=False)  14.4 us
    dot_general x1, matrix products, backward_work(): lax.dot_general(hidden_grad, w_up, (((1,), (1,)), ((), ())), preferred_el...  13.2 us
  transfers between devices with their start and end apart: 15, of which 12 were waited for; matrix products, arithmetic and copies ran while one was open for 14% of the time, Pallas kernels for 0%

profile of v7, /device:TPU:29, one launch (start us, length us, event | category | flops | bytes accessed | tf_op | source)
XLA Modules:
  0.0 592.8 jit_solution(3927167276129482439)
XLA Ops:
  7.2 0.7 all-gather.4.cloned.1.call-update
  7.9 0.7 all-gather.8.cloned.1.call-update
  8.7 0.7 convert_element_type.120
  10.0 0.7 pad_maximum_fusion.1
  10.7 14.4 %all_gather.12 = f32[4,128,8]{1,2,0:T(8,128)S(1)} all-gather(f32[1,128,8]{1,2,0:T(8,128)S(1)} %pad_maximum_fusion.1), channel_id=1, replica_groups=mesh['pp'=16,'ex'=4,'ez'=4] {'ez'}, dimensions={0}, use_global_device_ids=true | all-gather | bytes 20480 | tf_op jit(solution)/shard_map/gather_along_z/all_gather | solution.py:118
  25.6 2.3 reduce-window.14
  28.7 2.3 reduce-window.16
  31.5 1.2 compare_select_fusion
  33.1 46.7 %all-gather.4.cloned.1.call-done = bf16[4,128,3584]{2,1,0:T(8,128)(2,1)} async-done(((bf16[1,128,3584]{2,1,0:T(8,128)(2,1)}), bf16[4,128,3584]{2,1,0:T(8,128)(2,1)}) %all-gather.4.cloned.1.call-update) | async-done | bytes 3670032 | tf_op jit(solution)/shard_map/gather_along_z/all_gather | solution.py:118
  79.8 6.9 %convolution_convert_fusion.1 = bf16[768,3584]{1,0:T(8,128)(2,1)} fusion(bf16[512,768]{1,0:T(8,128)(2,1)S(1)} %fusion.9, bf16[512,3584]{1,0:T(8,128)(2,1)} %bitcast.148), kind=kOutput, calls=%fused_computation.2 | convolution fusion | flops 2821324800 | bytes 9961472 | tf_op jit(solution)/shard_map/backward_experts/dot_general | solution.py:44
  86.7 5.7 all-to-all-start.2
  92.4 0.7 all-gather.6.cloned.1.call-update
  93.1 64.8 %all-gather.8.cloned.1.call-done = bf16[4,128,3584]{2,1,0:T(8,128)(2,1)} async-done(((bf16[1,128,3584]{2,1,0:T(8,128)(2,1)}), bf16[4,128,3584]{2,1,0:T(8,128)(2,1)}) %all-gather.8.cloned.1.call-update) | async-done | bytes 3670032 | tf_op jit(solution)/shard_map/gather_along_z/all_gather | solution.py:118
  157.9 6.8 %convolution_convert_fusion.2 = bf16[768,3584]{1,0:T(8,128)(2,1)} fusion(bf16[512,768]{1,0:T(8,128)(2,1)S(1)} %fusion.9, bf16[512,3584]{1,0:T(8,128)(2,1)} %bitcast.147), kind=kOutput, calls=%fused_computation.3 | convolution fusion | flops 2821324800 | bytes 9961472 | tf_op jit(solution)/shard_map/backward_experts/dot_general | solution.py:44
  164.7 10.3 %all-to-all-start.1 = ((bf16[4,192,3584]{2,1,0:T(8,128)(2,1)}), bf16[4,192,3584]{2,1,0:T(8,128)(2,1)}, u32[]{:S(2)}, u32[]{:S(2)}) async-start(bf16[4,192,3584]{2,1,0:T(8,128)(2,1)} %bitcast.111), calls=%async_computation.1 | async-start | bytes 11010048 | tf_op jit(solution)/shard_map/backward_experts/all_to_all | solution.py:77
  175.5 60.8 %all-gather.6.cloned.1.call-done = bf16[4,128,3584]{2,1,0:T(8,128)(2,1)} async-done(((bf16[1,128,3584]{2,1,0:T(8,128)(2,1)}), bf16[4,128,3584]{2,1,0:T(8,128)(2,1)}) %all-gather.6.cloned.1.call-update) | async-done | bytes 3670032 | tf_op jit(solution)/shard_map/gather_along_z/all_gather | solution.py:118
  236.2 6.9 %convolution_convert_fusion.3 = bf16[768,3584]{1,0:T(8,128)(2,1)} fusion(bf16[512,768]{1,0:T(8,128)(2,1)S(1)} %fusion.10, bf16[512,3584]{1,0:T(8,128)(2,1)} %bitcast.149), kind=kOutput, calls=%fused_computation.4 | convolution fusion | flops 2821324800 | bytes 9961472 | tf_op jit(solution)/shard_map/forward_experts/dot_general | solution.py:44
  243.2 10.3 %all-to-all-start = ((bf16[4,192,3584]{2,1,0:T(8,128)(2,1)}), bf16[4,192,3584]{2,1,0:T(8,128)(2,1)}, u32[]{:S(2)}, u32[]{:S(2)}) async-start(bf16[4,192,3584]{2,1,0:T(8,128)(2,1)} %bitcast.113), calls=%async_computation | async-start | bytes 11010048 | tf_op jit(solution)/shard_map/forward_experts/all_to_all | solution.py:77
  253.4 6.1 %fusion.3 = f32[768,512]{1,0:T(8,128)S(1)} fusion(bf16[768,3584]{1,0:T(8,128)(2,1)} %bitcast.20, bf16[1,3584,512]{2,1,0:T(8,128)(2,1)} %param.16), kind=kOutput, calls=%fused_computation.8 | convolution fusion | flops 2818572288 | bytes 10747904 | tf_op jit(solution)/shard_map/backward_experts/dot_general | solution.py:67
  259.5 13.2 %convolution_convert_fusion = bf16[768,3584]{1,0:T(8,128)(2,1)} fusion(bf16[1,3584,512]{2,1,0:T(8,128)(2,1)} %param.16, f32[768,512]{1,0:T(8,128)S(1)} %fusion.3, bf16[768,3584]{1,0:T(8,128)(2,1)} %bitcast.24, bf16[1,512,3584]{2,1,0:T(8,128)(2,1)} %param.17), kind=kOutput, calls=%fused_computation.1 | convolution fusion | flops 5643436032 | bytes 19922944 | tf_op jit(solution)/shard_map/backward_experts/dot_general | solution.py:70
  272.7 40.6 %all-to-all-done = bf16[4,192,3584]{2,1,0:T(8,128)(2,1)} async-done(((bf16[4,192,3584]{2,1,0:T(8,128)(2,1)}), bf16[4,192,3584]{2,1,0:T(8,128)(2,1)}, u32[]{:S(2)}, u32[]{:S(2)}) %all-to-all-start) | async-done | bytes 5505056 | tf_op jit(solution)/shard_map/forward_experts/all_to_all | solution.py:77
  313.2 7.5 %all-to-all-start.3 = ((bf16[4,192,3584]{2,1,0:T(8,128)(2,1)}), bf16[4,192,3584]{2,1,0:T(8,128)(2,1)}, u32[]{:S(2)}, u32[]{:S(2)}) async-start(bf16[4,192,3584]{2,1,0:T(8,128)(2,1)} %bitcast.110), calls=%async_computation.3 | async-start | bytes 11010048 | tf_op jit(solution)/shard_map/backward_experts/all_to_all | solution.py:77
  321.0 7.0 %multiply_convert_fusion = bf16[768,512]{1,0:T(8,128)(2,1)S(1)} fusion(bf16[768,3584]{1,0:T(8,128)(2,1)} %bitcast.17, bf16[1,3584,512]{2,1,0:T(8,128)(2,1)} %param.16), kind=kOutput, calls=%fused_computation.27 | convolution fusion | flops 2820538368 | bytes 9961472 | tf_op jit(solution)/shard_map/forward_experts/dot_general | solution.py:62
  328.0 3.2 convolution_convert_fusion.4
  331.2 3.1 convolution_convert_fusion.5
  334.4 45.1 %all-to-all-done.3 = bf16[4,192,3584]{2,1,0:T(8,128)(2,1)} async-done(((bf16[4,192,3584]{2,1,0:T(8,128)(2,1)}), bf16[4,192,3584]{2,1,0:T(8,128)(2,1)}, u32[]{:S(2)}, u32[]{:S(2)}) %all-to-all-start.3) | async-done | bytes 5505056 | tf_op jit(solution)/shard_map/backward_experts/all_to_all | solution.py:77
  379.4 5.2 fusion.13
  384.6 7.4 %multiply_add_fusion = bf16[512,3584]{1,0:T(8,128)(2,1)} fusion(f32[512,3584]{1,0:T(8,128)S(1)} %fusion.13, bf16[768,3584]{1,0:T(8,128)(2,1)} %bitcast.27, f32[512]{0:T(512)S(1)} %bitcast.143, f32[512]{0:T(512)S(1)} %bitcast.144, s32[512]{0:T(512)S(1)} %bitcast.137), kind=kOutput, calls=%fused_computation | convolution fusion | flops 2826305536 | bytes 16521216 | tf_op jit(solution)/shard_map/backward_experts/dot_general | solution.py:55
  392.1 6.3 %all-to-all-start.5 = ((bf16[4,192,1792]{2,1,0:T(8,128)(2,1)}), bf16[4,192,1792]{2,1,0:T(8,128)(2,1)S(1)}, u32[]{:S(2)}, u32[]{:S(2)}) async-start(bf16[4,192,1792]{2,1,0:T(8,128)(2,1)} %bitcast.41), calls=%async_computation.7 | async-start | bytes 5505024 | tf_op jit(solution)/shard_map/forward_experts/all_to_all | solution.py:77
  398.6 28.0 %all-to-all-done.5 = bf16[4,192,1792]{2,1,0:T(8,128)(2,1)S(1)} async-done(((bf16[4,192,1792]{2,1,0:T(8,128)(2,1)}), bf16[4,192,1792]{2,1,0:T(8,128)(2,1)S(1)}, u32[]{:S(2)}, u32[]{:S(2)}) %all-to-all-start.5) | async-done | bytes 2752544 | tf_op jit(solution)/shard_map/forward_experts/all_to_all | solution.py:77
  426.6 1.5 copy-done.3
  428.1 6.3 %all-to-all-start.4 = ((bf16[4,192,1792]{2,1,0:T(8,128)(2,1)}), bf16[4,192,1792]{2,1,0:T(8,128)(2,1)S(1)}, u32[]{:S(2)}, u32[]{:S(2)}) async-start(bf16[4,192,1792]{2,1,0:T(8,128)(2,1)} %bitcast.34), calls=%async_computation.5 | async-start | bytes 5505024 | tf_op jit(solution)/shard_map/forward_experts/all_to_all | solution.py:77
  434.4 3.6 fusion.11
  438.0 3.1 add_convert_fusion
  441.5 20.4 %all-to-all-done.4 = bf16[4,192,1792]{2,1,0:T(8,128)(2,1)S(1)} async-done(((bf16[4,192,1792]{2,1,0:T(8,128)(2,1)}), bf16[4,192,1792]{2,1,0:T(8,128)(2,1)S(1)}, u32[]{:S(2)}, u32[]{:S(2)}) %all-to-all-start.4) | async-done | bytes 2752544 | tf_op jit(solution)/shard_map/forward_experts/all_to_all | solution.py:77
  461.9 1.5 copy-done.2
  463.4 1.7 fusion.12
  465.1 4.9 multiply_add_fusion.1
  470.1 3.6 reduce-scatter.4.cloned.1.call-done
  473.7 1.4 fusion.16
  475.1 1.8 collective-permute-start.2
  476.9 45.1 %reduce-scatter.8.cloned.1.call-done = bf16[1,128,1792]{2,1,0:T(8,128)(2,1)} async-done(((bf16[4,128,1792]{2,1,0:T(8,128)(2,1)}), bf16[1,128,1792]{2,1,0:T(8,128)(2,1)}) %reduce-scatter.8.cloned.1.call-update) | async-done | bytes 458768 | tf_op jit(solution)/shard_map/forward_experts/reduce_scatter | solution.py:87
  521.9 50.2 %reduce-scatter.6.cloned.1.call-done = bf16[1,128,1792]{2,1,0:T(8,128)(2,1)} async-done(((bf16[4,128,1792]{2,1,0:T(8,128)(2,1)}), bf16[1,128,1792]{2,1,0:T(8,128)(2,1)}) %reduce-scatter.6.cloned.1.call-update) | async-done | bytes 458768 | tf_op jit(solution)/shard_map/forward_experts/reduce_scatter | solution.py:87
  572.1 1.4 fusion.25
  573.8 5.3 collective-permute-done
  579.1 4.9 collective-permute-done.1
  584.1 1.0 pad_maximum_fusion
  585.0 0.9 copy.100
  (63 shorter events, 4.5 us)
Async XLA Ops:
  7.2 72.6 %all-gather.4.cloned.1.call-start = ((), (), s32[]{:S(2)}) async-start(), calls=%async_computation.9 | async-start | bytes 4587520 | tf_op jit(solution)/shard_map/gather_along_z/all_gather | solution.py:118
  7.9 150.0 %all-gather.8.cloned.1.call-start = ((), (), s32[]{:S(2)}) async-start(), calls=%async_computation.11 | async-start | bytes 4587520 | tf_op jit(solution)/shard_map/gather_along_z/all_gather | solution.py:118
  86.7 78.1 %all-to-all-start.2 = ((bf16[4,192,3584]{2,1,0:T(8,128)(2,1)}), bf16[4,192,3584]{2,1,0:T(8,128)(2,1)}, u32[]{:S(2)}, u32[]{:S(2)}) async-start(bf16[4,192,3584]{2,1,0:T(8,128)(2,1)} %bitcast.112), calls=%async_computation.2 | async-start | bytes 11010048 | tf_op jit(solution)/shard_map/backward_experts/all_to_all | solution.py:77
  92.4 143.9 %all-gather.6.cloned.1.call-start = ((), (), s32[]{:S(2)}) async-start(), calls=%async_computation.10 | async-start | bytes 4587520 | tf_op jit(solution)/shard_map/gather_along_z/all_gather | solution.py:118
  164.7 78.4 %all-to-all-start.1 = ((bf16[4,192,3584]{2,1,0:T(8,128)(2,1)}), bf16[4,192,3584]{2,1,0:T(8,128)(2,1)}, u32[]{:S(2)}, u32[]{:S(2)}) async-start(bf16[4,192,3584]{2,1,0:T(8,128)(2,1)} %bitcast.111), calls=%async_computation.1 | async-start | bytes 11010048 | tf_op jit(solution)/shard_map/backward_experts/all_to_all | solution.py:77
  243.2 70.1 %all-to-all-start = ((bf16[4,192,3584]{2,1,0:T(8,128)(2,1)}), bf16[4,192,3584]{2,1,0:T(8,128)(2,1)}, u32[]{:S(2)}, u32[]{:S(2)}) async-start(bf16[4,192,3584]{2,1,0:T(8,128)(2,1)} %bitcast.113), calls=%async_computation | async-start | bytes 11010048 | tf_op jit(solution)/shard_map/forward_experts/all_to_all | solution.py:77
  313.2 66.2 %all-to-all-start.3 = ((bf16[4,192,3584]{2,1,0:T(8,128)(2,1)}), bf16[4,192,3584]{2,1,0:T(8,128)(2,1)}, u32[]{:S(2)}, u32[]{:S(2)}) async-start(bf16[4,192,3584]{2,1,0:T(8,128)(2,1)} %bitcast.110), calls=%async_computation.3 | async-start | bytes 11010048 | tf_op jit(solution)/shard_map/backward_experts/all_to_all | solution.py:77
  320.7 153.0 %reduce-scatter.4.cloned.1.call-start = ((), (), s32[]{:S(2)}) async-start(), calls=%async_computation.12 | async-start | bytes 4587520 | tf_op jit(solution)/shard_map/backward_experts/reduce_scatter | solution.py:87
  321.0 7.0 %copy-start.5 = (bf16[1,512,3584]{2,1,0:T(8,128)(2,1)S(1)}, bf16[1,512,3584]{2,1,0:T(8,128)(2,1)}, u32[]{:S(2)}) copy-start(bf16[1,512,3584]{2,1,0:T(8,128)(2,1)} %param.17) | copy-start | bytes 11010052
  392.1 34.5 %all-to-all-start.5 = ((bf16[4,192,1792]{2,1,0:T(8,128)(2,1)}), bf16[4,192,1792]{2,1,0:T(8,128)(2,1)S(1)}, u32[]{:S(2)}, u32[]{:S(2)}) async-start(bf16[4,192,1792]{2,1,0:T(8,128)(2,1)} %bitcast.41), calls=%async_computation.7 | async-start | bytes 5505024 | tf_op jit(solution)/shard_map/forward_experts/all_to_all | solution.py:77
  426.6 1.5 copy-start.3
  428.1 33.7 %all-to-all-start.4 = ((bf16[4,192,1792]{2,1,0:T(8,128)(2,1)}), bf16[4,192,1792]{2,1,0:T(8,128)(2,1)S(1)}, u32[]{:S(2)}, u32[]{:S(2)}) async-start(bf16[4,192,1792]{2,1,0:T(8,128)(2,1)} %bitcast.34), calls=%async_computation.5 | async-start | bytes 5505024 | tf_op jit(solution)/shard_map/forward_experts/all_to_all | solution.py:77
  434.4 87.5 %reduce-scatter.8.cloned.1.call-start = ((), (), s32[]{:S(2)}) async-start(), calls=%async_computation.14 | async-start | bytes 2293760 | tf_op jit(solution)/shard_map/forward_experts/reduce_scatter | solution.py:87
  434.4 3.6 copy-start.4
  441.2 130.9 %reduce-scatter.6.cloned.1.call-start = ((), (), s32[]{:S(2)}) async-start(), calls=%async_computation.13 | async-start | bytes 2293760 | tf_op jit(solution)/shard_map/forward_experts/reduce_scatter | solution.py:87
  461.9 1.5 copy-start.2
  465.1 8.6 %copy-start = (bf16[1,128,3584]{2,1,0:T(8,128)(2,1)S(1)}, bf16[1,128,3584]{2,1,0:T(8,128)(2,1)}, u32[]{:S(2)}) copy-start(bf16[1,128,3584]{2,1,0:T(8,128)(2,1)} %param.13) | copy-start | bytes 2752516
  470.1 102.1 %copy-start.1 = (bf16[1,128,3584]{2,1,0:T(8,128)(2,1)S(1)}, bf16[1,128,3584]{2,1,0:T(8,128)(2,1)}, u32[]{:S(2)}) copy-start(bf16[1,128,3584]{2,1,0:T(8,128)(2,1)} %param.9) | copy-start | bytes 2752516
  475.1 98.7 %collective-permute-start.2 = (bf16[1,128,3584]{2,1,0:T(8,128)(2,1)S(1)}, bf16[1,128,3584]{2,1,0:T(8,128)(2,1)S(1)}, u32[]{:S(2)}, u32[]{:S(2)}) collective-permute-start(bf16[1,128,3584]{2,1,0:T(8,128)(2,1)S(1)} %bitcast.126), channel_id=1, source_target_pairs={{0,240},{16,0},{32,16},{48,32},{64,48},{80,64},{96,80},{112,96},{1... | collective-permute-start | bytes 2752520 | tf_op jit(solution)/shard_map/forward_experts/ppermute | solution.py:13
  573.5 5.7 collective-permute-start
  573.7 10.3 %collective-permute-start.1 = (bf16[1,128,1792]{2,1,0:T(8,128)(2,1)S(1)}, bf16[1,128,1792]{2,1,0:T(8,128)(2,1)S(1)}, u32[]{:S(2)}, u32[]{:S(2)}) collective-permute-start(bf16[1,128,1792]{2,1,0:T(8,128)(2,1)S(1)} %get-tuple-element.21), channel_id=1, source_target_pairs={{0,16},{16,32},{32,48},{48,64},{64,80},{80,96},{96,112},{112,128},... | collective-permute-start | bytes 1376264 | tf_op jit(solution)/shard_map/forward_experts/ppermute | solution.py:13
Sparse Core Ops, SparseCore 0:
  9.8 69.9 all-gather.3
  81.6 76.2 all-gather.7
  159.7 76.4 all-gather.5
  392.2 81.4 reduce-scatter.3
  476.1 45.7 reduce-scatter.7
  524.3 47.7 reduce-scatter.5

commit v8 on v6

--- a/solution.py
+++ b/solution.py
@@ -86,6 +86,12 @@
     else:
         summed = lax.psum_scatter(partial.astype(wire_type), "ez", scatter_dimension=0, tiled=False)
         total = residual.astype(jnp.float32) + summed.astype(jnp.float32)
+    return total.astype(jnp.bfloat16)
+
+
+def swap_sum_back(residual, partial):
+    got = lax.all_to_all(partial.astype(jnp.bfloat16), "ez", split_axis=0, concat_axis=0, tiled=True)
+    total = residual.astype(jnp.float32) + jnp.sum(got.astype(jnp.float32), axis=0)
     return total.astype(jnp.bfloat16)
 
 
@@ -123,8 +129,7 @@
     with jax.named_scope("gather_along_z"):
         bwd_tok_z = gather_z(bwd_tokens)
         bwd_grads_z = gather_z(bwd_grads)
-        fwd_tokens_in, bwd_grads_z = lax.optimization_barrier((fwd_tokens, bwd_grads_z))
-        fwd_tok_z = gather_z(fwd_tokens_in)
+        fwd_tok_z = gather_z(fwd_tokens)
         meta = jnp.concatenate(
             [fwd_routes.astype(jnp.float32), fwd_weights, bwd_routes.astype(jnp.float32), bwd_weights], axis=-1
         )
@@ -145,30 +150,39 @@
     with jax.named_scope("backward_experts"):
         bwd_table = slot_table(bwd_slots, slot_total)
         bwd_rows = swap_x(pack_rows(bwd_tok_z, bwd_table), x_count)
-        grad_rows = swap_x(pack_rows(bwd_grads_z, bwd_table), x_count)
+
+    with jax.named_scope("dispatch"):
+        fwd_table = slot_table(fwd_slots, slot_total)
+        pair = jnp.stack(
+            [
+                pack_rows(bwd_grads_z, bwd_table).reshape(x_count, -1, features),
+                pack_rows(fwd_tok_z, fwd_table).reshape(x_count, -1, features),
+            ],
+            axis=1,
+        )
+        pair = swap_x(pair, x_count)
+        grad_rows = pair[:, 0].reshape(-1, features)
+        fwd_rows = pair[:, 1].reshape(-1, features)
+
+    with jax.named_scope("experts"):
         bwd_res = backward_work(bwd_rows, grad_rows, w_up, w_down)
-
-    with jax.named_scope("forward_experts"):
-        fwd_table = slot_table(fwd_slots, slot_total)
-        fwd_rows = swap_x(pack_rows(fwd_tok_z, fwd_table), x_count)
-        fwd_rows, bwd_res = lax.optimization_barrier((fwd_rows, bwd_res))
+        fwd_res = forward_work(fwd_rows, w_up, [w_down])[0]
+        back = jnp.stack(
+            [bwd_res.reshape(x_count, -1, features), fwd_res.reshape(x_count, -1, features)], axis=1
+        )
+        back = swap_x(back, x_count)
+        bwd_back = back[:, 0].reshape(-1, features)
+        fwd_back = back[:, 1].reshape(-1, features)
 
     with jax.named_scope("backward_experts"):
-        bwd_back = swap_x(bwd_res, x_count)
         bwd_part = weighted_partial(bwd_back, bwd_slots, bwd_weights_z, slot_total)
         bwd_out = sum_back(bwd_grads[0], bwd_part, z_index, jnp.bfloat16)
         prev_grad = from_behind(bwd_out[None], "pp", -1)
 
     with jax.named_scope("forward_experts"):
-        w_down_parts = [w_down[:, lo:hi] for lo, hi in cuts]
-        fwd_res_parts = forward_work(fwd_rows, w_up, w_down_parts)
-        next_parts = []
-        for (lo, hi), fwd_res in zip(cuts, fwd_res_parts):
-            fwd_back = swap_x(fwd_res, x_count)
-            fwd_part = weighted_partial(fwd_back, fwd_slots, fwd_weights_z, slot_total)
-            fwd_out = sum_back(fwd_tokens[0][:, lo:hi], fwd_part, z_index, jnp.bfloat16)
-            next_parts.append(from_behind(fwd_out[None], "pp", 1))
-        next_input = jnp.concatenate(next_parts, axis=-1)
+        fwd_part = weighted_partial(fwd_back, fwd_slots, fwd_weights_z, slot_total)
+        fwd_out = swap_sum_back(fwd_tokens[0], fwd_part)
+        next_input = from_behind(fwd_out[None], "pp", 1)
 
     return (next_input, prev_grad)
 

time: 587 us -> 742 us (1.26)
  blocking collectives: 14.4 us -> 166 us
  starting transfers between devices: 54.2 us -> 30.5 us
  waiting for transfers between devices: 406 us -> 427 us
  matrix products: 79.2 us -> 61.2 us
  local copies, waits for them, and re-layouts: 4.61 us -> 21.7 us
  other arithmetic: 12.6 us -> 20.6 us
    all_to_all x0 -> x1, blocking collectives: none -> 152 us  [swap_sum_back(): lax.all_to_all(partial.astype(jnp.bfloat16), 'ez', split_axis=0, concat_a...]
    all_to_all x6 -> x3, waiting for transfers between devices: 138 us -> 230 us  [swap_x(): got = lax.all_to_all(spread, 'ex', split_axis=0, concat_axis=0, tiled=True)]
    reduce_scatter x3 -> x1, waiting for transfers between devices: 75.6 us -> 0.01 us  [sum_back(): lax.psum_scatter(partial.astype(wire_type), 'ez', scatter_dimension=0, ti...]
    slice x2 -> x4, local copies, waits for them, and re-layouts: 0.19 us -> 18 us  [the longest x1 8.93 us: on_device(): grad_rows = pair[:, 0].reshape(-1, features)]
    all_to_all x6 -> x3, starting transfers between devices: 41.7 us -> 27.6 us  [swap_x(): got = lax.all_to_all(spread, 'ex', split_axis=0, concat_axis=0, tiled=True)]
    dot_general x1, matrix products: 13.3 us -> 3.31 us  [backward_work(): lax.dot_general(hidden_grad, w_up, (((1,), (1,)), ((), ())), preferred_el...]
    reshape x0 -> x2, other arithmetic: none -> 9.7 us  [swap_x(): spread = rows.reshape((x_count, -1) + rows.shape[1:])]
    ppermute x3 -> x2, starting transfers between devices: 12.4 us -> 2.73 us  [from_behind(): lax.ppermute(value, axis, [(i, (i + by) % size) for i in range(size)])]
  transfers between devices with their start and end apart: 15 -> 9, of which waited for: 10 -> 7; matrix products, arithmetic and copies ran while one was open for 14% -> 7% of each run, Pallas kernels for 0% -> 0%
where the time goes in v8:
time: 742 us; the launch traced here: 741 us
  waiting for transfers between devices  427 us (58%)
  blocking collectives  166 us (22%)
  matrix products  61.2 us (8%)
  starting transfers between devices  30.5 us (4%)
  local copies, waits for them, and re-layouts  21.7 us (3%)
  other arithmetic  20.6 us (3%)
  between operations  14.1 us (2%)
    all_to_all x3, waiting for transfers between devices, swap_x(): got = lax.all_to_all(spread, 'ex', split_axis=0, concat_axis=0, tiled=True)  230 us
    all_gather x3, waiting for transfers between devices, gather_z(): return lax.all_gather(value[0], 'ez', axis=0, tiled=False)  180 us
    all_to_all x1, blocking collectives, swap_sum_back(): lax.all_to_all(partial.astype(jnp.bfloat16), 'ez', split_axis=0, concat_a...  152 us
    all_to_all x3, starting transfers between devices, swap_x(): got = lax.all_to_all(spread, 'ex', split_axis=0, concat_axis=0, tiled=True)  27.6 us
    dot_general x3, matrix products, pack_rows(): lax.dot_general(table, flat, (((0,), (0,)), ((), ())), preferred_element_...  19.3 us
    dot_general x4, matrix products, weighted_partial(): picked = jnp.dot(table, results, preferred_element_type=jnp.float32)  19 us
  transfers between devices with their start and end apart: 9, of which 7 were waited for; matrix products, arithmetic and copies ran while one was open for 7% of the time, Pallas kernels for 0%

profile of v8, /device:TPU:29, one launch (start us, length us, event | category | flops | bytes accessed | tf_op | source)
XLA Modules:
  0.0 740.9 jit_solution(9459642635500880035)
XLA Ops:
  7.2 0.7 all-gather.4.cloned.1.call-update
  7.9 0.7 all-gather.6.cloned.1.call-update
  8.7 0.7 all-gather.8.cloned.1.call-update
  9.4 0.7 convert_element_type.100
  10.1 0.7 convert_element_type.99
  10.8 0.7 pad_maximum_fusion
  11.5 14.4 %all_gather.12 = f32[4,128,8]{1,2,0:T(8,128)S(1)} all-gather(f32[1,128,8]{1,2,0:T(8,128)S(1)} %pad_maximum_fusion), channel_id=1, replica_groups=mesh['pp'=16,'ex'=4,'ez'=4] {'ez'}, dimensions={0}, use_global_device_ids=true | all-gather | bytes 20480 | tf_op jit(solution)/shard_map/gather_along_z/all_gather | solution.py:124
  25.9 0.2 copy.79
  26.2 2.3 reduce-window.14
  29.0 0.2 copy.86
  29.4 2.3 reduce-window.16
  32.2 1.2 compare_select_fusion
  33.4 0.4 fusion.12
  33.8 45.0 %all-gather.4.cloned.1.call-done = bf16[4,128,3584]{2,1,0:T(8,128)(2,1)} async-done(((bf16[1,128,3584]{2,1,0:T(8,128)(2,1)}), bf16[4,128,3584]{2,1,0:T(8,128)(2,1)}) %all-gather.4.cloned.1.call-update) | async-done | bytes 3670032 | tf_op jit(solution)/shard_map/gather_along_z/all_gather | solution.py:124
  78.8 6.9 convolution_convert_fusion.4
  85.7 8.0 %all-to-all-start = ((bf16[4,192,3584]{2,1,0:T(8,128)(2,1)}), bf16[4,192,3584]{2,1,0:T(8,128)(2,1)}, u32[]{:S(2)}, u32[]{:S(2)}) async-start(bf16[4,192,3584]{2,1,0:T(8,128)(2,1)} %bitcast.112), calls=%async_computation | async-start | bytes 11010048 | tf_op jit(solution)/shard_map/backward_experts/all_to_all | solution.py:77
  93.8 0.4 fusion.11
  94.2 62.4 %all-gather.6.cloned.1.call-done = bf16[4,128,3584]{2,1,0:T(8,128)(2,1)} async-done(((bf16[1,128,3584]{2,1,0:T(8,128)(2,1)}), bf16[4,128,3584]{2,1,0:T(8,128)(2,1)}) %all-gather.6.cloned.1.call-update) | async-done | bytes 3670032 | tf_op jit(solution)/shard_map/gather_along_z/all_gather | solution.py:124
  156.6 6.9 convolution_convert_fusion.3
  163.5 72.6 %all-gather.8.cloned.1.call-done = bf16[4,128,3584]{2,1,0:T(8,128)(2,1)} async-done(((bf16[1,128,3584]{2,1,0:T(8,128)(2,1)}), bf16[4,128,3584]{2,1,0:T(8,128)(2,1)}) %all-gather.8.cloned.1.call-update) | async-done | bytes 3670032 | tf_op jit(solution)/shard_map/gather_along_z/all_gather | solution.py:124
  236.1 5.5 convolution_convert_fusion.2
  241.6 4.8 maximum_bitcast_fusion
  246.5 11.2 %all-to-all-start.1 = ((bf16[4,1,2,192,3584]{4,3,2,1,0:T(8,128)(2,1)}), bf16[4,1,2,192,3584]{4,3,2,1,0:T(8,128)(2,1)}, u32[]{:S(2)}, u32[]{:S(2)}) async-start(bf16[4,1,2,192,3584]{4,3,2,1,0:T(8,128)(2,1)} %maximum_bitcast_fusion), calls=%async_computation.1 | async-start | bytes 22020096 | tf_op jit(solution)/shard_map/dispatch/all_to_all | solution.py:77
  257.7 6.1 fusion.6
  263.8 112.7 %all-to-all-done.1 = bf16[4,1,2,192,3584]{4,3,2,1,0:T(8,128)(2,1)} async-done(((bf16[4,1,2,192,3584]{4,3,2,1,0:T(8,128)(2,1)}), bf16[4,1,2,192,3584]{4,3,2,1,0:T(8,128)(2,1)}, u32[]{:S(2)}, u32[]{:S(2)}) %all-to-all-start.1) | async-done | bytes 11010080 | tf_op jit(solution)/shard_map/dispatch/all_to_all | solution.py:77
  376.5 8.9 %fusion.34 = (bf16[4,1,192,3584]{3,2,1,0:T(8,128)(2,1)}, bf16[4,1,192,3584]{3,2,1,0:T(8,128)(2,1)}) fusion(bf16[4,2,192,3584]{3,2,1,0:T(8,128)(2,1)} %bitcast.25), kind=kLoop, calls=%fused_computation.71 | loop fusion | bytes 22020096 | tf_op jit(solution)/shard_map/dispatch/slice | solution.py:164
  385.4 7.1 multiply_convert_fusion.1
  392.6 3.3 convolution_convert_fusion.1
  395.9 3.2 multiply_convert_fusion
  399.1 3.2 convolution_convert_fusion
  402.4 4.8 maximum_bitcast_fusion.1
  407.2 8.4 %all-to-all-start.2 = ((bf16[4,1,2,192,3584]{4,3,2,1,0:T(8,128)(2,1)}), bf16[4,1,2,192,3584]{4,3,2,1,0:T(8,128)(2,1)}, u32[]{:S(2)}, u32[]{:S(2)}) async-start(bf16[4,1,2,192,3584]{4,3,2,1,0:T(8,128)(2,1)} %maximum_bitcast_fusion.1), calls=%async_computation.2 | async-start | bytes 22020096 | tf_op jit(solution)/shard_map/experts/all_to_all | solution.py:77
  416.2 117.1 %all-to-all-done.2 = bf16[4,1,2,192,3584]{4,3,2,1,0:T(8,128)(2,1)} async-done(((bf16[4,1,2,192,3584]{4,3,2,1,0:T(8,128)(2,1)}), bf16[4,1,2,192,3584]{4,3,2,1,0:T(8,128)(2,1)}, u32[]{:S(2)}, u32[]{:S(2)}) %all-to-all-start.2) | async-done | bytes 11010080 | tf_op jit(solution)/shard_map/experts/all_to_all | solution.py:77
  533.4 8.9 %fusion.33 = (bf16[4,1,192,3584]{3,2,1,0:T(8,128)(2,1)}, bf16[4,1,192,3584]{3,2,1,0:T(8,128)(2,1)}) fusion(bf16[4,2,192,3584]{3,2,1,0:T(8,128)(2,1)} %bitcast.34), kind=kLoop, calls=%fused_computation.70 | loop fusion | bytes 22020096 | tf_op jit(solution)/shard_map/experts/slice | solution.py:174
  542.3 5.3 fusion.14
  547.6 4.8 add_convert_fusion
  552.5 5.3 fusion.13
  557.9 3.5 add_convert_fusion.1
  561.3 151.6 %all_to_all.20 = bf16[4,128,3584]{2,1,0:T(8,128)(2,1)S(1)} all-to-all(bf16[4,128,3584]{2,1,0:T(8,128)(2,1)S(1)} %bitcast.126), channel_id=1, replica_groups=mesh['pp'=16,'ex'=4,'ez'=4] {'ez'}, dimensions={0} | all-to-all | bytes 7340032 | tf_op jit(solution)/shard_map/forward_experts/all_to_all | solution.py:93
  713.0 0.5 convert_reduce_fusion
  713.5 0.2 fusion.10
  713.7 2.5 collective-permute-start
  716.1 1.4 add_convert_fusion.2
  717.5 0.3 collective-permute-start.1
  717.8 8.7 %collective-permute-done = bf16[1,128,3584]{2,1,0:T(8,128)(2,1)S(1)} collective-permute-done((bf16[1,128,3584]{2,1,0:T(8,128)(2,1)S(1)}, bf16[1,128,3584]{2,1,0:T(8,128)(2,1)S(1)}, u32[]{:S(2)}, u32[]{:S(2)}) %collective-permute-start) | collective-permute-done | bytes 917536 | tf_op jit(solution)/shard_map/forward_experts/ppermute | solution.py:13
  726.5 6.1 collective-permute-done.1
  732.5 0.9 copy.109
  733.5 0.9 copy.110
  (60 shorter events, 2.2 us)
Async XLA Ops:
  7.2 71.7 %all-gather.4.cloned.1.call-start = ((), (), s32[]{:S(2)}) async-start(), calls=%async_computation.5 | async-start | bytes 4587520 | tf_op jit(solution)/shard_map/gather_along_z/all_gather | solution.py:124
  7.9 148.7 %all-gather.6.cloned.1.call-start = ((), (), s32[]{:S(2)}) async-start(), calls=%async_computation.6 | async-start | bytes 4587520 | tf_op jit(solution)/shard_map/gather_along_z/all_gather | solution.py:124
  8.6 227.5 %all-gather.8.cloned.1.call-start = ((), (), s32[]{:S(2)}) async-start(), calls=%async_computation.7 | async-start | bytes 4587520 | tf_op jit(solution)/shard_map/gather_along_z/all_gather | solution.py:124
  85.7 160.7 %all-to-all-start = ((bf16[4,192,3584]{2,1,0:T(8,128)(2,1)}), bf16[4,192,3584]{2,1,0:T(8,128)(2,1)}, u32[]{:S(2)}, u32[]{:S(2)}) async-start(bf16[4,192,3584]{2,1,0:T(8,128)(2,1)} %bitcast.112), calls=%async_computation | async-start | bytes 11010048 | tf_op jit(solution)/shard_map/backward_experts/all_to_all | solution.py:77
  236.1 5.5 copy-start
  246.5 130.0 %all-to-all-start.1 = ((bf16[4,1,2,192,3584]{4,3,2,1,0:T(8,128)(2,1)}), bf16[4,1,2,192,3584]{4,3,2,1,0:T(8,128)(2,1)}, u32[]{:S(2)}, u32[]{:S(2)}) async-start(bf16[4,1,2,192,3584]{4,3,2,1,0:T(8,128)(2,1)} %maximum_bitcast_fusion), calls=%async_computation.1 | async-start | bytes 22020096 | tf_op jit(solution)/shard_map/dispatch/all_to_all | solution.py:77
  385.4 7.1 copy-start.5
  392.6 3.3 copy-start.2
  395.9 3.2 copy-start.6
  407.2 126.1 %all-to-all-start.2 = ((bf16[4,1,2,192,3584]{4,3,2,1,0:T(8,128)(2,1)}), bf16[4,1,2,192,3584]{4,3,2,1,0:T(8,128)(2,1)}, u32[]{:S(2)}, u32[]{:S(2)}) async-start(bf16[4,1,2,192,3584]{4,3,2,1,0:T(8,128)(2,1)} %maximum_bitcast_fusion.1), calls=%async_computation.2 | async-start | bytes 22020096 | tf_op jit(solution)/shard_map/experts/all_to_all | solution.py:77
  415.7 300.4 %reduce-scatter.2.cloned.1.call-start = ((), (), s32[]{:S(2)}) async-start(), calls=%async_computation.8 | async-start | bytes 4587520 | tf_op jit(solution)/shard_map/backward_experts/reduce_scatter | solution.py:87
  542.3 5.3 copy-start.1
  552.4 5.4 slice-start
  552.5 5.4 slice-start.1
  561.3 152.2 %copy-start.3 = (bf16[1,128,3584]{2,1,0:T(8,128)(2,1)S(1)}, bf16[1,128,3584]{2,1,0:T(8,128)(2,1)}, u32[]{:S(2)}) copy-start(bf16[1,128,3584]{2,1,0:T(8,128)(2,1)} %param.9) | copy-start | bytes 2752516
  713.0 3.2 copy-start.4
  713.7 12.8 %collective-permute-start = (bf16[1,128,3584]{2,1,0:T(8,128)(2,1)S(1)}, bf16[1,128,3584]{2,1,0:T(8,128)(2,1)S(1)}, u32[]{:S(2)}, u32[]{:S(2)}) collective-permute-start(bf16[1,128,3584]{2,1,0:T(8,128)(2,1)S(1)} %fusion.10), channel_id=1, source_target_pairs={{0,16},{16,32},{32,48},{48,64},{64,80},{80,96},{96,112},{112,128},... | collective-permute-start | bytes 2752520 | tf_op jit(solution)/shard_map/forward_experts/ppermute | solution.py:13
  717.5 15.0 %collective-permute-start.1 = (bf16[1,128,3584]{2,1,0:T(8,128)(2,1)S(1)}, bf16[1,128,3584]{2,1,0:T(8,128)(2,1)S(1)}, u32[]{:S(2)}, u32[]{:S(2)}) collective-permute-start(bf16[1,128,3584]{2,1,0:T(8,128)(2,1)S(1)} %add_convert_fusion.2), channel_id=1, source_target_pairs={{0,240},{16,0},{32,16},{48,32},{64,48},{80,64},{96,80},{112,96},{1... | collective-permute-start | bytes 2752520 | tf_op jit(solution)/shard_map/backward_experts/ppermute | solution.py:13
Sparse Core Ops, SparseCore 0:
  9.8 68.9 all-gather.3
  80.6 75.9 all-gather.5
  158.4 77.6 all-gather.7
  552.6 148.2 reduce-scatter.1

commit v9 on v7

--- a/solution.py
+++ b/solution.py
@@ -5,7 +5,7 @@
 from jax.sharding import PartitionSpec as P
 
 Z_PARTS = 4
-D_PARTS = 2
+D_PARTS = 1
 
 
 def from_behind(value, axis, by):

time: 598 us -> 583 us (0.975)
  starting transfers between devices: 48.7 us -> 35.3 us
    all_to_all x6 -> x5, starting transfers between devices: 46.3 us -> 34.5 us  [swap_x(): got = lax.all_to_all(spread, 'ex', split_axis=0, concat_axis=0, tiled=True)]
    reduce_scatter x3 -> x2, waiting for transfers between devices: 98.9 us -> 88.3 us  [sum_back(): lax.psum_scatter(partial.astype(wire_type), 'ez', scatter_dimension=0, ti...]
    all_to_all x6 -> x5, waiting for transfers between devices: 134 us -> 144 us  [swap_x(): got = lax.all_to_all(spread, 'ex', split_axis=0, concat_axis=0, tiled=True)]
    dot_general x1, matrix products: 13.2 us -> 4.9 us  [backward_work(): lax.dot_general(hidden_grad, w_up, (((1,), (1,)), ((), ())), preferred_el...]
    dot_general x0 -> x1, matrix products: none -> 6.04 us  [backward_work(): lax.dot_general(grad_rows, w_down, (((1,), (1,)), ((), ())), preferred_el...]
    dot_general x6 -> x4, matrix products: 26 us -> 25.2 us  [weighted_partial(): picked = jnp.dot(table, results, preferred_element_type=jnp.float32)]
  transfers between devices with their start and end apart: 15 -> 12, of which waited for: 12 -> 9; matrix products, arithmetic and copies ran while one was open for 14% -> 13% of each run, Pallas kernels for 0% -> 0%
where the time goes in v9:
time: 583 us; the launch traced here: 574 us
  waiting for transfers between devices  420 us (72%)
  matrix products  74.9 us (13%)
  starting transfers between devices  35.3 us (6%)
  blocking collectives  14.4 us (2%)
  between operations  14 us (2%)
  other arithmetic  11.6 us (2%)
    all_gather x3, waiting for transfers between devices, gather_z(): return lax.all_gather(value[0], 'ez', axis=0, tiled=False)  176 us
    all_to_all x5, waiting for transfers between devices, swap_x(): got = lax.all_to_all(spread, 'ex', split_axis=0, concat_axis=0, tiled=True)  144 us
    reduce_scatter x2, waiting for transfers between devices, sum_back(): lax.psum_scatter(partial.astype(wire_type), 'ez', scatter_dimension=0, ti...  88.3 us
    all_to_all x5, starting transfers between devices, swap_x(): got = lax.all_to_all(spread, 'ex', split_axis=0, concat_axis=0, tiled=True)  34.5 us
    dot_general x4, matrix products, weighted_partial(): picked = jnp.dot(table, results, preferred_element_type=jnp.float32)  25.2 us
    dot_general x3, matrix products, pack_rows(): lax.dot_general(table, flat, (((0,), (0,)), ((), ())), preferred_element_...  20.7 us
    all_gather x1, blocking collectives, gather_z(): return lax.all_gather(value[0], 'ez', axis=0, tiled=False)  14.4 us
  transfers between devices with their start and end apart: 12, of which 9 were waited for; matrix products, arithmetic and copies ran while one was open for 13% of the time, Pallas kernels for 0%

profile of v9, /device:TPU:29, one launch (start us, length us, event | category | flops | bytes accessed | tf_op | source)
XLA Modules:
  0.0 574.4 jit_solution(3334537732931527836)
XLA Ops:
  7.2 0.7 all-gather.4.cloned.1.call-update
  7.9 0.7 all-gather.8.cloned.1.call-update
  8.7 0.7 convert_element_type.97
  9.3 0.7 convert_element_type.98
  10.0 0.7 pad_maximum_fusion
  10.7 14.4 %all_gather.12 = f32[4,128,8]{1,2,0:T(8,128)S(1)} all-gather(f32[1,128,8]{1,2,0:T(8,128)S(1)} %pad_maximum_fusion), channel_id=1, replica_groups=mesh['pp'=16,'ex'=4,'ez'=4] {'ez'}, dimensions={0}, use_global_device_ids=true | all-gather | bytes 20480 | tf_op jit(solution)/shard_map/gather_along_z/all_gather | solution.py:118
  25.2 0.2 copy.75
  25.6 2.3 reduce-window.14
  27.9 0.1 copy.78
  28.2 0.1 copy.80
  28.3 0.2 copy.82
  28.7 2.3 reduce-window.16
  31.3 0.1 copy.87
  31.5 1.2 compare_select_fusion
  32.7 0.4 fusion.10
  33.1 46.7 %all-gather.4.cloned.1.call-done = bf16[4,128,3584]{2,1,0:T(8,128)(2,1)} async-done(((bf16[1,128,3584]{2,1,0:T(8,128)(2,1)}), bf16[4,128,3584]{2,1,0:T(8,128)(2,1)}) %all-gather.4.cloned.1.call-update) | async-done | bytes 3670032 | tf_op jit(solution)/shard_map/gather_along_z/all_gather | solution.py:118
  79.8 6.9 %convolution_convert_fusion.2 = bf16[768,3584]{1,0:T(8,128)(2,1)} fusion(bf16[512,768]{1,0:T(8,128)(2,1)S(1)} %fusion.10, bf16[512,3584]{1,0:T(8,128)(2,1)} %bitcast.124), kind=kOutput, calls=%fused_computation.4 | convolution fusion | flops 2821324800 | bytes 9961472 | tf_op jit(solution)/shard_map/backward_experts/dot_general | solution.py:44
  86.8 5.4 all-to-all-start.2
  92.2 0.7 all-gather.6.cloned.1.call-update
  92.9 63.9 %all-gather.8.cloned.1.call-done = bf16[4,128,3584]{2,1,0:T(8,128)(2,1)} async-done(((bf16[1,128,3584]{2,1,0:T(8,128)(2,1)}), bf16[4,128,3584]{2,1,0:T(8,128)(2,1)}) %all-gather.8.cloned.1.call-update) | async-done | bytes 3670032 | tf_op jit(solution)/shard_map/gather_along_z/all_gather | solution.py:118
  156.8 6.8 %convolution_convert_fusion.3 = bf16[768,3584]{1,0:T(8,128)(2,1)} fusion(bf16[512,768]{1,0:T(8,128)(2,1)S(1)} %fusion.10, bf16[512,3584]{1,0:T(8,128)(2,1)} %bitcast.123), kind=kOutput, calls=%fused_computation.5 | convolution fusion | flops 2821324800 | bytes 9961472 | tf_op jit(solution)/shard_map/backward_experts/dot_general | solution.py:44
  163.6 7.3 %all-to-all-start.1 = ((bf16[4,192,3584]{2,1,0:T(8,128)(2,1)}), bf16[4,192,3584]{2,1,0:T(8,128)(2,1)}, u32[]{:S(2)}, u32[]{:S(2)}) async-start(bf16[4,192,3584]{2,1,0:T(8,128)(2,1)} %bitcast.99), calls=%async_computation.1 | async-start | bytes 11010048 | tf_op jit(solution)/shard_map/backward_experts/all_to_all | solution.py:77
  171.0 0.4 fusion.11
  171.4 65.3 %all-gather.6.cloned.1.call-done = bf16[4,128,3584]{2,1,0:T(8,128)(2,1)} async-done(((bf16[1,128,3584]{2,1,0:T(8,128)(2,1)}), bf16[4,128,3584]{2,1,0:T(8,128)(2,1)}) %all-gather.6.cloned.1.call-update) | async-done | bytes 3670032 | tf_op jit(solution)/shard_map/gather_along_z/all_gather | solution.py:118
  236.7 6.9 %convolution_convert_fusion.4 = bf16[768,3584]{1,0:T(8,128)(2,1)} fusion(bf16[512,768]{1,0:T(8,128)(2,1)S(1)} %fusion.11, bf16[512,3584]{1,0:T(8,128)(2,1)} %bitcast.125), kind=kOutput, calls=%fused_computation.6 | convolution fusion | flops 2821324800 | bytes 9961472 | tf_op jit(solution)/shard_map/forward_experts/dot_general | solution.py:44
  243.6 5.1 all-to-all-start
  248.7 6.2 %fusion.6 = f32[768,512]{1,0:T(8,128)S(1)} fusion(bf16[768,3584]{1,0:T(8,128)(2,1)} %bitcast.19, bf16[1,3584,512]{2,1,0:T(8,128)(2,1)} %param.16), kind=kOutput, calls=%fused_computation.13 | convolution fusion | flops 2818572288 | bytes 10747904 | tf_op jit(solution)/shard_map/backward_experts/dot_general | solution.py:67
  254.9 6.0 %multiply_convert_fusion.1 = bf16[768,512]{1,0:T(8,128)(2,1)S(1)} fusion(f32[768,512]{1,0:T(8,128)S(1)} %fusion.6, bf16[768,3584]{1,0:T(8,128)(2,1)} %bitcast.23, bf16[1,512,3584]{2,1,0:T(8,128)(2,1)S(1)} %copy-done.3), kind=kOutput, calls=%fused_computation.27 | convolution fusion | flops 2822111232 | bytes 11534336 | tf_op jit(solution)/shard_map/backward_experts/dot_general | solution.py:68
  261.0 4.9 convolution_convert_fusion.1
  265.9 40.7 %all-to-all-done = bf16[4,192,3584]{2,1,0:T(8,128)(2,1)} async-done(((bf16[4,192,3584]{2,1,0:T(8,128)(2,1)}), bf16[4,192,3584]{2,1,0:T(8,128)(2,1)}, u32[]{:S(2)}, u32[]{:S(2)}) %all-to-all-start) | async-done | bytes 5505056 | tf_op jit(solution)/shard_map/forward_experts/all_to_all | solution.py:77
  306.6 9.0 %all-to-all-start.3 = ((bf16[4,192,3584]{2,1,0:T(8,128)(2,1)}), bf16[4,192,3584]{2,1,0:T(8,128)(2,1)}, u32[]{:S(2)}, u32[]{:S(2)}) async-start(bf16[4,192,3584]{2,1,0:T(8,128)(2,1)} %bitcast.98), calls=%async_computation.3 | async-start | bytes 11010048 | tf_op jit(solution)/shard_map/backward_experts/all_to_all | solution.py:77
  315.9 7.0 %multiply_convert_fusion = bf16[768,512]{1,0:T(8,128)(2,1)S(1)} fusion(bf16[768,3584]{1,0:T(8,128)(2,1)} %bitcast.16, bf16[1,3584,512]{2,1,0:T(8,128)(2,1)} %param.16), kind=kOutput, calls=%fused_computation.25 | convolution fusion | flops 2820538368 | bytes 9961472 | tf_op jit(solution)/shard_map/forward_experts/dot_general | solution.py:62
  322.9 4.8 convolution_convert_fusion
  327.7 45.9 %all-to-all-done.3 = bf16[4,192,3584]{2,1,0:T(8,128)(2,1)} async-done(((bf16[4,192,3584]{2,1,0:T(8,128)(2,1)}), bf16[4,192,3584]{2,1,0:T(8,128)(2,1)}, u32[]{:S(2)}, u32[]{:S(2)}) %all-to-all-start.3) | async-done | bytes 5505056 | tf_op jit(solution)/shard_map/backward_experts/all_to_all | solution.py:77
  373.7 5.2 fusion.12
  378.9 7.4 %multiply_add_fusion.1 = bf16[512,3584]{1,0:T(8,128)(2,1)} fusion(f32[512,3584]{1,0:T(8,128)S(1)} %fusion.12, bf16[768,3584]{1,0:T(8,128)(2,1)} %bitcast.26, f32[512]{0:T(512)S(1)} %bitcast.121, f32[512]{0:T(512)S(1)} %bitcast.122, s32[512]{0:T(512)S(1)} %bitcast.115), kind=kOutput, calls=%fused_computation.1 | convolution fusion | flops 2826305536 | bytes 16521216 | tf_op jit(solution)/shard_map/backward_experts/dot_general | solution.py:55
  386.3 7.7 %all-to-all-start.4 = ((bf16[4,192,3584]{2,1,0:T(8,128)(2,1)}), bf16[4,192,3584]{2,1,0:T(8,128)(2,1)}, u32[]{:S(2)}, u32[]{:S(2)}) async-start(bf16[4,192,3584]{2,1,0:T(8,128)(2,1)} %bitcast.97), calls=%async_computation.5 | async-start | bytes 11010048 | tf_op jit(solution)/shard_map/forward_experts/all_to_all | solution.py:77
  394.3 57.0 %all-to-all-done.4 = bf16[4,192,3584]{2,1,0:T(8,128)(2,1)} async-done(((bf16[4,192,3584]{2,1,0:T(8,128)(2,1)}), bf16[4,192,3584]{2,1,0:T(8,128)(2,1)}, u32[]{:S(2)}, u32[]{:S(2)}) %all-to-all-start.4) | async-done | bytes 5505056 | tf_op jit(solution)/shard_map/forward_experts/all_to_all | solution.py:77
  451.2 5.2 fusion.13
  456.4 7.5 %multiply_add_fusion = bf16[512,3584]{1,0:T(8,128)(2,1)} fusion(f32[512,3584]{1,0:T(8,128)S(1)} %fusion.13, bf16[768,3584]{1,0:T(8,128)(2,1)} %bitcast.34, f32[512]{0:T(512)S(1)} %bitcast.120, f32[512]{0:T(512)S(1)} %bitcast.119, s32[512]{0:T(512)S(1)} %bitcast.117), kind=kOutput, calls=%fused_computation | convolution fusion | flops 2826305536 | bytes 16521216 | tf_op jit(solution)/shard_map/forward_experts/dot_general | solution.py:55
  463.9 11.0 %reduce-scatter.3.cloned.1.call-done = bf16[1,128,3584]{2,1,0:T(8,128)(2,1)} async-done(((bf16[4,128,3584]{2,1,0:T(8,128)(2,1)}), bf16[1,128,3584]{2,1,0:T(8,128)(2,1)}) %reduce-scatter.3.cloned.1.call-update) | async-done | bytes 917520 | tf_op jit(solution)/shard_map/backward_experts/reduce_scatter | solution.py:87
  474.9 1.4 fusion.18
  476.3 0.7 collective-permute-start.1
  477.0 77.3 %reduce-scatter.5.cloned.1.call-done = bf16[1,128,3584]{2,1,0:T(8,128)(2,1)} async-done(((bf16[4,128,3584]{2,1,0:T(8,128)(2,1)}), bf16[1,128,3584]{2,1,0:T(8,128)(2,1)}) %reduce-scatter.5.cloned.1.call-update) | async-done | bytes 917520 | tf_op jit(solution)/shard_map/forward_experts/reduce_scatter | solution.py:87
  554.2 1.4 add_convert_fusion
  555.7 10.3 %collective-permute-done = bf16[1,128,3584]{2,1,0:T(8,128)(2,1)S(1)} collective-permute-done((bf16[1,128,3584]{2,1,0:T(8,128)(2,1)S(1)}, bf16[1,128,3584]{2,1,0:T(8,128)(2,1)S(1)}, u32[]{:S(2)}, u32[]{:S(2)}) %collective-permute-start) | collective-permute-done | bytes 917536 | tf_op jit(solution)/shard_map/forward_experts/ppermute | solution.py:13
  566.1 0.9 copy.101
  567.0 0.9 copy.102
  (52 shorter events, 1.8 us)
Async XLA Ops:
  7.2 72.7 %all-gather.4.cloned.1.call-start = ((), (), s32[]{:S(2)}) async-start(), calls=%async_computation.7 | async-start | bytes 4587520 | tf_op jit(solution)/shard_map/gather_along_z/all_gather | solution.py:118
  7.9 148.9 %all-gather.8.cloned.1.call-start = ((), (), s32[]{:S(2)}) async-start(), calls=%async_computation.9 | async-start | bytes 4587520 | tf_op jit(solution)/shard_map/gather_along_z/all_gather | solution.py:118
  86.8 76.9 %all-to-all-start.2 = ((bf16[4,192,3584]{2,1,0:T(8,128)(2,1)}), bf16[4,192,3584]{2,1,0:T(8,128)(2,1)}, u32[]{:S(2)}, u32[]{:S(2)}) async-start(bf16[4,192,3584]{2,1,0:T(8,128)(2,1)} %bitcast.100), calls=%async_computation.2 | async-start | bytes 11010048 | tf_op jit(solution)/shard_map/backward_experts/all_to_all | solution.py:77
  92.2 144.5 %all-gather.6.cloned.1.call-start = ((), (), s32[]{:S(2)}) async-start(), calls=%async_computation.8 | async-start | bytes 4587520 | tf_op jit(solution)/shard_map/gather_along_z/all_gather | solution.py:118
  163.6 80.0 %all-to-all-start.1 = ((bf16[4,192,3584]{2,1,0:T(8,128)(2,1)}), bf16[4,192,3584]{2,1,0:T(8,128)(2,1)}, u32[]{:S(2)}, u32[]{:S(2)}) async-start(bf16[4,192,3584]{2,1,0:T(8,128)(2,1)} %bitcast.99), calls=%async_computation.1 | async-start | bytes 11010048 | tf_op jit(solution)/shard_map/backward_experts/all_to_all | solution.py:77
  243.6 63.0 %all-to-all-start = ((bf16[4,192,3584]{2,1,0:T(8,128)(2,1)}), bf16[4,192,3584]{2,1,0:T(8,128)(2,1)}, u32[]{:S(2)}, u32[]{:S(2)}) async-start(bf16[4,192,3584]{2,1,0:T(8,128)(2,1)} %bitcast.101), calls=%async_computation | async-start | bytes 11010048 | tf_op jit(solution)/shard_map/forward_experts/all_to_all | solution.py:77
  248.7 6.2 %copy-start.3 = (bf16[1,512,3584]{2,1,0:T(8,128)(2,1)S(1)}, bf16[1,512,3584]{2,1,0:T(8,128)(2,1)}, u32[]{:S(2)}) copy-start(bf16[1,512,3584]{2,1,0:T(8,128)(2,1)} %param.17) | copy-start | bytes 11010052
  254.9 6.1 %copy-start.2 = (bf16[1,3584,512]{2,1,0:T(8,128)(2,1)S(1)}, bf16[1,3584,512]{2,1,0:T(8,128)(2,1)}, u32[]{:S(2)}) copy-start(bf16[1,3584,512]{2,1,0:T(8,128)(2,1)} %param.16) | copy-start | bytes 11010052
  306.6 67.1 %all-to-all-start.3 = ((bf16[4,192,3584]{2,1,0:T(8,128)(2,1)}), bf16[4,192,3584]{2,1,0:T(8,128)(2,1)}, u32[]{:S(2)}, u32[]{:S(2)}) async-start(bf16[4,192,3584]{2,1,0:T(8,128)(2,1)} %bitcast.98), calls=%async_computation.3 | async-start | bytes 11010048 | tf_op jit(solution)/shard_map/backward_experts/all_to_all | solution.py:77
  315.6 159.3 %reduce-scatter.3.cloned.1.call-start = ((), (), s32[]{:S(2)}) async-start(), calls=%async_computation.10 | async-start | bytes 4587520 | tf_op jit(solution)/shard_map/backward_experts/reduce_scatter | solution.py:87
  315.9 7.0 %copy-start.4 = (bf16[1,512,3584]{2,1,0:T(8,128)(2,1)S(1)}, bf16[1,512,3584]{2,1,0:T(8,128)(2,1)}, u32[]{:S(2)}) copy-start(bf16[1,512,3584]{2,1,0:T(8,128)(2,1)} %param.17) | copy-start | bytes 11010052
  386.3 64.9 %all-to-all-start.4 = ((bf16[4,192,3584]{2,1,0:T(8,128)(2,1)}), bf16[4,192,3584]{2,1,0:T(8,128)(2,1)}, u32[]{:S(2)}, u32[]{:S(2)}) async-start(bf16[4,192,3584]{2,1,0:T(8,128)(2,1)} %bitcast.97), calls=%async_computation.5 | async-start | bytes 11010048 | tf_op jit(solution)/shard_map/forward_experts/all_to_all | solution.py:77
  394.0 160.2 %reduce-scatter.5.cloned.1.call-start = ((), (), s32[]{:S(2)}) async-start(), calls=%async_computation.11 | async-start | bytes 4587520 | tf_op jit(solution)/shard_map/forward_experts/reduce_scatter | solution.py:87
  456.4 18.5 %copy-start = (bf16[1,128,3584]{2,1,0:T(8,128)(2,1)S(1)}, bf16[1,128,3584]{2,1,0:T(8,128)(2,1)}, u32[]{:S(2)}) copy-start(bf16[1,128,3584]{2,1,0:T(8,128)(2,1)} %param.13) | copy-start | bytes 2752516
  463.9 90.4 %copy-start.1 = (bf16[1,128,3584]{2,1,0:T(8,128)(2,1)S(1)}, bf16[1,128,3584]{2,1,0:T(8,128)(2,1)}, u32[]{:S(2)}) copy-start(bf16[1,128,3584]{2,1,0:T(8,128)(2,1)} %param.9) | copy-start | bytes 2752516
  476.3 79.4 %collective-permute-start.1 = (bf16[1,128,3584]{2,1,0:T(8,128)(2,1)S(1)}, bf16[1,128,3584]{2,1,0:T(8,128)(2,1)S(1)}, u32[]{:S(2)}, u32[]{:S(2)}) collective-permute-start(bf16[1,128,3584]{2,1,0:T(8,128)(2,1)S(1)} %bitcast.108), channel_id=1, source_target_pairs={{0,240},{16,0},{32,16},{48,32},{64,48},{80,64},{96,80},{112,96},{1... | collective-permute-start | bytes 2752520 | tf_op jit(solution)/shard_map/forward_experts/ppermute | solution.py:13
  555.6 10.4 %collective-permute-start = (bf16[1,128,3584]{2,1,0:T(8,128)(2,1)S(1)}, bf16[1,128,3584]{2,1,0:T(8,128)(2,1)S(1)}, u32[]{:S(2)}, u32[]{:S(2)}) collective-permute-start(bf16[1,128,3584]{2,1,0:T(8,128)(2,1)S(1)} %add_convert_fusion), channel_id=1, source_target_pairs={{0,16},{16,32},{32,48},{48,64},{64,80},{80,96},{96,112},{112,128},... | collective-permute-start | bytes 2752520 | tf_op jit(solution)/shard_map/forward_experts/ppermute | solution.py:13
Sparse Core Ops, SparseCore 0:
  9.8 69.9 all-gather.3
  81.6 75.1 all-gather.7
  158.6 77.9 all-gather.5
  386.4 88.4 reduce-scatter.2
  477.3 76.9 reduce-scatter.4

commit v10 on v9

--- a/solution.py
+++ b/solution.py
@@ -148,20 +148,17 @@
         grad_rows = swap_x(pack_rows(bwd_grads_z, bwd_table), x_count)
         bwd_res = backward_work(bwd_rows, grad_rows, w_up, w_down)
 
+    with jax.named_scope("backward_experts"):
+        bwd_back = swap_x(bwd_res, x_count)
+        bwd_back, fwd_tok_z = lax.optimization_barrier((bwd_back, fwd_tok_z))
+        bwd_part = weighted_partial(bwd_back, bwd_slots, bwd_weights_z, slot_total)
+        bwd_out = sum_back(bwd_grads[0], bwd_part, z_index, jnp.bfloat16)
+
     with jax.named_scope("forward_experts"):
         fwd_table = slot_table(fwd_slots, slot_total)
         fwd_rows = swap_x(pack_rows(fwd_tok_z, fwd_table), x_count)
-        fwd_rows, bwd_res = lax.optimization_barrier((fwd_rows, bwd_res))
-
-    with jax.named_scope("forward_experts"):
         w_down_parts = [w_down[:, lo:hi] for lo, hi in cuts]
         fwd_res_parts = forward_work(fwd_rows, w_up, w_down_parts)
-
-    with jax.named_scope("backward_experts"):
-        bwd_back = swap_x(bwd_res, x_count)
-        bwd_part = weighted_partial(bwd_back, bwd_slots, bwd_weights_z, slot_total)
-        bwd_part, fwd_res_parts = lax.optimization_barrier((bwd_part, fwd_res_parts))
-        bwd_out = sum_back(bwd_grads[0], bwd_part, z_index, jnp.bfloat16)
 
     with jax.named_scope("forward_experts"):
         next_parts = []

time: 583 us -> 588 us (level)
  starting transfers between devices: 35.3 us -> 47.5 us
  waiting for transfers between devices: 420 us -> 412 us
    all_gather x3, waiting for transfers between devices: 176 us -> 109 us  [gather_z(): return lax.all_gather(value[0], 'ez', axis=0, tiled=False)]
    all_to_all x5, waiting for transfers between devices: 144 us -> 195 us  [swap_x(): got = lax.all_to_all(spread, 'ex', split_axis=0, concat_axis=0, tiled=True)]
    all_to_all x5, starting transfers between devices: 34.5 us -> 42.8 us  [swap_x(): got = lax.all_to_all(spread, 'ex', split_axis=0, concat_axis=0, tiled=True)]
    reduce_scatter x2, waiting for transfers between devices: 88.3 us -> 95.5 us  [sum_back(): lax.psum_scatter(partial.astype(wire_type), 'ez', scatter_dimension=0, ti...]
  transfers between devices with their start and end apart: 12 -> 12, of which waited for: 9 -> 9; matrix products, arithmetic and copies ran while one was open for 13% -> 12% of each run, Pallas kernels for 0% -> 0%
where the time goes in v10:
time: 588 us; the launch traced here: 579 us
  waiting for transfers between devices  412 us (70%)
  matrix products  75.8 us (13%)
  starting transfers between devices  47.5 us (8%)
  blocking collectives  14.4 us (2%)
  between operations  14 us (2%)
  other arithmetic  11.6 us (2%)
    all_to_all x5, waiting for transfers between devices, swap_x(): got = lax.all_to_all(spread, 'ex', split_axis=0, concat_axis=0, tiled=True)  195 us
    all_gather x3, waiting for transfers between devices, gather_z(): return lax.all_gather(value[0], 'ez', axis=0, tiled=False)  109 us
    reduce_scatter x2, waiting for transfers between devices, sum_back(): lax.psum_scatter(partial.astype(wire_type), 'ez', scatter_dimension=0, ti...  95.5 us
    all_to_all x5, starting transfers between devices, swap_x(): got = lax.all_to_all(spread, 'ex', split_axis=0, concat_axis=0, tiled=True)  42.8 us
    dot_general x4, matrix products, weighted_partial(): picked = jnp.dot(table, results, preferred_element_type=jnp.float32)  25.1 us
    dot_general x3, matrix products, pack_rows(): lax.dot_general(table, flat, (((0,), (0,)), ((), ())), preferred_element_...  20.6 us
    all_gather x1, blocking collectives, gather_z(): return lax.all_gather(value[0], 'ez', axis=0, tiled=False)  14.4 us
  transfers between devices with their start and end apart: 12, of which 9 were waited for; matrix products, arithmetic and copies ran while one was open for 12% of the time, Pallas kernels for 0%

profile of v10, /device:TPU:29, one launch (start us, length us, event | category | flops | bytes accessed | tf_op | source)
XLA Modules:
  0.0 579.0 jit_solution(10984260523878514946)
XLA Ops:
  7.2 0.7 all-gather.4.cloned.1.call-update
  7.9 0.7 all-gather.6.cloned.1.call-update
  8.7 0.7 convert_element_type.101
  9.3 0.7 convert_element_type.100
  10.0 0.7 pad_maximum_fusion
  10.7 14.4 %all_gather.12 = f32[4,128,8]{1,2,0:T(8,128)S(1)} all-gather(f32[1,128,8]{1,2,0:T(8,128)S(1)} %pad_maximum_fusion), channel_id=1, replica_groups=mesh['pp'=16,'ex'=4,'ez'=4] {'ez'}, dimensions={0}, use_global_device_ids=true | all-gather | bytes 20480 | tf_op jit(solution)/shard_map/gather_along_z/all_gather | solution.py:118
  25.2 0.2 copy.84
  25.5 2.3 reduce-window.16
  27.8 0.1 copy.87
  28.2 0.1 copy.89
  28.3 0.2 copy.75
  28.6 2.3 reduce-window.14
  31.3 0.1 copy.80
  31.5 1.2 compare_select_fusion
  32.7 0.4 fusion.11
  33.1 45.8 %all-gather.4.cloned.1.call-done = bf16[4,128,3584]{2,1,0:T(8,128)(2,1)} async-done(((bf16[1,128,3584]{2,1,0:T(8,128)(2,1)}), bf16[4,128,3584]{2,1,0:T(8,128)(2,1)}) %all-gather.4.cloned.1.call-update) | async-done | bytes 3670032 | tf_op jit(solution)/shard_map/gather_along_z/all_gather | solution.py:118
  78.9 6.8 %convolution_convert_fusion.4 = bf16[768,3584]{1,0:T(8,128)(2,1)} fusion(bf16[512,768]{1,0:T(8,128)(2,1)S(1)} %fusion.11, bf16[512,3584]{1,0:T(8,128)(2,1)} %bitcast.124), kind=kOutput, calls=%fused_computation.6 | convolution fusion | flops 2821324800 | bytes 9961472 | tf_op jit(solution)/shard_map/backward_experts/dot_general | solution.py:44
  85.7 9.6 %all-to-all-start = ((bf16[4,192,3584]{2,1,0:T(8,128)(2,1)}), bf16[4,192,3584]{2,1,0:T(8,128)(2,1)}, u32[]{:S(2)}, u32[]{:S(2)}) async-start(bf16[4,192,3584]{2,1,0:T(8,128)(2,1)} %bitcast.101), calls=%async_computation | async-start | bytes 11010048 | tf_op jit(solution)/shard_map/backward_experts/all_to_all | solution.py:77
  95.3 63.0 %all-gather.6.cloned.1.call-done = bf16[4,128,3584]{2,1,0:T(8,128)(2,1)} async-done(((bf16[1,128,3584]{2,1,0:T(8,128)(2,1)}), bf16[4,128,3584]{2,1,0:T(8,128)(2,1)}) %all-gather.6.cloned.1.call-update) | async-done | bytes 3670032 | tf_op jit(solution)/shard_map/gather_along_z/all_gather | solution.py:118
  158.3 6.9 %convolution_convert_fusion.3 = bf16[768,3584]{1,0:T(8,128)(2,1)} fusion(bf16[512,768]{1,0:T(8,128)(2,1)S(1)} %fusion.11, bf16[512,3584]{1,0:T(8,128)(2,1)} %bitcast.123), kind=kOutput, calls=%fused_computation.5 | convolution fusion | flops 2821324800 | bytes 9961472 | tf_op jit(solution)/shard_map/backward_experts/dot_general | solution.py:44
  165.2 10.3 %all-to-all-start.1 = ((bf16[4,192,3584]{2,1,0:T(8,128)(2,1)}), bf16[4,192,3584]{2,1,0:T(8,128)(2,1)}, u32[]{:S(2)}, u32[]{:S(2)}) async-start(bf16[4,192,3584]{2,1,0:T(8,128)(2,1)} %bitcast.100), calls=%async_computation.1 | async-start | bytes 11010048 | tf_op jit(solution)/shard_map/backward_experts/all_to_all | solution.py:77
  175.5 0.7 all-gather.8.cloned.1.call-update
  176.2 6.1 %fusion.6 = f32[768,512]{1,0:T(8,128)S(1)} fusion(bf16[768,3584]{1,0:T(8,128)(2,1)} %bitcast.10, bf16[1,3584,512]{2,1,0:T(8,128)(2,1)} %param.16), kind=kOutput, calls=%fused_computation.13 | convolution fusion | flops 2818572288 | bytes 10747904 | tf_op jit(solution)/shard_map/backward_experts/dot_general | solution.py:67
  182.3 52.9 %all-to-all-done.1 = bf16[4,192,3584]{2,1,0:T(8,128)(2,1)} async-done(((bf16[4,192,3584]{2,1,0:T(8,128)(2,1)}), bf16[4,192,3584]{2,1,0:T(8,128)(2,1)}, u32[]{:S(2)}, u32[]{:S(2)}) %all-to-all-start.1) | async-done | bytes 5505056 | tf_op jit(solution)/shard_map/backward_experts/all_to_all | solution.py:77
  235.1 7.2 %multiply_convert_fusion.1 = bf16[768,512]{1,0:T(8,128)(2,1)S(1)} fusion(f32[768,512]{1,0:T(8,128)S(1)} %fusion.6, bf16[768,3584]{1,0:T(8,128)(2,1)} %bitcast.14, bf16[1,512,3584]{2,1,0:T(8,128)(2,1)} %param.17), kind=kOutput, calls=%fused_computation.27 | convolution fusion | flops 2822111232 | bytes 11534336 | tf_op jit(solution)/shard_map/backward_experts/dot_general | solution.py:68
  242.3 4.9 convolution_convert_fusion.2
  247.2 7.6 %all-to-all-start.2 = ((bf16[4,192,3584]{2,1,0:T(8,128)(2,1)}), bf16[4,192,3584]{2,1,0:T(8,128)(2,1)}, u32[]{:S(2)}, u32[]{:S(2)}) async-start(bf16[4,192,3584]{2,1,0:T(8,128)(2,1)} %bitcast.97), calls=%async_computation.2 | async-start | bytes 11010048 | tf_op jit(solution)/shard_map/backward_experts/all_to_all | solution.py:77
  255.2 0.4 fusion.10
  255.6 58.1 %all-to-all-done.2 = bf16[4,192,3584]{2,1,0:T(8,128)(2,1)} async-done(((bf16[4,192,3584]{2,1,0:T(8,128)(2,1)}), bf16[4,192,3584]{2,1,0:T(8,128)(2,1)}, u32[]{:S(2)}, u32[]{:S(2)}) %all-to-all-start.2) | async-done | bytes 5505056 | tf_op jit(solution)/shard_map/backward_experts/all_to_all | solution.py:77
  313.7 6.9 %convolution_convert_fusion.1 = bf16[768,3584]{1,0:T(8,128)(2,1)} fusion(bf16[512,768]{1,0:T(8,128)(2,1)S(1)} %fusion.10, bf16[512,3584]{1,0:T(8,128)(2,1)} %bitcast.125), kind=kOutput, calls=%fused_computation.3 | convolution fusion | flops 2821324800 | bytes 9961472 | tf_op jit(solution)/shard_map/forward_experts/dot_general | solution.py:44
  320.6 7.6 %all-to-all-start.3 = ((bf16[4,192,3584]{2,1,0:T(8,128)(2,1)}), bf16[4,192,3584]{2,1,0:T(8,128)(2,1)}, u32[]{:S(2)}, u32[]{:S(2)}) async-start(bf16[4,192,3584]{2,1,0:T(8,128)(2,1)} %bitcast.98), calls=%async_computation.4 | async-start | bytes 11010048 | tf_op jit(solution)/shard_map/forward_experts/all_to_all | solution.py:77
  328.2 5.2 fusion.12
  333.3 7.4 %add_convert_fusion = bf16[512,3584]{1,0:T(8,128)(2,1)} fusion(f32[512,3584]{1,0:T(8,128)S(1)} %fusion.12, bf16[768,3584]{1,0:T(8,128)(2,1)} %bitcast.17, f32[512]{0:T(512)S(1)} %bitcast.121, f32[512]{0:T(512)S(1)} %bitcast.122, s32[512]{0:T(512)S(1)} %bitcast.116), kind=kOutput, calls=%fused_computation.1 | convolution fusion | flops 2826305536 | bytes 16521216 | tf_op jit(solution)/shard_map/backward_experts/dot_general | solution.py:55
  340.8 45.2 %all-to-all-done.3 = bf16[4,192,3584]{2,1,0:T(8,128)(2,1)} async-done(((bf16[4,192,3584]{2,1,0:T(8,128)(2,1)}), bf16[4,192,3584]{2,1,0:T(8,128)(2,1)}, u32[]{:S(2)}, u32[]{:S(2)}) %all-to-all-start.3) | async-done | bytes 5505056 | tf_op jit(solution)/shard_map/forward_experts/all_to_all | solution.py:77
  385.9 7.1 %multiply_convert_fusion = bf16[768,512]{1,0:T(8,128)(2,1)S(1)} fusion(bf16[768,3584]{1,0:T(8,128)(2,1)} %bitcast.32, bf16[1,3584,512]{2,1,0:T(8,128)(2,1)} %param.16), kind=kOutput, calls=%fused_computation.24 | convolution fusion | flops 2820538368 | bytes 9961472 | tf_op jit(solution)/shard_map/forward_experts/dot_general | solution.py:62
  393.0 4.8 convolution_convert_fusion
  397.8 7.8 %all-to-all-start.4 = ((bf16[4,192,3584]{2,1,0:T(8,128)(2,1)}), bf16[4,192,3584]{2,1,0:T(8,128)(2,1)}, u32[]{:S(2)}, u32[]{:S(2)}) async-start(bf16[4,192,3584]{2,1,0:T(8,128)(2,1)} %bitcast.99), calls=%async_computation.5 | async-start | bytes 11010048 | tf_op jit(solution)/shard_map/forward_experts/all_to_all | solution.py:77
  405.9 16.2 %reduce-scatter.3.cloned.1.call-done = bf16[1,128,3584]{2,1,0:T(8,128)(2,1)} async-done(((bf16[4,128,3584]{2,1,0:T(8,128)(2,1)}), bf16[1,128,3584]{2,1,0:T(8,128)(2,1)}) %reduce-scatter.3.cloned.1.call-update) | async-done | bytes 917520 | tf_op jit(solution)/shard_map/backward_experts/reduce_scatter | solution.py:87
  422.1 1.4 fusion.18
  423.4 38.9 %all-to-all-done.4 = bf16[4,192,3584]{2,1,0:T(8,128)(2,1)} async-done(((bf16[4,192,3584]{2,1,0:T(8,128)(2,1)}), bf16[4,192,3584]{2,1,0:T(8,128)(2,1)}, u32[]{:S(2)}, u32[]{:S(2)}) %all-to-all-start.4) | async-done | bytes 5505056 | tf_op jit(solution)/shard_map/forward_experts/all_to_all | solution.py:77
  462.4 5.2 fusion.13
  467.6 7.4 %multiply_add_fusion = bf16[512,3584]{1,0:T(8,128)(2,1)} fusion(f32[512,3584]{1,0:T(8,128)S(1)} %fusion.13, bf16[768,3584]{1,0:T(8,128)(2,1)} %bitcast.34, f32[512]{0:T(512)S(1)} %bitcast.120, f32[512]{0:T(512)S(1)} %bitcast.119, s32[512]{0:T(512)S(1)} %bitcast.117), kind=kOutput, calls=%fused_computation | convolution fusion | flops 2826305536 | bytes 16521216 | tf_op jit(solution)/shard_map/forward_experts/dot_general | solution.py:55
  475.0 4.5 collective-permute-start.1
  479.5 79.3 %reduce-scatter.5.cloned.1.call-done = bf16[1,128,3584]{2,1,0:T(8,128)(2,1)} async-done(((bf16[4,128,3584]{2,1,0:T(8,128)(2,1)}), bf16[1,128,3584]{2,1,0:T(8,128)(2,1)}) %reduce-scatter.5.cloned.1.call-update) | async-done | bytes 917520 | tf_op jit(solution)/shard_map/forward_experts/reduce_scatter | solution.py:87
  558.8 1.4 add_convert_fusion.1
  560.3 10.3 %collective-permute-done = bf16[1,128,3584]{2,1,0:T(8,128)(2,1)S(1)} collective-permute-done((bf16[1,128,3584]{2,1,0:T(8,128)(2,1)S(1)}, bf16[1,128,3584]{2,1,0:T(8,128)(2,1)S(1)}, u32[]{:S(2)}, u32[]{:S(2)}) %collective-permute-start) | collective-permute-done | bytes 917536 | tf_op jit(solution)/shard_map/forward_experts/ppermute | solution.py:13
  570.6 0.9 copy.101
  571.5 0.9 copy.102
  (50 shorter events, 1.9 us)
Async XLA Ops:
  7.2 71.7 %all-gather.4.cloned.1.call-start = ((), (), s32[]{:S(2)}) async-start(), calls=%async_computation.7 | async-start | bytes 4587520 | tf_op jit(solution)/shard_map/gather_along_z/all_gather | solution.py:118
  7.9 150.4 %all-gather.6.cloned.1.call-start = ((), (), s32[]{:S(2)}) async-start(), calls=%async_computation.8 | async-start | bytes 4587520 | tf_op jit(solution)/shard_map/gather_along_z/all_gather | solution.py:118
  85.7 79.5 %all-to-all-start = ((bf16[4,192,3584]{2,1,0:T(8,128)(2,1)}), bf16[4,192,3584]{2,1,0:T(8,128)(2,1)}, u32[]{:S(2)}, u32[]{:S(2)}) async-start(bf16[4,192,3584]{2,1,0:T(8,128)(2,1)} %bitcast.101), calls=%async_computation | async-start | bytes 11010048 | tf_op jit(solution)/shard_map/backward_experts/all_to_all | solution.py:77
  165.2 69.9 %all-to-all-start.1 = ((bf16[4,192,3584]{2,1,0:T(8,128)(2,1)}), bf16[4,192,3584]{2,1,0:T(8,128)(2,1)}, u32[]{:S(2)}, u32[]{:S(2)}) async-start(bf16[4,192,3584]{2,1,0:T(8,128)(2,1)} %bitcast.100), calls=%async_computation.1 | async-start | bytes 11010048 | tf_op jit(solution)/shard_map/backward_experts/all_to_all | solution.py:77
  175.5 80.1 %all-gather.8.cloned.1.call-start = ((), (), s32[]{:S(2)}) async-start(), calls=%async_computation.9 | async-start | bytes 4587520 | tf_op jit(solution)/shard_map/gather_along_z/all_gather | solution.py:118
  235.1 7.2 %copy-start.2 = (bf16[1,3584,512]{2,1,0:T(8,128)(2,1)S(1)}, bf16[1,3584,512]{2,1,0:T(8,128)(2,1)}, u32[]{:S(2)}) copy-start(bf16[1,3584,512]{2,1,0:T(8,128)(2,1)} %param.16) | copy-start | bytes 11010052
  247.2 66.5 %all-to-all-start.2 = ((bf16[4,192,3584]{2,1,0:T(8,128)(2,1)}), bf16[4,192,3584]{2,1,0:T(8,128)(2,1)}, u32[]{:S(2)}, u32[]{:S(2)}) async-start(bf16[4,192,3584]{2,1,0:T(8,128)(2,1)} %bitcast.97), calls=%async_computation.2 | async-start | bytes 11010048 | tf_op jit(solution)/shard_map/backward_experts/all_to_all | solution.py:77
  320.6 65.3 %all-to-all-start.3 = ((bf16[4,192,3584]{2,1,0:T(8,128)(2,1)}), bf16[4,192,3584]{2,1,0:T(8,128)(2,1)}, u32[]{:S(2)}, u32[]{:S(2)}) async-start(bf16[4,192,3584]{2,1,0:T(8,128)(2,1)} %bitcast.98), calls=%async_computation.4 | async-start | bytes 11010048 | tf_op jit(solution)/shard_map/forward_experts/all_to_all | solution.py:77
  328.1 93.9 %reduce-scatter.3.cloned.1.call-start = ((), (), s32[]{:S(2)}) async-start(), calls=%async_computation.10 | async-start | bytes 4587520 | tf_op jit(solution)/shard_map/backward_experts/reduce_scatter | solution.py:87
  385.9 7.1 %copy-start.3 = (bf16[1,512,3584]{2,1,0:T(8,128)(2,1)S(1)}, bf16[1,512,3584]{2,1,0:T(8,128)(2,1)}, u32[]{:S(2)}) copy-start(bf16[1,512,3584]{2,1,0:T(8,128)(2,1)} %param.17) | copy-start | bytes 11010052
  397.8 24.2 %copy-start = (bf16[1,128,3584]{2,1,0:T(8,128)(2,1)S(1)}, bf16[1,128,3584]{2,1,0:T(8,128)(2,1)}, u32[]{:S(2)}) copy-start(bf16[1,128,3584]{2,1,0:T(8,128)(2,1)} %param.13) | copy-start | bytes 2752516
  397.8 64.5 %all-to-all-start.4 = ((bf16[4,192,3584]{2,1,0:T(8,128)(2,1)}), bf16[4,192,3584]{2,1,0:T(8,128)(2,1)}, u32[]{:S(2)}, u32[]{:S(2)}) async-start(bf16[4,192,3584]{2,1,0:T(8,128)(2,1)} %bitcast.99), calls=%async_computation.5 | async-start | bytes 11010048 | tf_op jit(solution)/shard_map/forward_experts/all_to_all | solution.py:77
  405.6 153.2 %reduce-scatter.5.cloned.1.call-start = ((), (), s32[]{:S(2)}) async-start(), calls=%async_computation.11 | async-start | bytes 4587520 | tf_op jit(solution)/shard_map/forward_experts/reduce_scatter | solution.py:87
  475.0 83.8 %copy-start.1 = (bf16[1,128,3584]{2,1,0:T(8,128)(2,1)S(1)}, bf16[1,128,3584]{2,1,0:T(8,128)(2,1)}, u32[]{:S(2)}) copy-start(bf16[1,128,3584]{2,1,0:T(8,128)(2,1)} %param.9) | copy-start | bytes 2752516
  475.0 85.3 %collective-permute-start.1 = (bf16[1,128,3584]{2,1,0:T(8,128)(2,1)S(1)}, bf16[1,128,3584]{2,1,0:T(8,128)(2,1)S(1)}, u32[]{:S(2)}, u32[]{:S(2)}) collective-permute-start(bf16[1,128,3584]{2,1,0:T(8,128)(2,1)S(1)} %bitcast.108), channel_id=1, source_target_pairs={{0,240},{16,0},{32,16},{48,32},{64,48},{80,64},{96,80},{112,96},{1... | collective-permute-start | bytes 2752520 | tf_op jit(solution)/shard_map/forward_experts/ppermute | solution.py:13
  560.2 10.4 %collective-permute-start = (bf16[1,128,3584]{2,1,0:T(8,128)(2,1)S(1)}, bf16[1,128,3584]{2,1,0:T(8,128)(2,1)S(1)}, u32[]{:S(2)}, u32[]{:S(2)}) collective-permute-start(bf16[1,128,3584]{2,1,0:T(8,128)(2,1)S(1)} %add_convert_fusion.1), channel_id=1, source_target_pairs={{0,16},{16,32},{32,48},{48,64},{64,80},{80,96},{96,112},{112,128},... | collective-permute-start | bytes 2752520 | tf_op jit(solution)/shard_map/forward_experts/ppermute | solution.py:13
Sparse Core Ops, SparseCore 0:
  9.8 69.0 all-gather.3
  80.7 77.5 all-gather.5
  178.1 71.3 all-gather.7
  340.9 81.1 reduce-scatter.2
  475.1 83.6 reduce-scatter.4

commit v11 on v9

--- a/solution.py
+++ b/solution.py
@@ -113,6 +113,12 @@
     expert_class = z_index // (z_count // class_count)
     w_up = up_proj[0]
     w_down = down_proj[0]
+    fwd_w_up = from_behind(up_proj, "pp", 1)[0]
+    fwd_w_down = from_behind(down_proj, "pp", 1)[0]
+    fwd_tokens = from_behind(fwd_tokens, "pp", 1)
+    fwd_meta = from_behind(jnp.concatenate([fwd_routes.astype(jnp.float32), fwd_weights], axis=-1), "pp", 1)
+    fwd_routes = fwd_meta[:, :, 0 : fwd_routes.shape[2]].astype(jnp.int32)
+    fwd_weights = fwd_meta[:, :, fwd_routes.shape[2] :]
 
     def gather_z(value):
         return lax.all_gather(value[0], "ez", axis=0, tiled=False)
@@ -145,6 +151,7 @@
     with jax.named_scope("backward_experts"):
         bwd_table = slot_table(bwd_slots, slot_total)
         bwd_rows = swap_x(pack_rows(bwd_tok_z, bwd_table), x_count)
+        fwd_w_up, fwd_w_down, bwd_rows = lax.optimization_barrier((fwd_w_up, fwd_w_down, bwd_rows))
         grad_rows = swap_x(pack_rows(bwd_grads_z, bwd_table), x_count)
         bwd_res = backward_work(bwd_rows, grad_rows, w_up, w_down)
 
@@ -154,8 +161,8 @@
         fwd_rows, bwd_res = lax.optimization_barrier((fwd_rows, bwd_res))
 
     with jax.named_scope("forward_experts"):
-        w_down_parts = [w_down[:, lo:hi] for lo, hi in cuts]
-        fwd_res_parts = forward_work(fwd_rows, w_up, w_down_parts)
+        w_down_parts = [fwd_w_down[:, lo:hi] for lo, hi in cuts]
+        fwd_res_parts = forward_work(fwd_rows, fwd_w_up, w_down_parts)
 
     with jax.named_scope("backward_experts"):
         bwd_back = swap_x(bwd_res, x_count)
@@ -172,7 +179,7 @@
                 bwd_out, fwd_part = lax.optimization_barrier((bwd_out, fwd_part))
                 prev_grad = from_behind(bwd_out[None], "pp", -1)
             fwd_out = sum_back(fwd_tokens[0][:, lo:hi], fwd_part, z_index, jnp.bfloat16)
-            next_parts.append(from_behind(fwd_out[None], "pp", 1))
+            next_parts.append(fwd_out[None])
         next_input = jnp.concatenate(next_parts, axis=-1)
 
     return (next_input, prev_grad)

time: 583 us -> 588 us (level)
  starting transfers between devices: 35.3 us -> 45.4 us
  waiting for transfers between devices: 420 us -> 410 us
  blocking collectives: 14.4 us -> 21.3 us
    ppermute x2 -> x5, waiting for transfers between devices: 10.3 us -> 77.2 us  [from_behind(): lax.ppermute(value, axis, [(i, (i + by) % size) for i in range(size)])]
    reduce_scatter x2, waiting for transfers between devices: 88.3 us -> 43.7 us  [sum_back(): lax.psum_scatter(partial.astype(wire_type), 'ez', scatter_dimension=0, ti...]
    all_to_all x5, waiting for transfers between devices: 144 us -> 106 us  [swap_x(): got = lax.all_to_all(spread, 'ex', split_axis=0, concat_axis=0, tiled=True)]
    ppermute x2 -> x5, starting transfers between devices: 0.77 us -> 10.2 us  [from_behind(): lax.ppermute(value, axis, [(i, (i + by) % size) for i in range(size)])]
    dot_general x1, matrix products: 4.85 us -> 13.2 us  [forward_work(): jnp.dot(hidden, part, preferred_element_type=jnp.float32)]
    dot_general x1 -> x0, matrix products: 7.02 us -> none  [forward_work(): jnp.dot(rows, w_up, preferred_element_type=jnp.float32)]
    all_gather x1, blocking collectives: 14.4 us -> 21.3 us  [gather_z(): return lax.all_gather(value[0], 'ez', axis=0, tiled=False)]
  transfers between devices with their start and end apart: 12 -> 15, of which waited for: 9 -> 9; matrix products, arithmetic and copies ran while one was open for 13% -> 13% of each run, Pallas kernels for 0% -> 0%
where the time goes in v11:
time: 588 us; the launch traced here: 583 us
  waiting for transfers between devices  410 us (70%)
  matrix products  76.2 us (13%)
  starting transfers between devices  45.4 us (8%)
  blocking collectives  21.3 us (4%)
  between operations  14 us (2%)
  other arithmetic  13.3 us (2%)
    all_gather x3, waiting for transfers between devices, gather_z(): return lax.all_gather(value[0], 'ez', axis=0, tiled=False)  180 us
    all_to_all x5, waiting for transfers between devices, swap_x(): got = lax.all_to_all(spread, 'ex', split_axis=0, concat_axis=0, tiled=True)  106 us
    ppermute x5, waiting for transfers between devices, from_behind(): lax.ppermute(value, axis, [(i, (i + by) % size) for i in range(size)])  77.2 us
    reduce_scatter x2, waiting for transfers between devices, sum_back(): lax.psum_scatter(partial.astype(wire_type), 'ez', scatter_dimension=0, ti...  43.7 us
    all_to_all x5, starting transfers between devices, swap_x(): got = lax.all_to_all(spread, 'ex', split_axis=0, concat_axis=0, tiled=True)  35 us
    dot_general x4, matrix products, weighted_partial(): picked = jnp.dot(table, results, preferred_element_type=jnp.float32)  25.3 us
    all_gather x1, blocking collectives, gather_z(): return lax.all_gather(value[0], 'ez', axis=0, tiled=False)  21.3 us
    dot_general x3, matrix products, pack_rows(): lax.dot_general(table, flat, (((0,), (0,)), ((), ())), preferred_element_...  20.6 us
  transfers between devices with their start and end apart: 15, of which 9 were waited for; matrix products, arithmetic and copies ran while one was open for 13% of the time, Pallas kernels for 0%

profile of v11, /device:TPU:29, one launch (start us, length us, event | category | flops | bytes accessed | tf_op | source)
XLA Modules:
  0.0 582.8 jit_solution(11300197268548042379)
XLA Ops:
  7.2 0.7 all-gather.4.cloned.1.call-update
  7.9 0.7 all-gather.8.cloned.1.call-update
  8.6 0.7 convert_element_type.103
  9.3 0.7 pad_maximum_fusion.1
  10.0 1.9 collective-permute-start.1
  12.0 0.7 convert_element_type.106
  12.6 0.7 pad_maximum_fusion
  13.3 21.3 %all_gather.12 = f32[4,128,8]{1,2,0:T(8,128)S(1)} all-gather(f32[1,128,8]{1,2,0:T(8,128)S(1)} %pad_maximum_fusion), channel_id=1, replica_groups=mesh['pp'=16,'ex'=4,'ez'=4] {'ez'}, dimensions={0}, use_global_device_ids=true | all-gather | bytes 20480 | tf_op jit(solution)/shard_map/gather_along_z/all_gather | solution.py:124
  34.6 0.2 copy.75
  35.0 2.3 reduce-window.14
  37.5 0.2 copy.82
  37.9 0.1 copy.80
  38.2 2.3 reduce-window.16
  40.7 0.1 copy.87
  40.9 1.2 compare_select_fusion
  42.1 0.4 fusion.7
  42.5 42.1 %all-gather.4.cloned.1.call-done = bf16[4,128,3584]{2,1,0:T(8,128)(2,1)} async-done(((bf16[1,128,3584]{2,1,0:T(8,128)(2,1)}), bf16[4,128,3584]{2,1,0:T(8,128)(2,1)}) %all-gather.4.cloned.1.call-update) | async-done | bytes 3670032 | tf_op jit(solution)/shard_map/gather_along_z/all_gather | solution.py:124
  84.6 6.8 %convolution_convert_fusion.2 = bf16[768,3584]{1,0:T(8,128)(2,1)} fusion(bf16[512,768]{1,0:T(8,128)(2,1)S(1)} %fusion.7, bf16[512,3584]{1,0:T(8,128)(2,1)} %bitcast.121), kind=kOutput, calls=%fused_computation.4 | convolution fusion | flops 2821324800 | bytes 9961472 | tf_op jit(solution)/shard_map/backward_experts/dot_general | solution.py:44
  91.5 5.1 all-to-all-start.2
  96.6 0.7 all-gather.6.cloned.1.call-update
  97.3 59.4 %all-gather.8.cloned.1.call-done = bf16[4,128,3584]{2,1,0:T(8,128)(2,1)} async-done(((bf16[1,128,3584]{2,1,0:T(8,128)(2,1)}), bf16[4,128,3584]{2,1,0:T(8,128)(2,1)}) %all-gather.8.cloned.1.call-update) | async-done | bytes 3670032 | tf_op jit(solution)/shard_map/gather_along_z/all_gather | solution.py:124
  156.7 6.9 %convolution_convert_fusion.3 = bf16[768,3584]{1,0:T(8,128)(2,1)} fusion(bf16[512,768]{1,0:T(8,128)(2,1)S(1)} %fusion.7, bf16[512,3584]{1,0:T(8,128)(2,1)} %bitcast.120), kind=kOutput, calls=%fused_computation.5 | convolution fusion | flops 2821324800 | bytes 9961472 | tf_op jit(solution)/shard_map/backward_experts/dot_general | solution.py:44
  163.7 11.6 %all-to-all-start.1 = ((bf16[4,192,3584]{2,1,0:T(8,128)(2,1)}), bf16[4,192,3584]{2,1,0:T(8,128)(2,1)}, u32[]{:S(2)}, u32[]{:S(2)}) async-start(bf16[4,192,3584]{2,1,0:T(8,128)(2,1)} %bitcast.95), calls=%async_computation.1 | async-start | bytes 11010048 | tf_op jit(solution)/shard_map/backward_experts/all_to_all | solution.py:77
  175.3 6.7 %collective-permute-start.3 = (bf16[1,512,3584]{2,1,0:T(8,128)(2,1)}, bf16[1,512,3584]{2,1,0:T(8,128)(2,1)}, u32[]{:S(2)}, u32[]{:S(2)}) collective-permute-start(bf16[1,512,3584]{2,1,0:T(8,128)(2,1)} %param.17), channel_id=1, source_target_pairs={{0,16},{16,32},{32,48},{48,64},{64,80},{80,96},{96,112},{112,128},... | collective-permute-start | bytes 11010056 | tf_op jit(solution)/shard_map/ppermute | solution.py:13
  182.1 0.4 fusion.8
  182.5 78.8 %all-gather.6.cloned.1.call-done = bf16[4,128,3584]{2,1,0:T(8,128)(2,1)} async-done(((bf16[1,128,3584]{2,1,0:T(8,128)(2,1)}), bf16[4,128,3584]{2,1,0:T(8,128)(2,1)}) %all-gather.6.cloned.1.call-update) | async-done | bytes 3670032 | tf_op jit(solution)/shard_map/gather_along_z/all_gather | solution.py:124
  261.3 6.9 %convolution_convert_fusion.4 = bf16[768,3584]{1,0:T(8,128)(2,1)} fusion(bf16[512,768]{1,0:T(8,128)(2,1)S(1)} %fusion.8, bf16[512,3584]{1,0:T(8,128)(2,1)} %bitcast.122), kind=kOutput, calls=%fused_computation.6 | convolution fusion | flops 2821324800 | bytes 9961472 | tf_op jit(solution)/shard_map/forward_experts/dot_general | solution.py:44
  268.2 5.3 all-to-all-start
  273.5 7.5 %collective-permute-done.3 = bf16[1,512,3584]{2,1,0:T(8,128)(2,1)} collective-permute-done((bf16[1,512,3584]{2,1,0:T(8,128)(2,1)}, bf16[1,512,3584]{2,1,0:T(8,128)(2,1)}, u32[]{:S(2)}, u32[]{:S(2)}) %collective-permute-start.3) | collective-permute-done | bytes 3670048 | tf_op jit(solution)/shard_map/ppermute | solution.py:13
  281.1 39.3 %collective-permute-done.2 = bf16[1,3584,512]{2,1,0:T(8,128)(2,1)} collective-permute-done((bf16[1,3584,512]{2,1,0:T(8,128)(2,1)}, bf16[1,3584,512]{2,1,0:T(8,128)(2,1)}, u32[]{:S(2)}, u32[]{:S(2)}) %collective-permute-start.2) | collective-permute-done | bytes 3670048 | tf_op jit(solution)/shard_map/ppermute | solution.py:13
  320.4 6.3 %fusion = f32[768,512]{1,0:T(8,128)S(1)} fusion(bf16[768,3584]{1,0:T(8,128)(2,1)} %bitcast.25, bf16[1,512,3584]{2,1,0:T(8,128)(2,1)} %param.17), kind=kOutput, calls=%fused_computation.7 | convolution fusion | flops 2818572288 | bytes 10747904 | tf_op jit(solution)/shard_map/backward_experts/dot_general | solution.py:68
  326.7 5.9 %multiply_convert_fusion.1 = bf16[768,512]{1,0:T(8,128)(2,1)S(1)} fusion(f32[768,512]{1,0:T(8,128)S(1)} %fusion, bf16[768,3584]{1,0:T(8,128)(2,1)} %bitcast.21, bf16[1,3584,512]{2,1,0:T(8,128)(2,1)S(1)} %copy-done.3), kind=kOutput, calls=%fused_computation.24 | convolution fusion | flops 2822111232 | bytes 11534336 | tf_op jit(solution)/shard_map/backward_experts/dot_general | solution.py:67
  332.6 4.9 convolution_convert_fusion.1
  337.5 5.1 all-to-all-start.3
  342.9 13.2 %convolution_convert_fusion = bf16[768,3584]{1,0:T(8,128)(2,1)} fusion(bf16[512,3584]{1,0:T(8,128)(2,1)} %bitcast.18, bf16[768,3584]{1,0:T(8,128)(2,1)} %bitcast.16, bf16[3584,512]{1,0:T(8,128)(2,1)} %bitcast.17), kind=kOutput, calls=%fused_computation.2 | convolution fusion | flops 5641863168 | bytes 18350080 | tf_op jit(solution)/shard_map/forward_experts/dot_general | solution.py:63
  356.1 46.9 %all-to-all-done.3 = bf16[4,192,3584]{2,1,0:T(8,128)(2,1)} async-done(((bf16[4,192,3584]{2,1,0:T(8,128)(2,1)}), bf16[4,192,3584]{2,1,0:T(8,128)(2,1)}, u32[]{:S(2)}, u32[]{:S(2)}) %all-to-all-start.3) | async-done | bytes 5505056 | tf_op jit(solution)/shard_map/backward_experts/all_to_all | solution.py:77
  402.9 5.2 fusion.9
  408.1 7.4 %multiply_add_fusion.1 = bf16[512,3584]{1,0:T(8,128)(2,1)} fusion(f32[512,3584]{1,0:T(8,128)S(1)} %fusion.9, bf16[768,3584]{1,0:T(8,128)(2,1)} %bitcast.28, f32[512]{0:T(512)S(1)} %bitcast.118, f32[512]{0:T(512)S(1)} %bitcast.119, s32[512]{0:T(512)S(1)} %bitcast.112), kind=kOutput, calls=%fused_computation.1 | convolution fusion | flops 2826305536 | bytes 16521216 | tf_op jit(solution)/shard_map/backward_experts/dot_general | solution.py:55
  415.5 7.9 %all-to-all-start.4 = ((bf16[4,192,3584]{2,1,0:T(8,128)(2,1)}), bf16[4,192,3584]{2,1,0:T(8,128)(2,1)}, u32[]{:S(2)}, u32[]{:S(2)}) async-start(bf16[4,192,3584]{2,1,0:T(8,128)(2,1)} %bitcast.94), calls=%async_computation.5 | async-start | bytes 11010048 | tf_op jit(solution)/shard_map/forward_experts/all_to_all | solution.py:77
  423.7 59.6 %all-to-all-done.4 = bf16[4,192,3584]{2,1,0:T(8,128)(2,1)} async-done(((bf16[4,192,3584]{2,1,0:T(8,128)(2,1)}), bf16[4,192,3584]{2,1,0:T(8,128)(2,1)}, u32[]{:S(2)}, u32[]{:S(2)}) %all-to-all-start.4) | async-done | bytes 5505056 | tf_op jit(solution)/shard_map/forward_experts/all_to_all | solution.py:77
  483.3 5.2 fusion.10
  488.5 7.6 %multiply_add_fusion = bf16[512,3584]{1,0:T(8,128)(2,1)} fusion(f32[512,3584]{1,0:T(8,128)S(1)} %fusion.10, bf16[768,3584]{1,0:T(8,128)(2,1)} %bitcast.36, f32[512]{0:T(512)S(1)} %bitcast.117, f32[512]{0:T(512)S(1)} %bitcast.116, s32[512]{0:T(512)S(1)} %bitcast.114), kind=kOutput, calls=%fused_computation | convolution fusion | flops 2826305536 | bytes 16521216 | tf_op jit(solution)/shard_map/forward_experts/dot_general | solution.py:55
  496.0 1.5 fusion.13
  497.5 1.5 collective-permute-start.4
  499.1 30.3 %collective-permute-done.4 = bf16[1,128,3584]{2,1,0:T(8,128)(2,1)S(1)} collective-permute-done((bf16[1,128,3584]{2,1,0:T(8,128)(2,1)S(1)}, bf16[1,128,3584]{2,1,0:T(8,128)(2,1)S(1)}, u32[]{:S(2)}, u32[]{:S(2)}) %collective-permute-start.4) | collective-permute-done | bytes 917536 | tf_op jit(solution)/shard_map/forward_experts/ppermute | solution.py:13
  529.4 43.7 %reduce-scatter.5.cloned.1.call-done = bf16[1,128,3584]{2,1,0:T(8,128)(2,1)} async-done(((bf16[4,128,3584]{2,1,0:T(8,128)(2,1)}), bf16[1,128,3584]{2,1,0:T(8,128)(2,1)}) %reduce-scatter.5.cloned.1.call-update) | async-done | bytes 917520 | tf_op jit(solution)/shard_map/forward_experts/reduce_scatter | solution.py:87
  573.0 2.3 add_convert_fusion
  575.3 0.9 copy.100
  (56 shorter events, 2.1 us)
Async XLA Ops:
  7.2 77.5 %all-gather.4.cloned.1.call-start = ((), (), s32[]{:S(2)}) async-start(), calls=%async_computation.7 | async-start | bytes 4587520 | tf_op jit(solution)/shard_map/gather_along_z/all_gather | solution.py:124
  7.9 148.8 %all-gather.8.cloned.1.call-start = ((), (), s32[]{:S(2)}) async-start(), calls=%async_computation.9 | async-start | bytes 4587520 | tf_op jit(solution)/shard_map/gather_along_z/all_gather | solution.py:124
  10.0 2.6 collective-permute-start.1
  11.9 30.6 %collective-permute-start = (bf16[1,128,3584]{2,1,0:T(8,128)(2,1)}, bf16[1,128,3584]{2,1,0:T(8,128)(2,1)S(1)}, u32[]{:S(2)}, u32[]{:S(2)}) collective-permute-start(bf16[1,128,3584]{2,1,0:T(8,128)(2,1)} %param.9), channel_id=1, source_target_pairs={{0,16},{16,32},{32,48},{48,64},{64,80},{80,96},{96,112},{112,128},... | collective-permute-start | bytes 2752520 | tf_op jit(solution)/shard_map/ppermute | solution.py:13
  42.5 49.0 %copy-start.1 = (bf16[1,128,3584]{2,1,0:T(8,128)(2,1)}, bf16[1,128,3584]{2,1,0:T(8,128)(2,1)S(1)}, u32[]{:S(2)}) copy-start(bf16[1,128,3584]{2,1,0:T(8,128)(2,1)S(1)} %collective-permute-done) | copy-start | bytes 2752516
  91.5 72.2 %all-to-all-start.2 = ((bf16[4,192,3584]{2,1,0:T(8,128)(2,1)}), bf16[4,192,3584]{2,1,0:T(8,128)(2,1)}, u32[]{:S(2)}, u32[]{:S(2)}) async-start(bf16[4,192,3584]{2,1,0:T(8,128)(2,1)} %bitcast.98), calls=%async_computation.2 | async-start | bytes 11010048 | tf_op jit(solution)/shard_map/backward_experts/all_to_all | solution.py:77
  96.6 164.7 %all-gather.6.cloned.1.call-start = ((), (), s32[]{:S(2)}) async-start(), calls=%async_computation.8 | async-start | bytes 4587520 | tf_op jit(solution)/shard_map/gather_along_z/all_gather | solution.py:124
  163.7 104.5 %all-to-all-start.1 = ((bf16[4,192,3584]{2,1,0:T(8,128)(2,1)}), bf16[4,192,3584]{2,1,0:T(8,128)(2,1)}, u32[]{:S(2)}, u32[]{:S(2)}) async-start(bf16[4,192,3584]{2,1,0:T(8,128)(2,1)} %bitcast.95), calls=%async_computation.1 | async-start | bytes 11010048 | tf_op jit(solution)/shard_map/backward_experts/all_to_all | solution.py:77
  175.3 105.8 %collective-permute-start.3 = (bf16[1,512,3584]{2,1,0:T(8,128)(2,1)}, bf16[1,512,3584]{2,1,0:T(8,128)(2,1)}, u32[]{:S(2)}, u32[]{:S(2)}) collective-permute-start(bf16[1,512,3584]{2,1,0:T(8,128)(2,1)} %param.17), channel_id=1, source_target_pairs={{0,16},{16,32},{32,48},{48,64},{64,80},{80,96},{96,112},{112,128},... | collective-permute-start | bytes 11010056 | tf_op jit(solution)/shard_map/ppermute | solution.py:13
  182.0 138.4 %collective-permute-start.2 = (bf16[1,3584,512]{2,1,0:T(8,128)(2,1)}, bf16[1,3584,512]{2,1,0:T(8,128)(2,1)}, u32[]{:S(2)}, u32[]{:S(2)}) collective-permute-start(bf16[1,3584,512]{2,1,0:T(8,128)(2,1)} %param.16), channel_id=1, source_target_pairs={{0,16},{16,32},{32,48},{48,64},{64,80},{80,96},{96,112},{112,128},... | collective-permute-start | bytes 11010056 | tf_op jit(solution)/shard_map/ppermute | solution.py:13
  268.2 69.3 %all-to-all-start = ((bf16[4,192,3584]{2,1,0:T(8,128)(2,1)}), bf16[4,192,3584]{2,1,0:T(8,128)(2,1)}, u32[]{:S(2)}, u32[]{:S(2)}) async-start(bf16[4,192,3584]{2,1,0:T(8,128)(2,1)} %bitcast.97), calls=%async_computation | async-start | bytes 11010048 | tf_op jit(solution)/shard_map/forward_experts/all_to_all | solution.py:77
  320.4 6.3 %copy-start.3 = (bf16[1,3584,512]{2,1,0:T(8,128)(2,1)S(1)}, bf16[1,3584,512]{2,1,0:T(8,128)(2,1)}, u32[]{:S(2)}) copy-start(bf16[1,3584,512]{2,1,0:T(8,128)(2,1)} %param.16) | copy-start | bytes 11010052
  337.5 65.5 %all-to-all-start.3 = ((bf16[4,192,3584]{2,1,0:T(8,128)(2,1)}), bf16[4,192,3584]{2,1,0:T(8,128)(2,1)}, u32[]{:S(2)}, u32[]{:S(2)}) async-start(bf16[4,192,3584]{2,1,0:T(8,128)(2,1)} %bitcast.96), calls=%async_computation.3 | async-start | bytes 11010048 | tf_op jit(solution)/shard_map/backward_experts/all_to_all | solution.py:77
  342.6 153.5 %reduce-scatter.3.cloned.1.call-start = ((), (), s32[]{:S(2)}) async-start(), calls=%async_computation.10 | async-start | bytes 4587520 | tf_op jit(solution)/shard_map/backward_experts/reduce_scatter | solution.py:87
  415.5 67.7 %all-to-all-start.4 = ((bf16[4,192,3584]{2,1,0:T(8,128)(2,1)}), bf16[4,192,3584]{2,1,0:T(8,128)(2,1)}, u32[]{:S(2)}, u32[]{:S(2)}) async-start(bf16[4,192,3584]{2,1,0:T(8,128)(2,1)} %bitcast.94), calls=%async_computation.5 | async-start | bytes 11010048 | tf_op jit(solution)/shard_map/forward_experts/all_to_all | solution.py:77
  423.5 149.6 %reduce-scatter.5.cloned.1.call-start = ((), (), s32[]{:S(2)}) async-start(), calls=%async_computation.11 | async-start | bytes 4587520 | tf_op jit(solution)/shard_map/forward_experts/reduce_scatter | solution.py:87
  488.5 7.6 %copy-start = (bf16[1,128,3584]{2,1,0:T(8,128)(2,1)S(1)}, bf16[1,128,3584]{2,1,0:T(8,128)(2,1)}, u32[]{:S(2)}) copy-start(bf16[1,128,3584]{2,1,0:T(8,128)(2,1)} %param.13) | copy-start | bytes 2752516
  496.0 77.0 %copy-start.2 = (bf16[1,128,3584]{2,1,0:T(8,128)(2,1)S(1)}, bf16[1,128,3584]{2,1,0:T(8,128)(2,1)}, u32[]{:S(2)}) copy-start(bf16[1,128,3584]{2,1,0:T(8,128)(2,1)} %copy-done.1) | copy-start | bytes 2752516
  497.5 31.8 %collective-permute-start.4 = (bf16[1,128,3584]{2,1,0:T(8,128)(2,1)S(1)}, bf16[1,128,3584]{2,1,0:T(8,128)(2,1)S(1)}, u32[]{:S(2)}, u32[]{:S(2)}) collective-permute-start(bf16[1,128,3584]{2,1,0:T(8,128)(2,1)S(1)} %bitcast.105), channel_id=1, source_target_pairs={{0,240},{16,0},{32,16},{48,32},{64,48},{80,64},{96,80},{112,96},{1... | collective-permute-start | bytes 2752520 | tf_op jit(solution)/shard_map/forward_experts/ppermute | solution.py:13
Sparse Core Ops, SparseCore 0:
  9.8 74.7 all-gather.3
  86.4 70.2 all-gather.7
  159.1 102.1 all-gather.5
  415.7 74.4 reduce-scatter.2
  497.7 75.3 reduce-scatter.4

commit v12 on v11

--- a/solution.py
+++ b/solution.py
@@ -151,7 +151,7 @@
     with jax.named_scope("backward_experts"):
         bwd_table = slot_table(bwd_slots, slot_total)
         bwd_rows = swap_x(pack_rows(bwd_tok_z, bwd_table), x_count)
-        fwd_w_up, fwd_w_down, bwd_rows = lax.optimization_barrier((fwd_w_up, fwd_w_down, bwd_rows))
+        fwd_w_up, fwd_w_down, bwd_grads_z = lax.optimization_barrier((fwd_w_up, fwd_w_down, bwd_grads_z))
         grad_rows = swap_x(pack_rows(bwd_grads_z, bwd_table), x_count)
         bwd_res = backward_work(bwd_rows, grad_rows, w_up, w_down)
 

time: 588 us -> 650 us (1.11)
  waiting for transfers between devices: 410 us -> 478 us
    all_gather x3, waiting for transfers between devices: 180 us -> 29 us  [gather_z(): return lax.all_gather(value[0], 'ez', axis=0, tiled=False)]
    ppermute x5, waiting for transfers between devices: 77.2 us -> 211 us  [from_behind(): lax.ppermute(value, axis, [(i, (i + by) % size) for i in range(size)])]
    all_to_all x5, waiting for transfers between devices: 106 us -> 169 us  [swap_x(): got = lax.all_to_all(spread, 'ex', split_axis=0, concat_axis=0, tiled=True)]
    reduce_scatter x2, waiting for transfers between devices: 43.7 us -> 67.3 us  [sum_back(): lax.psum_scatter(partial.astype(wire_type), 'ez', scatter_dimension=0, ti...]
  transfers between devices with their start and end apart: 15 -> 15, of which waited for: 9 -> 9; matrix products, arithmetic and copies ran while one was open for 13% -> 12% of each run, Pallas kernels for 0% -> 0%
where the time goes in v12:
time: 650 us; the launch traced here: 647 us
  waiting for transfers between devices  478 us (74%)
  matrix products  76.5 us (12%)
  starting transfers between devices  42.9 us (7%)
  blocking collectives  20.3 us (3%)
  between operations  14 us (2%)
  other arithmetic  13.2 us (2%)
    ppermute x5, waiting for transfers between devices, from_behind(): lax.ppermute(value, axis, [(i, (i + by) % size) for i in range(size)])  211 us
    all_to_all x5, waiting for transfers between devices, swap_x(): got = lax.all_to_all(spread, 'ex', split_axis=0, concat_axis=0, tiled=True)  169 us
    reduce_scatter x2, waiting for transfers between devices, sum_back(): lax.psum_scatter(partial.astype(wire_type), 'ez', scatter_dimension=0, ti...  67.3 us
    all_to_all x5, starting transfers between devices, swap_x(): got = lax.all_to_all(spread, 'ex', split_axis=0, concat_axis=0, tiled=True)  38.4 us
    all_gather x3, waiting for transfers between devices, gather_z(): return lax.all_gather(value[0], 'ez', axis=0, tiled=False)  29 us
    dot_general x4, matrix products, weighted_partial(): picked = jnp.dot(table, results, preferred_element_type=jnp.float32)  25.3 us
    dot_general x3, matrix products, pack_rows(): lax.dot_general(table, flat, (((0,), (0,)), ((), ())), preferred_element_...  20.9 us
    all_gather x1, blocking collectives, gather_z(): return lax.all_gather(value[0], 'ez', axis=0, tiled=False)  20.3 us
  transfers between devices with their start and end apart: 15, of which 9 were waited for; matrix products, arithmetic and copies ran while one was open for 12% of the time, Pallas kernels for 0%

profile of v12, /device:TPU:29, one launch (start us, length us, event | category | flops | bytes accessed | tf_op | source)
XLA Modules:
  0.0 647.3 jit_solution(15950975539050097824)
XLA Ops:
  7.2 0.7 all-gather.4.cloned.1.call-update
  7.9 1.9 collective-permute-start.2
  10.0 0.7 convert_element_type.103
  10.7 0.7 pad_maximum_fusion.1
  11.4 1.6 collective-permute-start.1
  13.1 0.7 convert_element_type.106
  13.7 193.7 %collective-permute-done.1 = f32[1,128,4]{1,2,0:T(4,128)S(1)} collective-permute-done((f32[1,128,4]{1,2,0:T(4,128)S(1)}, f32[1,128,4]{1,2,0:T(4,128)S(1)}, u32[]{:S(2)}, u32[]{:S(2)}) %collective-permute-start.1) | collective-permute-done | bytes 2080 | tf_op jit(solution)/shard_map/ppermute | solution.py:13
  207.5 0.7 pad_maximum_fusion
  208.1 20.3 %all_gather.12 = f32[4,128,8]{1,2,0:T(8,128)S(1)} all-gather(f32[1,128,8]{1,2,0:T(8,128)S(1)} %pad_maximum_fusion), channel_id=1, replica_groups=mesh['pp'=16,'ex'=4,'ez'=4] {'ez'}, dimensions={0}, use_global_device_ids=true | all-gather | bytes 20480 | tf_op jit(solution)/shard_map/gather_along_z/all_gather | solution.py:124
  228.5 0.2 copy.75
  228.8 2.3 reduce-window.14
  231.3 0.2 copy.82
  231.8 0.1 copy.80
  231.9 2.3 reduce-window.16
  234.3 0.1 copy.85
  234.6 0.1 copy.87
  234.7 1.2 compare_select_fusion
  236.0 0.4 fusion.7
  236.4 7.1 %convolution_convert_fusion.2 = bf16[768,3584]{1,0:T(8,128)(2,1)} fusion(bf16[512,768]{1,0:T(8,128)(2,1)S(1)} %fusion.7, bf16[512,3584]{1,0:T(8,128)(2,1)} %bitcast.121), kind=kOutput, calls=%fused_computation.4 | convolution fusion | flops 2821324800 | bytes 9961472 | tf_op jit(solution)/shard_map/backward_experts/dot_general | solution.py:44
  243.5 5.3 all-to-all-start.2
  248.8 0.7 all-gather.6.cloned.1.call-update
  249.6 6.9 %convolution_convert_fusion.3 = bf16[768,3584]{1,0:T(8,128)(2,1)} fusion(bf16[512,768]{1,0:T(8,128)(2,1)S(1)} %fusion.7, bf16[512,3584]{1,0:T(8,128)(2,1)} %bitcast.120), kind=kOutput, calls=%fused_computation.5 | convolution fusion | flops 2821324800 | bytes 9961472 | tf_op jit(solution)/shard_map/backward_experts/dot_general | solution.py:44
  256.5 23.6 %all-to-all-done.2 = bf16[4,192,3584]{2,1,0:T(8,128)(2,1)} async-done(((bf16[4,192,3584]{2,1,0:T(8,128)(2,1)}), bf16[4,192,3584]{2,1,0:T(8,128)(2,1)}, u32[]{:S(2)}, u32[]{:S(2)}) %all-to-all-start.2) | async-done | bytes 5505056 | tf_op jit(solution)/shard_map/backward_experts/all_to_all | solution.py:77
  280.2 7.7 %all-to-all-start.1 = ((bf16[4,192,3584]{2,1,0:T(8,128)(2,1)}), bf16[4,192,3584]{2,1,0:T(8,128)(2,1)}, u32[]{:S(2)}, u32[]{:S(2)}) async-start(bf16[4,192,3584]{2,1,0:T(8,128)(2,1)} %bitcast.96), calls=%async_computation.1 | async-start | bytes 11010048 | tf_op jit(solution)/shard_map/backward_experts/all_to_all | solution.py:77
  288.0 0.4 fusion.8
  288.4 28.9 %all-gather.6.cloned.1.call-done = bf16[4,128,3584]{2,1,0:T(8,128)(2,1)} async-done(((bf16[1,128,3584]{2,1,0:T(8,128)(2,1)}), bf16[4,128,3584]{2,1,0:T(8,128)(2,1)}) %all-gather.6.cloned.1.call-update) | async-done | bytes 3670032 | tf_op jit(solution)/shard_map/gather_along_z/all_gather | solution.py:124
  317.3 6.8 %convolution_convert_fusion.4 = bf16[768,3584]{1,0:T(8,128)(2,1)} fusion(bf16[512,768]{1,0:T(8,128)(2,1)S(1)} %fusion.8, bf16[512,3584]{1,0:T(8,128)(2,1)} %bitcast.122), kind=kOutput, calls=%fused_computation.6 | convolution fusion | flops 2821324800 | bytes 9961472 | tf_op jit(solution)/shard_map/forward_experts/dot_general | solution.py:44
  324.1 10.2 %all-to-all-start = ((bf16[4,192,3584]{2,1,0:T(8,128)(2,1)}), bf16[4,192,3584]{2,1,0:T(8,128)(2,1)}, u32[]{:S(2)}, u32[]{:S(2)}) async-start(bf16[4,192,3584]{2,1,0:T(8,128)(2,1)} %bitcast.98), calls=%async_computation | async-start | bytes 11010048 | tf_op jit(solution)/shard_map/forward_experts/all_to_all | solution.py:77
  334.4 6.2 fusion.3
  340.6 6.0 multiply_convert_fusion.1
  346.6 4.9 convolution_convert_fusion.1
  351.5 42.7 %all-to-all-done = bf16[4,192,3584]{2,1,0:T(8,128)(2,1)} async-done(((bf16[4,192,3584]{2,1,0:T(8,128)(2,1)}), bf16[4,192,3584]{2,1,0:T(8,128)(2,1)}, u32[]{:S(2)}, u32[]{:S(2)}) %all-to-all-start) | async-done | bytes 5505056 | tf_op jit(solution)/shard_map/forward_experts/all_to_all | solution.py:77
  394.2 7.5 %all-to-all-start.3 = ((bf16[4,192,3584]{2,1,0:T(8,128)(2,1)}), bf16[4,192,3584]{2,1,0:T(8,128)(2,1)}, u32[]{:S(2)}, u32[]{:S(2)}) async-start(bf16[4,192,3584]{2,1,0:T(8,128)(2,1)} %bitcast.95), calls=%async_computation.3 | async-start | bytes 11010048 | tf_op jit(solution)/shard_map/backward_experts/all_to_all | solution.py:77
  401.9 13.2 %convolution_convert_fusion = bf16[768,3584]{1,0:T(8,128)(2,1)} fusion(bf16[512,3584]{1,0:T(8,128)(2,1)} %bitcast.22, bf16[768,3584]{1,0:T(8,128)(2,1)} %bitcast.16, bf16[3584,512]{1,0:T(8,128)(2,1)} %bitcast.21), kind=kOutput, calls=%fused_computation.2 | convolution fusion | flops 5641863168 | bytes 18350080 | tf_op jit(solution)/shard_map/forward_experts/dot_general | solution.py:63
  415.1 45.2 %all-to-all-done.3 = bf16[4,192,3584]{2,1,0:T(8,128)(2,1)} async-done(((bf16[4,192,3584]{2,1,0:T(8,128)(2,1)}), bf16[4,192,3584]{2,1,0:T(8,128)(2,1)}, u32[]{:S(2)}, u32[]{:S(2)}) %all-to-all-start.3) | async-done | bytes 5505056 | tf_op jit(solution)/shard_map/backward_experts/all_to_all | solution.py:77
  460.3 5.2 fusion.9
  465.5 7.4 %multiply_add_fusion.1 = bf16[512,3584]{1,0:T(8,128)(2,1)} fusion(f32[512,3584]{1,0:T(8,128)S(1)} %fusion.9, bf16[768,3584]{1,0:T(8,128)(2,1)} %bitcast.28, f32[512]{0:T(512)S(1)} %bitcast.118, f32[512]{0:T(512)S(1)} %bitcast.119, s32[512]{0:T(512)S(1)} %bitcast.113), kind=kOutput, calls=%fused_computation.1 | convolution fusion | flops 2826305536 | bytes 16521216 | tf_op jit(solution)/shard_map/backward_experts/dot_general | solution.py:55
  473.0 7.7 %all-to-all-start.4 = ((bf16[4,192,3584]{2,1,0:T(8,128)(2,1)}), bf16[4,192,3584]{2,1,0:T(8,128)(2,1)}, u32[]{:S(2)}, u32[]{:S(2)}) async-start(bf16[4,192,3584]{2,1,0:T(8,128)(2,1)} %bitcast.94), calls=%async_computation.5 | async-start | bytes 11010048 | tf_op jit(solution)/shard_map/forward_experts/all_to_all | solution.py:77
  480.9 57.5 %all-to-all-done.4 = bf16[4,192,3584]{2,1,0:T(8,128)(2,1)} async-done(((bf16[4,192,3584]{2,1,0:T(8,128)(2,1)}), bf16[4,192,3584]{2,1,0:T(8,128)(2,1)}, u32[]{:S(2)}, u32[]{:S(2)}) %all-to-all-start.4) | async-done | bytes 5505056 | tf_op jit(solution)/shard_map/forward_experts/all_to_all | solution.py:77
  538.4 5.2 fusion.10
  543.6 7.5 %multiply_add_fusion = bf16[512,3584]{1,0:T(8,128)(2,1)} fusion(f32[512,3584]{1,0:T(8,128)S(1)} %fusion.10, bf16[768,3584]{1,0:T(8,128)(2,1)} %bitcast.36, f32[512]{0:T(512)S(1)} %bitcast.117, f32[512]{0:T(512)S(1)} %bitcast.116, s32[512]{0:T(512)S(1)} %bitcast.114), kind=kOutput, calls=%fused_computation | convolution fusion | flops 2826305536 | bytes 16521216 | tf_op jit(solution)/shard_map/forward_experts/dot_general | solution.py:55
  551.1 4.0 reduce-scatter.3.cloned.1.call-done
  555.1 1.4 fusion.13
  556.5 0.7 collective-permute-start.4
  557.2 17.1 %collective-permute-done.4 = bf16[1,128,3584]{2,1,0:T(8,128)(2,1)S(1)} collective-permute-done((bf16[1,128,3584]{2,1,0:T(8,128)(2,1)S(1)}, bf16[1,128,3584]{2,1,0:T(8,128)(2,1)S(1)}, u32[]{:S(2)}, u32[]{:S(2)}) %collective-permute-start.4) | collective-permute-done | bytes 917536 | tf_op jit(solution)/shard_map/forward_experts/ppermute | solution.py:13
  574.3 63.3 %reduce-scatter.5.cloned.1.call-done = bf16[1,128,3584]{2,1,0:T(8,128)(2,1)} async-done(((bf16[4,128,3584]{2,1,0:T(8,128)(2,1)}), bf16[1,128,3584]{2,1,0:T(8,128)(2,1)}) %reduce-scatter.5.cloned.1.call-update) | async-done | bytes 917520 | tf_op jit(solution)/shard_map/forward_experts/reduce_scatter | solution.py:87
  637.6 2.3 add_convert_fusion
  639.9 0.9 copy.100
  (58 shorter events, 2.0 us)
Async XLA Ops:
  7.2 229.2 %all-gather.4.cloned.1.call-start = ((), (), s32[]{:S(2)}) async-start(), calls=%async_computation.7 | async-start | bytes 4587520 | tf_op jit(solution)/shard_map/gather_along_z/all_gather | solution.py:124
  7.9 241.7 %all-gather.8.cloned.1.call-start = ((), (), s32[]{:S(2)}) async-start(), calls=%async_computation.9 | async-start | bytes 4587520 | tf_op jit(solution)/shard_map/gather_along_z/all_gather | solution.py:124
  7.9 228.5 %collective-permute-start.2 = (bf16[1,3584,512]{2,1,0:T(8,128)(2,1)}, bf16[1,3584,512]{2,1,0:T(8,128)(2,1)}, u32[]{:S(2)}, u32[]{:S(2)}) collective-permute-start(bf16[1,3584,512]{2,1,0:T(8,128)(2,1)} %param.16), channel_id=1, source_target_pairs={{0,16},{16,32},{32,48},{48,64},{64,80},{80,96},{96,112},{112,128},... | collective-permute-start | bytes 11010056 | tf_op jit(solution)/shard_map/ppermute | solution.py:13
  9.9 226.5 %collective-permute-start.3 = (bf16[1,512,3584]{2,1,0:T(8,128)(2,1)}, bf16[1,512,3584]{2,1,0:T(8,128)(2,1)}, u32[]{:S(2)}, u32[]{:S(2)}) collective-permute-start(bf16[1,512,3584]{2,1,0:T(8,128)(2,1)} %param.17), channel_id=1, source_target_pairs={{0,16},{16,32},{32,48},{48,64},{64,80},{80,96},{96,112},{112,128},... | collective-permute-start | bytes 11010056 | tf_op jit(solution)/shard_map/ppermute | solution.py:13
  11.4 196.1 %collective-permute-start.1 = (f32[1,128,4]{1,2,0:T(4,128)S(1)}, f32[1,128,4]{1,2,0:T(4,128)S(1)}, u32[]{:S(2)}, u32[]{:S(2)}) collective-permute-start(f32[1,128,4]{1,2,0:T(4,128)S(1)} %pad_maximum_fusion.1), channel_id=1, source_target_pairs={{0,16},{16,32},{32,48},{48,64},{64,80},{80,96},{96,112},{112,128},... | collective-permute-start | bytes 6152 | tf_op jit(solution)/shard_map/ppermute | solution.py:13
  13.0 223.4 %collective-permute-start = (bf16[1,128,3584]{2,1,0:T(8,128)(2,1)}, bf16[1,128,3584]{2,1,0:T(8,128)(2,1)S(1)}, u32[]{:S(2)}, u32[]{:S(2)}) collective-permute-start(bf16[1,128,3584]{2,1,0:T(8,128)(2,1)} %param.9), channel_id=1, source_target_pairs={{0,16},{16,32},{32,48},{48,64},{64,80},{80,96},{96,112},{112,128},... | collective-permute-start | bytes 2752520 | tf_op jit(solution)/shard_map/ppermute | solution.py:13
  236.4 7.2 %copy-start.1 = (bf16[1,128,3584]{2,1,0:T(8,128)(2,1)}, bf16[1,128,3584]{2,1,0:T(8,128)(2,1)S(1)}, u32[]{:S(2)}) copy-start(bf16[1,128,3584]{2,1,0:T(8,128)(2,1)S(1)} %collective-permute-done) | copy-start | bytes 2752516
  243.5 36.6 %all-to-all-start.2 = ((bf16[4,192,3584]{2,1,0:T(8,128)(2,1)}), bf16[4,192,3584]{2,1,0:T(8,128)(2,1)}, u32[]{:S(2)}, u32[]{:S(2)}) async-start(bf16[4,192,3584]{2,1,0:T(8,128)(2,1)} %bitcast.97), calls=%async_computation.2 | async-start | bytes 11010048 | tf_op jit(solution)/shard_map/backward_experts/all_to_all | solution.py:77
  248.8 68.5 %all-gather.6.cloned.1.call-start = ((), (), s32[]{:S(2)}) async-start(), calls=%async_computation.8 | async-start | bytes 4587520 | tf_op jit(solution)/shard_map/gather_along_z/all_gather | solution.py:124
  280.2 44.0 %all-to-all-start.1 = ((bf16[4,192,3584]{2,1,0:T(8,128)(2,1)}), bf16[4,192,3584]{2,1,0:T(8,128)(2,1)}, u32[]{:S(2)}, u32[]{:S(2)}) async-start(bf16[4,192,3584]{2,1,0:T(8,128)(2,1)} %bitcast.96), calls=%async_computation.1 | async-start | bytes 11010048 | tf_op jit(solution)/shard_map/backward_experts/all_to_all | solution.py:77
  324.1 70.1 %all-to-all-start = ((bf16[4,192,3584]{2,1,0:T(8,128)(2,1)}), bf16[4,192,3584]{2,1,0:T(8,128)(2,1)}, u32[]{:S(2)}, u32[]{:S(2)}) async-start(bf16[4,192,3584]{2,1,0:T(8,128)(2,1)} %bitcast.98), calls=%async_computation | async-start | bytes 11010048 | tf_op jit(solution)/shard_map/forward_experts/all_to_all | solution.py:77
  334.4 6.2 copy-start.3
  340.6 6.0 copy-start.4
  394.2 66.2 %all-to-all-start.3 = ((bf16[4,192,3584]{2,1,0:T(8,128)(2,1)}), bf16[4,192,3584]{2,1,0:T(8,128)(2,1)}, u32[]{:S(2)}, u32[]{:S(2)}) async-start(bf16[4,192,3584]{2,1,0:T(8,128)(2,1)} %bitcast.95), calls=%async_computation.3 | async-start | bytes 11010048 | tf_op jit(solution)/shard_map/backward_experts/all_to_all | solution.py:77
  401.6 153.4 %reduce-scatter.3.cloned.1.call-start = ((), (), s32[]{:S(2)}) async-start(), calls=%async_computation.10 | async-start | bytes 4587520 | tf_op jit(solution)/shard_map/backward_experts/reduce_scatter | solution.py:87
  473.0 65.5 %all-to-all-start.4 = ((bf16[4,192,3584]{2,1,0:T(8,128)(2,1)}), bf16[4,192,3584]{2,1,0:T(8,128)(2,1)}, u32[]{:S(2)}, u32[]{:S(2)}) async-start(bf16[4,192,3584]{2,1,0:T(8,128)(2,1)} %bitcast.94), calls=%async_computation.5 | async-start | bytes 11010048 | tf_op jit(solution)/shard_map/forward_experts/all_to_all | solution.py:77
  480.6 156.9 %reduce-scatter.5.cloned.1.call-start = ((), (), s32[]{:S(2)}) async-start(), calls=%async_computation.11 | async-start | bytes 4587520 | tf_op jit(solution)/shard_map/forward_experts/reduce_scatter | solution.py:87
  543.6 11.5 %copy-start = (bf16[1,128,3584]{2,1,0:T(8,128)(2,1)S(1)}, bf16[1,128,3584]{2,1,0:T(8,128)(2,1)}, u32[]{:S(2)}) copy-start(bf16[1,128,3584]{2,1,0:T(8,128)(2,1)} %param.13) | copy-start | bytes 2752516
  551.1 86.5 %copy-start.2 = (bf16[1,128,3584]{2,1,0:T(8,128)(2,1)S(1)}, bf16[1,128,3584]{2,1,0:T(8,128)(2,1)}, u32[]{:S(2)}) copy-start(bf16[1,128,3584]{2,1,0:T(8,128)(2,1)} %copy-done.1) | copy-start | bytes 2752516
  556.5 17.8 %collective-permute-start.4 = (bf16[1,128,3584]{2,1,0:T(8,128)(2,1)S(1)}, bf16[1,128,3584]{2,1,0:T(8,128)(2,1)S(1)}, u32[]{:S(2)}, u32[]{:S(2)}) collective-permute-start(bf16[1,128,3584]{2,1,0:T(8,128)(2,1)S(1)} %bitcast.105), channel_id=1, source_target_pairs={{0,240},{16,0},{32,16},{48,32},{64,48},{80,64},{96,80},{112,96},{1... | collective-permute-start | bytes 2752520 | tf_op jit(solution)/shard_map/forward_experts/ppermute | solution.py:13
Sparse Core Ops, SparseCore 0:
  9.8 95.0 all-gather.3
  106.7 90.2 all-gather.7
  252.0 65.1 all-gather.5
  473.1 81.9 reduce-scatter.2
  557.5 80.0 reduce-scatter.4

commit v13 on v9

--- a/solution.py
+++ b/solution.py
@@ -49,11 +49,12 @@
 def weighted_partial(results, slots, route_weights, slot_total):
     groups, tok_rows, route_count = slots.shape
     places = jnp.arange(slot_total, dtype=jnp.int32)
+    by_route = jnp.moveaxis(slots, 2, 0).reshape(route_count * groups * tok_rows, 1)
+    table = (by_route == places).astype(jnp.bfloat16)
+    picked = jnp.dot(table, results, preferred_element_type=jnp.float32).reshape(route_count, groups * tok_rows, -1)
     total = None
     for k in range(route_count):
-        table = (slots[:, :, k].reshape(-1, 1) == places).astype(jnp.bfloat16)
-        picked = jnp.dot(table, results, preferred_element_type=jnp.float32)
-        term = route_weights[:, :, k].reshape(-1, 1) * picked
+        term = route_weights[:, :, k].reshape(-1, 1) * picked[k]
         total = term if total is None else total + term
     return total.reshape(groups, tok_rows, -1)
 

time: 583 us -> 621 us (1.065)
  local copies, waits for them, and re-layouts: 3.87 us -> 26.3 us
  other arithmetic: 11.6 us -> 29.9 us
    slice x9 -> x5, local copies, waits for them, and re-layouts: 0.7 us -> 23 us  [the longest x3 22.8 us: weighted_partial(): term = route_weights[:, :, k].reshape(-1, 1) * picked[k]]
    add x0 -> x2, other arithmetic: none -> 18.3 us  [weighted_partial(): total = term if total is None else total + term]
    dot_general x4 -> x2, matrix products: 25.2 us -> 23.6 us  [weighted_partial(): jnp.dot(table, results, preferred_element_type=jnp.float32)]
  transfers between devices with their start and end apart: 12 -> 12, of which waited for: 9 -> 9; matrix products, arithmetic and copies ran while one was open for 13% -> 15% of each run, Pallas kernels for 0% -> 0%
where the time goes in v13:
time: 621 us; the launch traced here: 615 us
  waiting for transfers between devices  420 us (68%)
  matrix products  73.3 us (12%)
  starting transfers between devices  37.4 us (6%)
  other arithmetic  29.9 us (5%)
  local copies, waits for them, and re-layouts  26.3 us (4%)
  blocking collectives  14.4 us (2%)
  between operations  14 us (2%)
    all_gather x3, waiting for transfers between devices, gather_z(): return lax.all_gather(value[0], 'ez', axis=0, tiled=False)  176 us
    all_to_all x5, waiting for transfers between devices, swap_x(): got = lax.all_to_all(spread, 'ex', split_axis=0, concat_axis=0, tiled=True)  143 us
    reduce_scatter x2, waiting for transfers between devices, sum_back(): lax.psum_scatter(partial.astype(wire_type), 'ez', scatter_dimension=0, ti...  87.8 us
    all_to_all x5, starting transfers between devices, swap_x(): got = lax.all_to_all(spread, 'ex', split_axis=0, concat_axis=0, tiled=True)  34.4 us
    dot_general x2, matrix products, weighted_partial(): jnp.dot(table, results, preferred_element_type=jnp.float32)  23.6 us
    slice x3, local copies, waits for them, and re-layouts, weighted_partial(): term = route_weights[:, :, k].reshape(-1, 1) * picked[k]  22.8 us
    dot_general x3, matrix products, pack_rows(): lax.dot_general(table, flat, (((0,), (0,)), ((), ())), preferred_element_...  20.7 us
    add x2, other arithmetic, weighted_partial(): total = term if total is None else total + term  18.3 us
  transfers between devices with their start and end apart: 12, of which 9 were waited for; matrix products, arithmetic and copies ran while one was open for 15% of the time, Pallas kernels for 0%

profile of v13, /device:TPU:29, one launch (start us, length us, event | category | flops | bytes accessed | tf_op | source)
XLA Modules:
  0.0 615.2 jit_solution(1712422572325414811)
XLA Ops:
  7.2 0.7 all-gather.4.cloned.1.call-update
  7.9 0.7 all-gather.8.cloned.1.call-update
  8.7 0.7 convert_element_type.95
  9.3 0.7 convert_element_type.96
  10.0 0.7 pad_maximum_fusion
  10.7 14.4 %all_gather.12 = f32[4,128,8]{1,2,0:T(8,128)S(1)} all-gather(f32[1,128,8]{1,2,0:T(8,128)S(1)} %pad_maximum_fusion), channel_id=1, replica_groups=mesh['pp'=16,'ex'=4,'ez'=4] {'ez'}, dimensions={0}, use_global_device_ids=true | all-gather | bytes 20480 | tf_op jit(solution)/shard_map/gather_along_z/all_gather | solution.py:119
  25.6 2.3 reduce-window.14
  28.3 0.2 copy.62
  28.7 2.3 reduce-window.16
  31.5 1.2 compare_select_fusion
  32.7 0.4 fusion.12
  33.1 46.7 %all-gather.4.cloned.1.call-done = bf16[4,128,3584]{2,1,0:T(8,128)(2,1)} async-done(((bf16[1,128,3584]{2,1,0:T(8,128)(2,1)}), bf16[4,128,3584]{2,1,0:T(8,128)(2,1)}) %all-gather.4.cloned.1.call-update) | async-done | bytes 3670032 | tf_op jit(solution)/shard_map/gather_along_z/all_gather | solution.py:119
  79.8 6.9 %convolution_convert_fusion.2 = bf16[768,3584]{1,0:T(8,128)(2,1)} fusion(bf16[512,768]{1,0:T(8,128)(2,1)S(1)} %fusion.12, bf16[512,3584]{1,0:T(8,128)(2,1)} %bitcast.126), kind=kOutput, calls=%fused_computation.4 | convolution fusion | flops 2821324800 | bytes 9961472 | tf_op jit(solution)/shard_map/backward_experts/dot_general | solution.py:44
  86.8 5.4 all-to-all-start.2
  92.2 0.7 all-gather.6.cloned.1.call-update
  92.9 63.9 %all-gather.8.cloned.1.call-done = bf16[4,128,3584]{2,1,0:T(8,128)(2,1)} async-done(((bf16[1,128,3584]{2,1,0:T(8,128)(2,1)}), bf16[4,128,3584]{2,1,0:T(8,128)(2,1)}) %all-gather.8.cloned.1.call-update) | async-done | bytes 3670032 | tf_op jit(solution)/shard_map/gather_along_z/all_gather | solution.py:119
  156.8 6.8 %convolution_convert_fusion.3 = bf16[768,3584]{1,0:T(8,128)(2,1)} fusion(bf16[512,768]{1,0:T(8,128)(2,1)S(1)} %fusion.12, bf16[512,3584]{1,0:T(8,128)(2,1)} %bitcast.125), kind=kOutput, calls=%fused_computation.5 | convolution fusion | flops 2821324800 | bytes 9961472 | tf_op jit(solution)/shard_map/backward_experts/dot_general | solution.py:44
  163.6 7.3 %all-to-all-start.1 = ((bf16[4,192,3584]{2,1,0:T(8,128)(2,1)}), bf16[4,192,3584]{2,1,0:T(8,128)(2,1)}, u32[]{:S(2)}, u32[]{:S(2)}) async-start(bf16[4,192,3584]{2,1,0:T(8,128)(2,1)} %bitcast.102), calls=%async_computation.1 | async-start | bytes 11010048 | tf_op jit(solution)/shard_map/backward_experts/all_to_all | solution.py:78
  171.0 0.4 fusion.13
  171.4 65.3 %all-gather.6.cloned.1.call-done = bf16[4,128,3584]{2,1,0:T(8,128)(2,1)} async-done(((bf16[1,128,3584]{2,1,0:T(8,128)(2,1)}), bf16[4,128,3584]{2,1,0:T(8,128)(2,1)}) %all-gather.6.cloned.1.call-update) | async-done | bytes 3670032 | tf_op jit(solution)/shard_map/gather_along_z/all_gather | solution.py:119
  236.7 6.9 %convolution_convert_fusion.4 = bf16[768,3584]{1,0:T(8,128)(2,1)} fusion(bf16[512,768]{1,0:T(8,128)(2,1)S(1)} %fusion.13, bf16[512,3584]{1,0:T(8,128)(2,1)} %bitcast.127), kind=kOutput, calls=%fused_computation.6 | convolution fusion | flops 2821324800 | bytes 9961472 | tf_op jit(solution)/shard_map/forward_experts/dot_general | solution.py:44
  243.6 5.1 all-to-all-start
  248.7 6.2 %fusion.6 = f32[768,512]{1,0:T(8,128)S(1)} fusion(bf16[768,3584]{1,0:T(8,128)(2,1)} %bitcast.20, bf16[1,3584,512]{2,1,0:T(8,128)(2,1)} %param.16), kind=kOutput, calls=%fused_computation.13 | convolution fusion | flops 2818572288 | bytes 10747904 | tf_op jit(solution)/shard_map/backward_experts/dot_general | solution.py:68
  254.9 6.0 multiply_convert_fusion.1
  261.0 4.9 convolution_convert_fusion.1
  265.9 40.7 %all-to-all-done = bf16[4,192,3584]{2,1,0:T(8,128)(2,1)} async-done(((bf16[4,192,3584]{2,1,0:T(8,128)(2,1)}), bf16[4,192,3584]{2,1,0:T(8,128)(2,1)}, u32[]{:S(2)}, u32[]{:S(2)}) %all-to-all-start) | async-done | bytes 5505056 | tf_op jit(solution)/shard_map/forward_experts/all_to_all | solution.py:78
  306.6 8.9 %all-to-all-start.3 = ((bf16[4,192,3584]{2,1,0:T(8,128)(2,1)}), bf16[4,192,3584]{2,1,0:T(8,128)(2,1)}, u32[]{:S(2)}, u32[]{:S(2)}) async-start(bf16[4,192,3584]{2,1,0:T(8,128)(2,1)} %bitcast.103), calls=%async_computation.3 | async-start | bytes 11010048 | tf_op jit(solution)/shard_map/backward_experts/all_to_all | solution.py:78
  315.7 7.0 %multiply_convert_fusion = bf16[768,512]{1,0:T(8,128)(2,1)S(1)} fusion(bf16[768,3584]{1,0:T(8,128)(2,1)} %bitcast.17, bf16[1,3584,512]{2,1,0:T(8,128)(2,1)} %param.16), kind=kOutput, calls=%fused_computation.28 | convolution fusion | flops 2820538368 | bytes 9961472 | tf_op jit(solution)/shard_map/forward_experts/dot_general | solution.py:63
  322.7 4.9 convolution_convert_fusion
  327.6 46.1 %all-to-all-done.3 = bf16[4,192,3584]{2,1,0:T(8,128)(2,1)} async-done(((bf16[4,192,3584]{2,1,0:T(8,128)(2,1)}), bf16[4,192,3584]{2,1,0:T(8,128)(2,1)}, u32[]{:S(2)}, u32[]{:S(2)}) %all-to-all-start.3) | async-done | bytes 5505056 | tf_op jit(solution)/shard_map/backward_experts/all_to_all | solution.py:78
  373.7 11.8 %fusion.8 = f32[1024,3584]{1,0:T(8,128)} fusion(bf16[768,3584]{1,0:T(8,128)(2,1)} %bitcast.27, s32[1024]{0:T(1024)S(1)} %bitcast.123), kind=kOutput, calls=%fused_computation.19 | convolution fusion | flops 5637931008 | bytes 20189184 | tf_op jit(solution)/shard_map/backward_experts/dot_general | solution.py:54
  385.5 11.3 %fusion.32 = (f32[512,3584]{1,0:T(8,128)}, f32[512,3584]{1,0:T(8,128)}) fusion(f32[1024,3584]{1,0:T(8,128)} %fusion.8), kind=kLoop, calls=%fused_computation.64 | loop fusion | bytes 29360128 | tf_op jit(solution)/shard_map/backward_experts/slice | solution.py:57
  396.8 9.1 %multiply_add_fusion.1 = bf16[4,128,3584]{2,1,0:T(8,128)(2,1)} fusion(f32[4,128,3584]{2,1,0:T(8,128)} %bitcast.100, f32[4,128,3584]{2,1,0:T(8,128)} %bitcast.99, f32[4,128]{1,0:T(4,128)S(1)} %bitcast.121, f32[4,128]{1,0:T(4,128)S(1)} %bitcast.122), kind=kLoop, calls=%fused_computation.1 | loop fusion | flops 7340032 | bytes 18354176 | tf_op jit(solution)/shard_map/backward_experts/add | solution.py:58
  405.9 7.7 %all-to-all-start.4 = ((bf16[4,192,3584]{2,1,0:T(8,128)(2,1)}), bf16[4,192,3584]{2,1,0:T(8,128)(2,1)}, u32[]{:S(2)}, u32[]{:S(2)}) async-start(bf16[4,192,3584]{2,1,0:T(8,128)(2,1)} %bitcast.101), calls=%async_computation.5 | async-start | bytes 11010048 | tf_op jit(solution)/shard_map/forward_experts/all_to_all | solution.py:78
  413.6 0.6 reduce-scatter.3.cloned.1.call-update
  414.2 0.3 reduce-scatter.5.cloned.1.call-start
  414.5 56.3 %all-to-all-done.4 = bf16[4,192,3584]{2,1,0:T(8,128)(2,1)} async-done(((bf16[4,192,3584]{2,1,0:T(8,128)(2,1)}), bf16[4,192,3584]{2,1,0:T(8,128)(2,1)}, u32[]{:S(2)}, u32[]{:S(2)}) %all-to-all-start.4) | async-done | bytes 5505056 | tf_op jit(solution)/shard_map/forward_experts/all_to_all | solution.py:78
  470.8 11.8 %fusion.11 = f32[1024,3584]{1,0:T(8,128)} fusion(bf16[768,3584]{1,0:T(8,128)(2,1)} %bitcast.36, s32[1024]{0:T(1024)S(1)} %bitcast.124), kind=kOutput, calls=%fused_computation.22 | convolution fusion | flops 5637931008 | bytes 20189184 | tf_op jit(solution)/shard_map/forward_experts/dot_general | solution.py:54
  482.6 11.4 %fusion.31 = (f32[512,3584]{1,0:T(8,128)}, f32[512,3584]{1,0:T(8,128)}) fusion(f32[1024,3584]{1,0:T(8,128)} %fusion.11), kind=kLoop, calls=%fused_computation.63 | loop fusion | bytes 29360128 | tf_op jit(solution)/shard_map/forward_experts/slice | solution.py:57
  494.0 9.2 %multiply_add_fusion = bf16[4,128,3584]{2,1,0:T(8,128)(2,1)} fusion(f32[4,128,3584]{2,1,0:T(8,128)} %bitcast.98, f32[4,128,3584]{2,1,0:T(8,128)} %bitcast.97, f32[4,128]{1,0:T(4,128)S(1)} %bitcast.120, f32[4,128]{1,0:T(4,128)S(1)} %bitcast.119), kind=kLoop, calls=%fused_computation | loop fusion | flops 7340032 | bytes 18354176 | tf_op jit(solution)/shard_map/forward_experts/add | solution.py:58
  503.2 1.6 reduce-scatter.3.cloned.1.call-done
  504.9 1.4 fusion.20
  506.3 2.6 collective-permute-start.1
  508.8 86.2 %reduce-scatter.5.cloned.1.call-done = bf16[1,128,3584]{2,1,0:T(8,128)(2,1)} async-done(((bf16[4,128,3584]{2,1,0:T(8,128)(2,1)}), bf16[1,128,3584]{2,1,0:T(8,128)(2,1)}) %reduce-scatter.5.cloned.1.call-update) | async-done | bytes 917520 | tf_op jit(solution)/shard_map/forward_experts/reduce_scatter | solution.py:88
  595.0 1.4 add_convert_fusion
  596.5 10.3 %collective-permute-done = bf16[1,128,3584]{2,1,0:T(8,128)(2,1)S(1)} collective-permute-done((bf16[1,128,3584]{2,1,0:T(8,128)(2,1)S(1)}, bf16[1,128,3584]{2,1,0:T(8,128)(2,1)S(1)}, u32[]{:S(2)}, u32[]{:S(2)}) %collective-permute-start) | collective-permute-done | bytes 917536 | tf_op jit(solution)/shard_map/forward_experts/ppermute | solution.py:13
  606.8 0.9 copy.79
  607.7 0.9 copy.80
  (50 shorter events, 2.0 us)
Async XLA Ops:
  7.2 72.7 %all-gather.4.cloned.1.call-start = ((), (), s32[]{:S(2)}) async-start(), calls=%async_computation.7 | async-start | bytes 4587520 | tf_op jit(solution)/shard_map/gather_along_z/all_gather | solution.py:119
  7.9 148.9 %all-gather.8.cloned.1.call-start = ((), (), s32[]{:S(2)}) async-start(), calls=%async_computation.9 | async-start | bytes 4587520 | tf_op jit(solution)/shard_map/gather_along_z/all_gather | solution.py:119
  86.8 76.9 %all-to-all-start.2 = ((bf16[4,192,3584]{2,1,0:T(8,128)(2,1)}), bf16[4,192,3584]{2,1,0:T(8,128)(2,1)}, u32[]{:S(2)}, u32[]{:S(2)}) async-start(bf16[4,192,3584]{2,1,0:T(8,128)(2,1)} %bitcast.104), calls=%async_computation.2 | async-start | bytes 11010048 | tf_op jit(solution)/shard_map/backward_experts/all_to_all | solution.py:78
  92.2 144.5 %all-gather.6.cloned.1.call-start = ((), (), s32[]{:S(2)}) async-start(), calls=%async_computation.8 | async-start | bytes 4587520 | tf_op jit(solution)/shard_map/gather_along_z/all_gather | solution.py:119
  163.6 80.0 %all-to-all-start.1 = ((bf16[4,192,3584]{2,1,0:T(8,128)(2,1)}), bf16[4,192,3584]{2,1,0:T(8,128)(2,1)}, u32[]{:S(2)}, u32[]{:S(2)}) async-start(bf16[4,192,3584]{2,1,0:T(8,128)(2,1)} %bitcast.102), calls=%async_computation.1 | async-start | bytes 11010048 | tf_op jit(solution)/shard_map/backward_experts/all_to_all | solution.py:78
  243.6 63.0 %all-to-all-start = ((bf16[4,192,3584]{2,1,0:T(8,128)(2,1)}), bf16[4,192,3584]{2,1,0:T(8,128)(2,1)}, u32[]{:S(2)}, u32[]{:S(2)}) async-start(bf16[4,192,3584]{2,1,0:T(8,128)(2,1)} %bitcast.105), calls=%async_computation | async-start | bytes 11010048 | tf_op jit(solution)/shard_map/forward_experts/all_to_all | solution.py:78
  248.7 6.2 %copy-start.3 = (bf16[1,512,3584]{2,1,0:T(8,128)(2,1)S(1)}, bf16[1,512,3584]{2,1,0:T(8,128)(2,1)}, u32[]{:S(2)}) copy-start(bf16[1,512,3584]{2,1,0:T(8,128)(2,1)} %param.17) | copy-start | bytes 11010052
  254.9 6.1 copy-start.2
  306.6 67.1 %all-to-all-start.3 = ((bf16[4,192,3584]{2,1,0:T(8,128)(2,1)}), bf16[4,192,3584]{2,1,0:T(8,128)(2,1)}, u32[]{:S(2)}, u32[]{:S(2)}) async-start(bf16[4,192,3584]{2,1,0:T(8,128)(2,1)} %bitcast.103), calls=%async_computation.3 | async-start | bytes 11010048 | tf_op jit(solution)/shard_map/backward_experts/all_to_all | solution.py:78
  315.6 7.0 %copy-start.4 = (bf16[1,512,3584]{2,1,0:T(8,128)(2,1)S(1)}, bf16[1,512,3584]{2,1,0:T(8,128)(2,1)}, u32[]{:S(2)}) copy-start(bf16[1,512,3584]{2,1,0:T(8,128)(2,1)} %param.17) | copy-start | bytes 11010052
  405.9 64.9 %all-to-all-start.4 = ((bf16[4,192,3584]{2,1,0:T(8,128)(2,1)}), bf16[4,192,3584]{2,1,0:T(8,128)(2,1)}, u32[]{:S(2)}, u32[]{:S(2)}) async-start(bf16[4,192,3584]{2,1,0:T(8,128)(2,1)} %bitcast.101), calls=%async_computation.5 | async-start | bytes 11010048 | tf_op jit(solution)/shard_map/forward_experts/all_to_all | solution.py:78
  413.6 91.2 %reduce-scatter.3.cloned.1.call-start = ((), (), s32[]{:S(2)}) async-start(), calls=%async_computation.10 | async-start | bytes 4587520 | tf_op jit(solution)/shard_map/backward_experts/reduce_scatter | solution.py:88
  414.2 180.8 %reduce-scatter.5.cloned.1.call-start = ((), (), s32[]{:S(2)}) async-start(), calls=%async_computation.11 | async-start | bytes 4587520 | tf_op jit(solution)/shard_map/forward_experts/reduce_scatter | solution.py:88
  494.0 10.8 %copy-start = (bf16[1,128,3584]{2,1,0:T(8,128)(2,1)S(1)}, bf16[1,128,3584]{2,1,0:T(8,128)(2,1)}, u32[]{:S(2)}) copy-start(bf16[1,128,3584]{2,1,0:T(8,128)(2,1)} %param.13) | copy-start | bytes 2752516
  503.2 91.8 %copy-start.1 = (bf16[1,128,3584]{2,1,0:T(8,128)(2,1)S(1)}, bf16[1,128,3584]{2,1,0:T(8,128)(2,1)}, u32[]{:S(2)}) copy-start(bf16[1,128,3584]{2,1,0:T(8,128)(2,1)} %param.9) | copy-start | bytes 2752516
  506.3 90.2 %collective-permute-start.1 = (bf16[1,128,3584]{2,1,0:T(8,128)(2,1)S(1)}, bf16[1,128,3584]{2,1,0:T(8,128)(2,1)S(1)}, u32[]{:S(2)}, u32[]{:S(2)}) collective-permute-start(bf16[1,128,3584]{2,1,0:T(8,128)(2,1)S(1)} %bitcast.112), channel_id=1, source_target_pairs={{0,240},{16,0},{32,16},{48,32},{64,48},{80,64},{96,80},{112,96},{1... | collective-permute-start | bytes 2752520 | tf_op jit(solution)/shard_map/forward_experts/ppermute | solution.py:13
  596.4 10.4 %collective-permute-start = (bf16[1,128,3584]{2,1,0:T(8,128)(2,1)S(1)}, bf16[1,128,3584]{2,1,0:T(8,128)(2,1)S(1)}, u32[]{:S(2)}, u32[]{:S(2)}) collective-permute-start(bf16[1,128,3584]{2,1,0:T(8,128)(2,1)S(1)} %add_convert_fusion), channel_id=1, source_target_pairs={{0,16},{16,32},{32,48},{48,64},{64,80},{80,96},{96,112},{112,128},... | collective-permute-start | bytes 2752520 | tf_op jit(solution)/shard_map/forward_experts/ppermute | solution.py:13
Sparse Core Ops, SparseCore 0:
  9.8 69.9 all-gather.3
  81.6 75.1 all-gather.7
  158.6 77.9 all-gather.5
  416.7 88.1 reduce-scatter.2
  507.3 87.6 reduce-scatter.4
